TPU v7x, 512 devices: a whole 4x8x8 slice. The times are simulated.
512 devices in a mesh: tm: 64 (over y, x, core), head: 8 (over z).
Axes of the slice: x: 4, y: 8, z: 8, core: 2. Of those that a mesh axis runs over, the one named last changes fastest.
Arguments:
- queries: bfloat16 [24576, 5120], P('tm', 'head')
- keys: bfloat16 [24576, 5120], P('tm', 'head')
- values: bfloat16 [24576, 5120], P('tm', 'head')
- text_keys: bfloat16 [512, 5120], P('tm', 'head'), may hold values from -6 to 6
- text_values: bfloat16 [512, 5120], P('tm', 'head')
- out_weight: bfloat16 [5120, 5120], P('head', 'tm'), may hold values from -0.25 to 0.25
- windows: int32 [64], replicated, may hold values from 0 to 4, as said below
- lengths: int32 [64], replicated, may hold values from 96 to 384, as said below
Outputs:
- mixed: bfloat16 [24576, 5120], P('tm', 'head')
Inputs may be any that keep to these rules, and one draw needn't show every extreme that they name: windows reach 4 for some frame in every draw. `lengths`: some frame is full in every draw.
All inputs are finite; a program needn't handle non-finite values.
Results may differ from a plain program's by a relative error of at most 0.014.
Values may be sent and summed in bfloat16 or wider, within the bound.
No kernel may reach another device: no remote copies, remote signals or barrier semaphores. Data moves between devices by JAX's collectives and lax.ppermute only.
A program may use at most 64 MiB of HBM per device.

v0:
```python
import math

import jax
import jax.numpy as jnp
from jax import lax
from jax.sharding import PartitionSpec as P

HD = 128
WIN = 4


def from_behind(value, axis, steps):
    count = lax.axis_size(axis)
    initial, last = (max(0, -steps), min(count, count - steps))
    return lax.ppermute(value, axis, [(source, source + steps) for source in range(initial, last)])


def on_device(queries, keys, values, text_keys, text_values, out_weight, windows, lengths):
    rows = queries.shape[0]
    width = queries.shape[1]
    local_heads = width // HD
    scale = 1.0 / math.sqrt(HD)
    position = lax.axis_index("tm")
    text_k, text_v = (
        lax.all_gather(text_keys, "tm", axis=0, tiled=True),
        lax.all_gather(text_values, "tm", axis=0, tiled=True),
    )
    key_list = [keys]
    value_list = [values]
    for step in range(1, WIN + 1):
        moved_k, moved_v = from_behind((keys, values), "tm", step)
        key_list.append(moved_k)
        value_list.append(moved_v)
    token_ids = jnp.arange(rows, dtype=jnp.int32)
    own_window = windows[position]
    mask_list = []
    for step in range(WIN + 1):
        source = position - step
        usable = (step <= own_window) & (source >= 0)
        source_len = lengths[jnp.maximum(source, 0)]
        mask_list.append(usable & (token_ids < source_len))
    mask_list.append(jnp.ones((text_k.shape[0],), bool))
    key_mask = jnp.concatenate(mask_list)
    all_keys = jnp.concatenate(key_list + [text_k], axis=0)
    all_values = jnp.concatenate(value_list + [text_v], axis=0)
    head_outputs = []
    for head_index in range(local_heads):
        lower = head_index * HD
        query_h = queries[:, lower : lower + HD]
        key_h = all_keys[:, lower : lower + HD]
        value_h = all_values[:, lower : lower + HD]
        scores = (
            lax.dot_general(
                query_h, key_h, (((1,), (1,)), ((), ())), preferred_element_type=jnp.float32
            )
            * scale
        )
        scores = jnp.where(key_mask[None, :], scores, -jnp.inf)
        top = jnp.max(scores, axis=-1, keepdims=True)
        weights = jnp.exp(scores - top)
        total = jnp.sum(weights, axis=-1, keepdims=True)
        attended = (
            jnp.dot(weights.astype(jnp.bfloat16), value_h, preferred_element_type=jnp.float32)
            / total
        )
        head_outputs.append(attended.astype(jnp.bfloat16))
    attended_all = jnp.concatenate(head_outputs, axis=1)
    partial_out = jnp.dot(
        attended_all,
        lax.all_gather(out_weight, "tm", axis=1, tiled=True),
        preferred_element_type=jnp.float32,
    )
    return lax.psum_scatter(
        partial_out.astype(jnp.bfloat16), "head", scatter_dimension=1, tiled=True
    )


def solution(mesh):
    return jax.shard_map(
        on_device,
        mesh=mesh,
        in_specs=(
            P("tm", "head"),
            P("tm", "head"),
            P("tm", "head"),
            P("tm", "head"),
            P("tm", "head"),
            P("head", "tm"),
            P(),
            P(),
        ),
        out_specs=P("tm", "head"),
        check_vma=False,
    )
```

profile of v0, /device:TPU:1, one launch (start us, length us, event | category | flops | bytes accessed | tf_op | source)
XLA Modules:
  0.0 300.5 jit_solution(977108429921644657)
XLA Ops:
  6.5 0.7 all-gather.2.cloned.1.call-update
  7.3 4.5 %collective-permute-start = (bf16[384,640]{1,0:T(8,128)(2,1)}, bf16[384,640]{1,0:T(8,128)(2,1)S(1)}, u32[]{:S(2)}, u32[]{:S(2)}) collective-permute-start(bf16[384,640]{1,0:T(8,128)(2,1)} %param.9), channel_id=1, source_target_pairs={{0,8},{8,16},{16,24},{24,32},{32,40},{40,48},{48,56},{56,64},{64,7... | collective-permute-start | bytes 1474568 | tf_op jit(solution)/shard_map/ppermute | solution.py:15
  11.8 3.1 %collective-permute-start.1 = (bf16[384,640]{1,0:T(8,128)(2,1)}, bf16[384,640]{1,0:T(8,128)(2,1)S(1)}, u32[]{:S(2)}, u32[]{:S(2)}) collective-permute-start(bf16[384,640]{1,0:T(8,128)(2,1)} %param.9), channel_id=1, source_target_pairs={{0,16},{8,24},{16,32},{24,40},{32,48},{40,56},{48,64},{56,72},{64,... | collective-permute-start | bytes 1474568 | tf_op jit(solution)/shard_map/ppermute | solution.py:15
  15.0 3.4 %collective-permute-start.2 = (bf16[384,640]{1,0:T(8,128)(2,1)}, bf16[384,640]{1,0:T(8,128)(2,1)S(1)}, u32[]{:S(2)}, u32[]{:S(2)}) collective-permute-start(bf16[384,640]{1,0:T(8,128)(2,1)} %param.9), channel_id=1, source_target_pairs={{0,24},{8,32},{16,40},{24,48},{32,56},{40,64},{48,72},{56,80},{64,... | collective-permute-start | bytes 1474568 | tf_op jit(solution)/shard_map/ppermute | solution.py:15
  18.4 3.4 %collective-permute-start.3 = (bf16[384,640]{1,0:T(8,128)(2,1)}, bf16[384,640]{1,0:T(8,128)(2,1)S(1)}, u32[]{:S(2)}, u32[]{:S(2)}) collective-permute-start(bf16[384,640]{1,0:T(8,128)(2,1)} %param.9), channel_id=1, source_target_pairs={{0,32},{8,40},{16,48},{24,56},{32,64},{40,72},{48,80},{56,88},{64,... | collective-permute-start | bytes 1474568 | tf_op jit(solution)/shard_map/ppermute | solution.py:15
  21.9 3.7 %collective-permute-start.4 = (bf16[384,640]{1,0:T(8,128)(2,1)}, bf16[384,640]{1,0:T(8,128)(2,1)S(1)}, u32[]{:S(2)}, u32[]{:S(2)}) collective-permute-start(bf16[384,640]{1,0:T(8,128)(2,1)} %param.10), channel_id=1, source_target_pairs={{0,8},{8,16},{16,24},{24,32},{32,40},{40,48},{48,56},{56,64},{64,7... | collective-permute-start | bytes 1474568 | tf_op jit(solution)/shard_map/ppermute | solution.py:15
  25.6 1.2 dynamic_slice.18
  30.1 1.5 fusion.95
  31.6 0.6 fusion.90
  32.2 0.3 dynamic-update-slice.17
  32.4 0.6 fusion.91
  33.1 0.3 dynamic-update-slice.18
  33.3 0.6 fusion.92
  34.0 0.3 dynamic-update-slice.19
  34.2 0.6 fusion.93
  34.9 0.3 dynamic-update-slice.20
  35.1 0.7 fusion.94
  35.8 0.3 dynamic-update-slice.21
  36.0 0.2 dynamic-update-slice.22
  36.3 74.3 %all_gather.9 = bf16[512,640]{1,0:T(8,128)(2,1)S(1)} all-gather(bf16[8,640]{1,0:T(8,128)(2,1)} %param.11), channel_id=1, replica_groups=mesh['tm'=64,'head'=8] {'tm'}, dimensions={0}, use_global_device_ids=true | all-gather | bytes 665600 | tf_op jit(solution)/shard_map/all_gather | solution.py:25
  110.6 48.6 %all_gather.10 = bf16[512,640]{1,0:T(8,128)(2,1)S(1)} all-gather(bf16[8,640]{1,0:T(8,128)(2,1)} %param.12), channel_id=1, replica_groups=mesh['tm'=64,'head'=8] {'tm'}, dimensions={0}, use_global_device_ids=true | all-gather | bytes 665600 | tf_op jit(solution)/shard_map/all_gather | solution.py:26
  159.3 1.1 constant_dynamic-update-slice_fusion.5
  160.3 1.1 constant_dynamic-update-slice_fusion.11
  161.4 2.3 collective-permute-start.5
  163.8 4.6 %collective-permute-start.6 = (bf16[384,640]{1,0:T(8,128)(2,1)S(1)}, bf16[384,640]{1,0:T(8,128)(2,1)S(1)}, u32[]{:S(2)}, u32[]{:S(2)}) collective-permute-start(bf16[384,640]{1,0:T(8,128)(2,1)S(1)} %copy-done), channel_id=1, source_target_pairs={{0,24},{8,32},{16,40},{24,48},{32,56},{40,64},{48,72},{56,80},{64,... | collective-permute-start | bytes 1474568 | tf_op jit(solution)/shard_map/ppermute | solution.py:15
  168.6 2.3 collective-permute-start.7
  171.1 3.4 %collective-permute-done.5 = bf16[384,640]{1,0:T(8,128)(2,1)S(1)} collective-permute-done((bf16[384,640]{1,0:T(8,128)(2,1)}, bf16[384,640]{1,0:T(8,128)(2,1)S(1)}, u32[]{:S(2)}, u32[]{:S(2)}) %collective-permute-start.5) | collective-permute-done | bytes 491552 | tf_op jit(solution)/shard_map/ppermute | solution.py:15
  174.5 10.4 %collective-permute-done.6 = bf16[384,640]{1,0:T(8,128)(2,1)S(1)} collective-permute-done((bf16[384,640]{1,0:T(8,128)(2,1)S(1)}, bf16[384,640]{1,0:T(8,128)(2,1)S(1)}, u32[]{:S(2)}, u32[]{:S(2)}) %collective-permute-start.6) | collective-permute-done | bytes 491552 | tf_op jit(solution)/shard_map/ppermute | solution.py:15
  185.0 10.5 %collective-permute-done.7 = bf16[384,640]{1,0:T(8,128)(2,1)S(1)} collective-permute-done((bf16[384,640]{1,0:T(8,128)(2,1)S(1)}, bf16[384,640]{1,0:T(8,128)(2,1)S(1)}, u32[]{:S(2)}, u32[]{:S(2)}) %collective-permute-start.7) | collective-permute-done | bytes 491552 | tf_op jit(solution)/shard_map/ppermute | solution.py:15
  195.7 0.9 fusion.96
  196.6 0.6 fusion.5
  197.3 0.9 fusion.97
  198.1 0.6 fusion.7
  198.8 0.9 fusion.98
  199.7 0.6 fusion.9
  200.3 0.9 fusion.99
  201.2 0.6 fusion.11
  201.8 0.9 fusion.100
  202.7 0.6 fusion.13
  203.4 0.7 fusion.72
  204.1 0.7 fusion.66
  204.8 0.8 fusion.60
  205.6 0.7 fusion.54
  206.4 0.7 fusion.48
  207.1 8.9 %convolution_convert_fusion = bf16[384,5120]{1,0:T(8,128)(2,1)} fusion(bf16[384,640]{1,0:T(8,128)(2,1)S(1)} %fusion.48, bf16[640,5120]{0,1:T(8,128)(2,1)} %all-gather.2.cloned.1.call-done), kind=kOutput, calls=%fused_computation | convolution fusion | flops 2518548480 | bytes 10977280 | tf_op jit(solution)/shard_map/dot_general | solution.py:68
  216.1 6.3 %copy.9 = bf16[384,5120]{0,1:T(8,128)(2,1)} copy(bf16[384,5120]{1,0:T(8,128)(2,1)} %convolution_convert_fusion) | data formatting | bytes 7864320
  222.4 69.3 %reduce-scatter.4.cloned.1.call-done = bf16[640,384]{1,0:T(8,128)(2,1)} async-done(((bf16[5120,384]{1,0:T(8,128)(2,1)}), bf16[640,384]{1,0:T(8,128)(2,1)}) %reduce-scatter.4.cloned.1.call-update) | async-done | bytes 491536
  291.6 2.0 copy.10
  (25 shorter events, 0.8 us)
Async XLA Ops:
  6.5 157.3 %copy-start = (bf16[384,640]{1,0:T(8,128)(2,1)S(1)}, bf16[384,640]{1,0:T(8,128)(2,1)}, u32[]{:S(2)}) copy-start(bf16[384,640]{1,0:T(8,128)(2,1)} %param.10) | copy-start | bytes 1474564
  6.5 200.6 %all-gather.2.cloned.1.call-start = ((), (), s32[]{:S(2)}) async-start(), calls=%async_computation.1 | async-start | bytes 6656000 | tf_op jit(solution)/shard_map/all_gather | solution.py:70
  7.3 284.4 %reduce-scatter.4.cloned.1.call-start = ((), (), s32[]{:S(2)}) async-start(), calls=%async_computation.2 | async-start | bytes 4423680
  7.3 154.1 %collective-permute-start = (bf16[384,640]{1,0:T(8,128)(2,1)}, bf16[384,640]{1,0:T(8,128)(2,1)S(1)}, u32[]{:S(2)}, u32[]{:S(2)}) collective-permute-start(bf16[384,640]{1,0:T(8,128)(2,1)} %param.9), channel_id=1, source_target_pairs={{0,8},{8,16},{16,24},{24,32},{32,40},{40,48},{48,56},{56,64},{64,7... | collective-permute-start | bytes 1474568 | tf_op jit(solution)/shard_map/ppermute | solution.py:15
  11.8 152.0 %collective-permute-start.1 = (bf16[384,640]{1,0:T(8,128)(2,1)}, bf16[384,640]{1,0:T(8,128)(2,1)S(1)}, u32[]{:S(2)}, u32[]{:S(2)}) collective-permute-start(bf16[384,640]{1,0:T(8,128)(2,1)} %param.9), channel_id=1, source_target_pairs={{0,16},{8,24},{16,32},{24,40},{32,48},{40,56},{48,64},{56,72},{64,... | collective-permute-start | bytes 1474568 | tf_op jit(solution)/shard_map/ppermute | solution.py:15
  15.0 153.6 %collective-permute-start.2 = (bf16[384,640]{1,0:T(8,128)(2,1)}, bf16[384,640]{1,0:T(8,128)(2,1)S(1)}, u32[]{:S(2)}, u32[]{:S(2)}) collective-permute-start(bf16[384,640]{1,0:T(8,128)(2,1)} %param.9), channel_id=1, source_target_pairs={{0,24},{8,32},{16,40},{24,48},{32,56},{40,64},{48,72},{56,80},{64,... | collective-permute-start | bytes 1474568 | tf_op jit(solution)/shard_map/ppermute | solution.py:15
  18.4 152.5 %collective-permute-start.3 = (bf16[384,640]{1,0:T(8,128)(2,1)}, bf16[384,640]{1,0:T(8,128)(2,1)S(1)}, u32[]{:S(2)}, u32[]{:S(2)}) collective-permute-start(bf16[384,640]{1,0:T(8,128)(2,1)} %param.9), channel_id=1, source_target_pairs={{0,32},{8,40},{16,48},{24,56},{32,64},{40,72},{48,80},{56,88},{64,... | collective-permute-start | bytes 1474568 | tf_op jit(solution)/shard_map/ppermute | solution.py:15
  21.9 149.1 %collective-permute-start.4 = (bf16[384,640]{1,0:T(8,128)(2,1)}, bf16[384,640]{1,0:T(8,128)(2,1)S(1)}, u32[]{:S(2)}, u32[]{:S(2)}) collective-permute-start(bf16[384,640]{1,0:T(8,128)(2,1)} %param.10), channel_id=1, source_target_pairs={{0,8},{8,16},{16,24},{24,32},{32,40},{40,48},{48,56},{56,64},{64,7... | collective-permute-start | bytes 1474568 | tf_op jit(solution)/shard_map/ppermute | solution.py:15
  161.4 13.1 %collective-permute-start.5 = (bf16[384,640]{1,0:T(8,128)(2,1)}, bf16[384,640]{1,0:T(8,128)(2,1)S(1)}, u32[]{:S(2)}, u32[]{:S(2)}) collective-permute-start(bf16[384,640]{1,0:T(8,128)(2,1)} %param.10), channel_id=1, source_target_pairs={{0,16},{8,24},{16,32},{24,40},{32,48},{40,56},{48,64},{56,72},{64,... | collective-permute-start | bytes 1474568 | tf_op jit(solution)/shard_map/ppermute | solution.py:15
  163.8 21.1 %collective-permute-start.6 = (bf16[384,640]{1,0:T(8,128)(2,1)S(1)}, bf16[384,640]{1,0:T(8,128)(2,1)S(1)}, u32[]{:S(2)}, u32[]{:S(2)}) collective-permute-start(bf16[384,640]{1,0:T(8,128)(2,1)S(1)} %copy-done), channel_id=1, source_target_pairs={{0,24},{8,32},{16,40},{24,48},{32,56},{40,64},{48,72},{56,80},{64,... | collective-permute-start | bytes 1474568 | tf_op jit(solution)/shard_map/ppermute | solution.py:15
  168.6 26.9 %collective-permute-start.7 = (bf16[384,640]{1,0:T(8,128)(2,1)S(1)}, bf16[384,640]{1,0:T(8,128)(2,1)S(1)}, u32[]{:S(2)}, u32[]{:S(2)}) collective-permute-start(bf16[384,640]{1,0:T(8,128)(2,1)S(1)} %copy-done), channel_id=1, source_target_pairs={{0,32},{8,40},{16,48},{24,56},{32,64},{40,72},{48,80},{56,88},{64,... | collective-permute-start | bytes 1474568 | tf_op jit(solution)/shard_map/ppermute | solution.py:15
  170.9 24.8 %copy-start.1 = (bf16[384,640]{1,0:T(8,128)(2,1)S(1)}, bf16[384,640]{1,0:T(8,128)(2,1)}, u32[]{:S(2)}) copy-start(bf16[384,640]{1,0:T(8,128)(2,1)} %param.8) | copy-start | bytes 1474564
Sparse Core Ops, SparseCore 0:
  10.6 113.0 all-gather.1
  222.5 69.0 reduce-scatter.3
where the time goes:
time: 301 us; the launch traced here: 300 us
  blocking collectives  123 us (41%)
  waiting for transfers between devices  94.2 us (31%)
  starting transfers between devices  27.5 us (9%)
  matrix products  17.1 us (6%)
  between operations  17 us (6%)
  local copies, waits for them, and re-layouts  15.4 us (5%)
  other arithmetic  6.31 us (2%)
    all_gather x1, blocking collectives, on_device(): lax.all_gather(text_keys, 'tm', axis=0, tiled=True)  74.3 us
    unnamed x3, waiting for transfers between devices  70 us
    all_gather x1, blocking collectives, on_device(): lax.all_gather(text_values, 'tm', axis=0, tiled=True)  48.6 us
    ppermute x8, starting transfers between devices, from_behind(): lax.ppermute(value, axis, [(source, source + steps) for source in range(i...  27.5 us
    ppermute x8, waiting for transfers between devices, from_behind(): lax.ppermute(value, axis, [(source, source + steps) for source in range(i...  24.2 us
    unnamed x21, local copies, waits for them, and re-layouts  12.2 us
    dot_general x1, matrix products, on_device(): jnp.dot(attended_all, lax.all_gather(out_weight, 'tm', axis=1, tiled=True...  8.94 us
  transfers between devices with their start and end apart: 10, of which 4 were waited for; matrix products, arithmetic and copies ran while one was open for 7% of the time, Pallas kernels for 0%

commit v1 on v0

--- a/solution.py
+++ b/solution.py
@@ -15,22 +15,26 @@
     return lax.ppermute(value, axis, [(source, source + steps) for source in range(initial, last)])
 
 
+def gather_text(text_keys, text_values):
+    width = text_keys.shape[1]
+    both = jnp.concatenate([text_keys, text_values], axis=1)
+    full = lax.all_gather(both, "tm", axis=0, tiled=True)
+    return full[:, :width], full[:, width:]
+
+
 def on_device(queries, keys, values, text_keys, text_values, out_weight, windows, lengths):
     rows = queries.shape[0]
     width = queries.shape[1]
     local_heads = width // HD
+    groups = lax.axis_size("head")
     scale = 1.0 / math.sqrt(HD)
     position = lax.axis_index("tm")
-    text_k, text_v = (
-        lax.all_gather(text_keys, "tm", axis=0, tiled=True),
-        lax.all_gather(text_values, "tm", axis=0, tiled=True),
-    )
-    key_list = [keys]
-    value_list = [values]
+    text_k, text_v = gather_text(text_keys, text_values)
+    weight_all = lax.all_gather(out_weight, "tm", axis=1, tiled=True)
+    kv = jnp.stack([keys, values])
+    kv_list = [kv]
     for step in range(1, WIN + 1):
-        moved_k, moved_v = from_behind((keys, values), "tm", step)
-        key_list.append(moved_k)
-        value_list.append(moved_v)
+        kv_list.append(from_behind(kv, "tm", step))
     token_ids = jnp.arange(rows, dtype=jnp.int32)
     own_window = windows[position]
     mask_list = []
@@ -41,8 +45,8 @@
         mask_list.append(usable & (token_ids < source_len))
     mask_list.append(jnp.ones((text_k.shape[0],), bool))
     key_mask = jnp.concatenate(mask_list)
-    all_keys = jnp.concatenate(key_list + [text_k], axis=0)
-    all_values = jnp.concatenate(value_list + [text_v], axis=0)
+    all_keys = jnp.concatenate([p[0] for p in kv_list] + [text_k], axis=0)
+    all_values = jnp.concatenate([p[1] for p in kv_list] + [text_v], axis=0)
     head_outputs = []
     for head_index in range(local_heads):
         lower = head_index * HD
@@ -65,14 +69,10 @@
         )
         head_outputs.append(attended.astype(jnp.bfloat16))
     attended_all = jnp.concatenate(head_outputs, axis=1)
-    partial_out = jnp.dot(
-        attended_all,
-        lax.all_gather(out_weight, "tm", axis=1, tiled=True),
-        preferred_element_type=jnp.float32,
-    )
-    return lax.psum_scatter(
-        partial_out.astype(jnp.bfloat16), "head", scatter_dimension=1, tiled=True
-    )
+    w3 = weight_all.reshape(width, groups, weight_all.shape[1] // groups)
+    partial_out = jnp.einsum("rk,kgc->grc", attended_all, w3, preferred_element_type=jnp.float32)
+    mixed = lax.psum_scatter(partial_out.astype(jnp.bfloat16), "head", scatter_dimension=0, tiled=True)
+    return mixed.reshape(rows, -1)
 
 
 def solution(mesh):

time: 301 us -> 311 us (1.033)
  waiting for transfers between devices: 94.2 us -> 228 us
  blocking collectives: 123 us -> 0 us
  starting transfers between devices: 27.5 us -> 15.6 us
  matrix products: 17.1 us -> 23.5 us
  other arithmetic: 6.31 us -> 9.85 us
    all_gather x1 -> x2, waiting for transfers between devices: 0.02 us -> 129 us  [the longest x1 67.8 us: on_device(): weight_all = lax.all_gather(out_weight, 'tm', axis=1, tiled=True)]
    all_gather x2 -> x0, blocking collectives: 123 us -> none  [the longest x1 74.3 us: on_device(): lax.all_gather(text_keys, 'tm', axis=0, tiled=True)]
    unnamed x3, waiting for transfers between devices: 70 us -> 0.73 us
    reduce_scatter x0 -> x1, waiting for transfers between devices: none -> 53.1 us  [on_device(): lax.psum_scatter(partial_out.astype(jnp.bfloat16), 'head', scatter_dimens...]
    ppermute x8 -> x4, waiting for transfers between devices: 24.2 us -> 44.8 us  [from_behind(): lax.ppermute(value, axis, [(source, source + steps) for source in range(i...]
    ppermute x8 -> x4, starting transfers between devices: 27.5 us -> 15.5 us  [from_behind(): lax.ppermute(value, axis, [(source, source + steps) for source in range(i...]
    dot_general x5, matrix products: 3.71 us -> 9.3 us  [on_device(): jnp.dot(weights.astype(jnp.bfloat16), value_h, preferred_element_type=jnp...]
    unnamed x21 -> x12, local copies, waits for them, and re-layouts: 12.2 us -> 11.6 us
  transfers between devices with their start and end apart: 10 -> 7, of which waited for: 4 -> 6; matrix products, arithmetic and copies ran while one was open for 7% -> 13% of each run, Pallas kernels for 0% -> 0%
where the time goes in v1:
time: 311 us; the launch traced here: 310 us
  waiting for transfers between devices  228 us (73%)
  matrix products  23.5 us (8%)
  local copies, waits for them, and re-layouts  17 us (5%)
  between operations  16.4 us (5%)
  starting transfers between devices  15.6 us (5%)
  other arithmetic  9.85 us (3%)
    all_gather x1, waiting for transfers between devices, on_device(): weight_all = lax.all_gather(out_weight, 'tm', axis=1, tiled=True)  67.8 us
    all_gather x1, waiting for transfers between devices, gather_text(): full = lax.all_gather(both, 'tm', axis=0, tiled=True)  61.3 us
    reduce_scatter x1, waiting for transfers between devices, on_device(): lax.psum_scatter(partial_out.astype(jnp.bfloat16), 'head', scatter_dimens...  53.1 us
    ppermute x4, waiting for transfers between devices, from_behind(): lax.ppermute(value, axis, [(source, source + steps) for source in range(i...  44.8 us
    ppermute x4, starting transfers between devices, from_behind(): lax.ppermute(value, axis, [(source, source + steps) for source in range(i...  15.5 us
    unnamed x12, local copies, waits for them, and re-layouts  11.6 us
    dot_general x5, matrix products, on_device(): jnp.dot(weights.astype(jnp.bfloat16), value_h, preferred_element_type=jnp...  9.3 us
    dot_general x1, matrix products, on_device(): jnp.einsum('rk,kgc->grc', attended_all, w3, preferred_element_type=jnp.fl...  8.89 us
  transfers between devices with their start and end apart: 7, of which 6 were waited for; matrix products, arithmetic and copies ran while one was open for 13% of the time, Pallas kernels for 0%

profile of v1, /device:TPU:1, one launch (start us, length us, event | category | flops | bytes accessed | tf_op | source)
XLA Modules:
  0.0 310.1 jit_solution(5613431030098832081)
XLA Ops:
  6.5 1.3 pad_maximum_fusion.1
  7.9 0.7 all-gather.5.cloned.1.call-update
  8.7 2.2 pad_maximum_fusion
  10.9 4.5 %collective-permute-start = (bf16[2,384,640]{2,1,0:T(8,128)(2,1)}, bf16[2,384,640]{2,1,0:T(8,128)(2,1)}, u32[]{:S(2)}, u32[]{:S(2)}) collective-permute-start(bf16[2,384,640]{2,1,0:T(8,128)(2,1)} %pad_maximum_fusion), channel_id=1, source_target_pairs={{0,8},{8,16},{16,24},{24,32},{32,40},{40,48},{48,56},{56,64},{64,7... | collective-permute-start | bytes 2949128 | tf_op jit(solution)/shard_map/ppermute | solution.py:15
  15.4 4.1 %collective-permute-start.1 = (bf16[2,384,640]{2,1,0:T(8,128)(2,1)}, bf16[2,384,640]{2,1,0:T(8,128)(2,1)}, u32[]{:S(2)}, u32[]{:S(2)}) collective-permute-start(bf16[2,384,640]{2,1,0:T(8,128)(2,1)} %pad_maximum_fusion), channel_id=1, source_target_pairs={{0,16},{8,24},{16,32},{24,40},{32,48},{40,56},{48,64},{56,72},{64,... | collective-permute-start | bytes 2949128 | tf_op jit(solution)/shard_map/ppermute | solution.py:15
  19.5 3.5 %collective-permute-start.2 = (bf16[2,384,640]{2,1,0:T(8,128)(2,1)}, bf16[2,384,640]{2,1,0:T(8,128)(2,1)}, u32[]{:S(2)}, u32[]{:S(2)}) collective-permute-start(bf16[2,384,640]{2,1,0:T(8,128)(2,1)} %pad_maximum_fusion), channel_id=1, source_target_pairs={{0,24},{8,32},{16,40},{24,48},{32,56},{40,64},{48,72},{56,80},{64,... | collective-permute-start | bytes 2949128 | tf_op jit(solution)/shard_map/ppermute | solution.py:15
  23.0 3.4 %collective-permute-start.3 = (bf16[2,384,640]{2,1,0:T(8,128)(2,1)}, bf16[2,384,640]{2,1,0:T(8,128)(2,1)}, u32[]{:S(2)}, u32[]{:S(2)}) collective-permute-start(bf16[2,384,640]{2,1,0:T(8,128)(2,1)} %pad_maximum_fusion), channel_id=1, source_target_pairs={{0,32},{8,40},{16,48},{24,56},{32,64},{40,72},{48,80},{56,88},{64,... | collective-permute-start | bytes 2949128 | tf_op jit(solution)/shard_map/ppermute | solution.py:15
  26.4 1.3 dynamic_slice.18
  30.9 1.5 fusion.104
  32.4 0.6 fusion.99
  33.0 0.3 dynamic-update-slice.17
  33.3 0.6 fusion.100
  33.9 0.3 dynamic-update-slice.18
  34.1 0.6 fusion.101
  34.8 0.3 dynamic-update-slice.19
  35.0 0.6 fusion.102
  35.6 0.3 dynamic-update-slice.20
  35.9 0.6 fusion.103
  36.5 0.3 dynamic-update-slice.21
  36.8 0.4 dynamic-update-slice.22
  37.2 2.1 constant_dynamic-update-slice_fusion
  39.2 2.0 fusion.88
  41.3 11.2 %collective-permute-done.1 = bf16[2,384,640]{2,1,0:T(8,128)(2,1)} collective-permute-done((bf16[2,384,640]{2,1,0:T(8,128)(2,1)}, bf16[2,384,640]{2,1,0:T(8,128)(2,1)}, u32[]{:S(2)}, u32[]{:S(2)}) %collective-permute-start.1) | collective-permute-done | bytes 983072 | tf_op jit(solution)/shard_map/ppermute | solution.py:15
  52.4 2.0 fusion.87
  54.5 19.1 %collective-permute-done.2 = bf16[2,384,640]{2,1,0:T(8,128)(2,1)} collective-permute-done((bf16[2,384,640]{2,1,0:T(8,128)(2,1)}, bf16[2,384,640]{2,1,0:T(8,128)(2,1)}, u32[]{:S(2)}, u32[]{:S(2)}) %collective-permute-start.2) | collective-permute-done | bytes 983072 | tf_op jit(solution)/shard_map/ppermute | solution.py:15
  73.5 2.1 fusion.86
  75.6 14.6 %collective-permute-done.3 = bf16[2,384,640]{2,1,0:T(8,128)(2,1)} collective-permute-done((bf16[2,384,640]{2,1,0:T(8,128)(2,1)}, bf16[2,384,640]{2,1,0:T(8,128)(2,1)}, u32[]{:S(2)}, u32[]{:S(2)}) %collective-permute-start.3) | collective-permute-done | bytes 983072 | tf_op jit(solution)/shard_map/ppermute | solution.py:15
  90.2 2.1 fusion.85
  92.3 61.3 %all-gather.3.cloned.1.call-done = bf16[512,1280]{1,0:T(8,128)(2,1)} async-done(((bf16[8,1280]{1,0:T(8,128)(2,1)}), bf16[512,1280]{1,0:T(8,128)(2,1)}) %all-gather.3.cloned.1.call-update) | async-done | bytes 1310736 | tf_op jit(solution)/shard_map/all_gather | solution.py:21
  153.7 2.3 slice_dynamic-update-slice_fusion
  156.0 1.8 fusion.105
  157.8 0.6 fusion.5
  158.4 0.9 fusion.106
  159.3 0.6 fusion.7
  159.9 0.9 fusion.107
  160.8 0.6 fusion.9
  161.5 0.9 fusion.108
  162.3 0.6 fusion.11
  163.0 0.9 fusion.109
  163.8 0.6 fusion.13
  164.5 1.9 fusion.72
  166.3 1.8 fusion.66
  168.2 1.9 fusion.60
  170.0 1.9 fusion.54
  171.9 1.9 fusion.48
  173.8 67.8 %all-gather.5.cloned.1.call-done = bf16[640,5120]{0,1:T(8,128)(2,1)} async-done(((bf16[640,80]{0,1:T(8,128)(2,1)}), bf16[640,5120]{0,1:T(8,128)(2,1)}) %all-gather.5.cloned.1.call-update) | async-done | bytes 6553616 | tf_op jit(solution)/shard_map/all_gather | solution.py:33
  241.6 8.9 %convert_bitcast_fusion = bf16[8,384,640]{2,1,0:T(8,128)(2,1)} fusion(bf16[640,8,640]{0,2,1:T(8,128)(2,1)} %bitcast.54, bf16[384,640]{1,0:T(8,128)(2,1)S(1)} %fusion.48), kind=kOutput, calls=%fused_computation.10 | convolution fusion | flops 2518548480 | bytes 10977280 | tf_op jit(solution)/shard_map/rk,kgc->grc/dot_general | solution.py:73
  250.5 53.1 %reduce-scatter.2.cloned.1.call-done = bf16[1,384,640]{2,1,0:T(8,128)(2,1)} async-done(((bf16[8,384,640]{2,1,0:T(8,128)(2,1)}), bf16[1,384,640]{2,1,0:T(8,128)(2,1)}) %reduce-scatter.2.cloned.1.call-update) | async-done | bytes 491536 | tf_op jit(solution)/shard_map/reduce_scatter | solution.py:74
  (10 shorter events, 0.1 us)
Async XLA Ops:
  6.5 147.1 %all-gather.3.cloned.1.call-start = ((), (), s32[]{:S(2)}) async-start(), calls=%async_computation.1 | async-start | bytes 1331200 | tf_op jit(solution)/shard_map/all_gather | solution.py:21
  7.9 233.7 %all-gather.5.cloned.1.call-start = ((), (), s32[]{:S(2)}) async-start(), calls=%async_computation.2 | async-start | bytes 6656000 | tf_op jit(solution)/shard_map/all_gather | solution.py:33
  8.6 294.9 %reduce-scatter.2.cloned.1.call-start = ((), (), s32[]{:S(2)}) async-start(), calls=%async_computation.3 | async-start | bytes 4423680 | tf_op jit(solution)/shard_map/reduce_scatter | solution.py:74
  10.9 28.3 %collective-permute-start = (bf16[2,384,640]{2,1,0:T(8,128)(2,1)}, bf16[2,384,640]{2,1,0:T(8,128)(2,1)}, u32[]{:S(2)}, u32[]{:S(2)}) collective-permute-start(bf16[2,384,640]{2,1,0:T(8,128)(2,1)} %pad_maximum_fusion), channel_id=1, source_target_pairs={{0,8},{8,16},{16,24},{24,32},{32,40},{40,48},{48,56},{56,64},{64,7... | collective-permute-start | bytes 2949128 | tf_op jit(solution)/shard_map/ppermute | solution.py:15
  15.4 37.0 %collective-permute-start.1 = (bf16[2,384,640]{2,1,0:T(8,128)(2,1)}, bf16[2,384,640]{2,1,0:T(8,128)(2,1)}, u32[]{:S(2)}, u32[]{:S(2)}) collective-permute-start(bf16[2,384,640]{2,1,0:T(8,128)(2,1)} %pad_maximum_fusion), channel_id=1, source_target_pairs={{0,16},{8,24},{16,32},{24,40},{32,48},{40,56},{48,64},{56,72},{64,... | collective-permute-start | bytes 2949128 | tf_op jit(solution)/shard_map/ppermute | solution.py:15
  19.5 54.0 %collective-permute-start.2 = (bf16[2,384,640]{2,1,0:T(8,128)(2,1)}, bf16[2,384,640]{2,1,0:T(8,128)(2,1)}, u32[]{:S(2)}, u32[]{:S(2)}) collective-permute-start(bf16[2,384,640]{2,1,0:T(8,128)(2,1)} %pad_maximum_fusion), channel_id=1, source_target_pairs={{0,24},{8,32},{16,40},{24,48},{32,56},{40,64},{48,72},{56,80},{64,... | collective-permute-start | bytes 2949128 | tf_op jit(solution)/shard_map/ppermute | solution.py:15
  23.0 67.2 %collective-permute-start.3 = (bf16[2,384,640]{2,1,0:T(8,128)(2,1)}, bf16[2,384,640]{2,1,0:T(8,128)(2,1)}, u32[]{:S(2)}, u32[]{:S(2)}) collective-permute-start(bf16[2,384,640]{2,1,0:T(8,128)(2,1)} %pad_maximum_fusion), channel_id=1, source_target_pairs={{0,32},{8,40},{16,48},{24,56},{32,64},{40,72},{48,80},{56,88},{64,... | collective-permute-start | bytes 2949128 | tf_op jit(solution)/shard_map/ppermute | solution.py:15
  156.0 2.5 copy-start
Sparse Core Ops, SparseCore 0:
  10.6 142.9 all-gather.2
  156.9 84.6 all-gather.4
  250.6 52.9 reduce-scatter.1

commit v2 on v1

--- a/solution.py
+++ b/solution.py
@@ -15,10 +15,19 @@
     return lax.ppermute(value, axis, [(source, source + steps) for source in range(initial, last)])
 
 
+FRAME_AXES = ("y", "x", "c")
+
+
+def gather_frames(value, axis):
+    for name in reversed(FRAME_AXES):
+        value = lax.all_gather(value, name, axis=axis, tiled=True)
+    return value
+
+
 def gather_text(text_keys, text_values):
     width = text_keys.shape[1]
     both = jnp.concatenate([text_keys, text_values], axis=1)
-    full = lax.all_gather(both, "tm", axis=0, tiled=True)
+    full = gather_frames(both, 0)
     return full[:, :width], full[:, width:]
 
 
@@ -28,13 +37,13 @@
     local_heads = width // HD
     groups = lax.axis_size("head")
     scale = 1.0 / math.sqrt(HD)
-    position = lax.axis_index("tm")
+    position = lax.axis_index(FRAME_AXES)
     text_k, text_v = gather_text(text_keys, text_values)
-    weight_all = lax.all_gather(out_weight, "tm", axis=1, tiled=True)
+    weight_all = gather_frames(out_weight, 1)
     kv = jnp.stack([keys, values])
     kv_list = [kv]
     for step in range(1, WIN + 1):
-        kv_list.append(from_behind(kv, "tm", step))
+        kv_list.append(from_behind(kv, FRAME_AXES, step))
     token_ids = jnp.arange(rows, dtype=jnp.int32)
     own_window = windows[position]
     mask_list = []
@@ -76,19 +85,24 @@
 
 
 def solution(mesh):
+    frames = mesh.devices.shape[0]
+    cores = 2
+    xs = 4 if frames % (4 * cores) == 0 else 1
+    grid = mesh.devices.reshape(frames // (xs * cores), xs, cores, mesh.devices.shape[1])
+    fine = jax.sharding.Mesh(grid, FRAME_AXES + ("head",))
     return jax.shard_map(
         on_device,
-        mesh=mesh,
+        mesh=fine,
         in_specs=(
-            P("tm", "head"),
-            P("tm", "head"),
-            P("tm", "head"),
-            P("tm", "head"),
-            P("tm", "head"),
-            P("head", "tm"),
+            P(FRAME_AXES, "head"),
+            P(FRAME_AXES, "head"),
+            P(FRAME_AXES, "head"),
+            P(FRAME_AXES, "head"),
+            P(FRAME_AXES, "head"),
+            P("head", FRAME_AXES),
             P(),
             P(),
         ),
-        out_specs=P("tm", "head"),
+        out_specs=P(FRAME_AXES, "head"),
         check_vma=False,
     )

time: 311 us -> 301 us (0.968)
  waiting for transfers between devices: 228 us -> 186 us
  blocking collectives: 0 us -> 35.1 us
    all_gather x2, waiting for transfers between devices: 129 us -> 5.69 us  [gather_frames(): value = lax.all_gather(value, name, axis=axis, tiled=True)]
    reduce_scatter x1, waiting for transfers between devices: 53.1 us -> 134 us  [on_device(): lax.psum_scatter(partial_out.astype(jnp.bfloat16), 'head', scatter_dimens...]
    all_gather x0 -> x4, blocking collectives: none -> 35.1 us  [gather_frames(): value = lax.all_gather(value, name, axis=axis, tiled=True)]
    unnamed x12 -> x16, local copies, waits for them, and re-layouts: 11.6 us -> 11.6 us
  transfers between devices with their start and end apart: 7 -> 7, of which waited for: 6 -> 5; matrix products, arithmetic and copies ran while one was open for 13% -> 13% of each run, Pallas kernels for 0% -> 0%
where the time goes in v2:
time: 301 us; the launch traced here: 300 us
  waiting for transfers between devices  186 us (62%)
  blocking collectives  35.1 us (12%)
  matrix products  23.5 us (8%)
  between operations  16.5 us (5%)
  local copies, waits for them, and re-layouts  15.5 us (5%)
  starting transfers between devices  13.9 us (5%)
  other arithmetic  9.29 us (3%)
    reduce_scatter x1, waiting for transfers between devices, on_device(): lax.psum_scatter(partial_out.astype(jnp.bfloat16), 'head', scatter_dimens...  134 us
    ppermute x4, waiting for transfers between devices, from_behind(): lax.ppermute(value, axis, [(source, source + steps) for source in range(i...  46.8 us
    all_gather x4, blocking collectives, gather_frames(): value = lax.all_gather(value, name, axis=axis, tiled=True)  35.1 us
    ppermute x4, starting transfers between devices, from_behind(): lax.ppermute(value, axis, [(source, source + steps) for source in range(i...  13.8 us
    unnamed x16, local copies, waits for them, and re-layouts  11.6 us
    dot_general x5, matrix products, on_device(): jnp.dot(weights.astype(jnp.bfloat16), value_h, preferred_element_type=jnp...  9.29 us
    dot_general x1, matrix products, on_device(): jnp.einsum('rk,kgc->grc', attended_all, w3, preferred_element_type=jnp.fl...  8.89 us
  transfers between devices with their start and end apart: 7, of which 5 were waited for; matrix products, arithmetic and copies ran while one was open for 13% of the time, Pallas kernels for 0%

profile of v2, /device:TPU:1, one launch (start us, length us, event | category | flops | bytes accessed | tf_op | source)
XLA Modules:
  0.0 300.1 jit_solution(17963004261733054563)
XLA Ops:
  6.5 0.7 pad_maximum_fusion.1
  7.3 8.4 %all_gather.18 = bf16[16,1280]{1,0:T(8,128)(2,1)S(1)} all-gather(bf16[8,1280]{1,0:T(8,128)(2,1)S(1)} %pad_maximum_fusion.1), channel_id=1, replica_groups=mesh['y'=8,'x'=4,'c'=2,'head'=8] {'c'}, dimensions={0}, use_global_device_ids=true | all-gather | bytes 61440 | tf_op jit(solution)/shard_map/all_gather | solution.py:23
  15.6 9.9 %all_gather.19 = bf16[64,1280]{1,0:T(8,128)(2,1)} all-gather(bf16[16,1280]{1,0:T(8,128)(2,1)S(1)} %all_gather.18), channel_id=1, replica_groups=mesh['y'=8,'x'=4,'c'=2,'head'=8] {'x'}, dimensions={0}, use_global_device_ids=true | all-gather | bytes 204800 | tf_op jit(solution)/shard_map/all_gather | solution.py:23
  25.6 5.0 %all_gather.21 = bf16[640,160]{0,1:T(8,128)(2,1)S(1)} all-gather(bf16[640,80]{0,1:T(8,128)(2,1)} %param.13), channel_id=1, replica_groups=mesh['y'=8,'x'=4,'c'=2,'head'=8] {'c'}, dimensions={1}, use_global_device_ids=true | all-gather | bytes 307200 | tf_op jit(solution)/shard_map/all_gather | solution.py:23
  30.7 11.8 %all_gather.22 = bf16[640,640]{0,1:T(8,128)(2,1)} all-gather(bf16[640,160]{0,1:T(8,128)(2,1)S(1)} %all_gather.21), channel_id=1, replica_groups=mesh['y'=8,'x'=4,'c'=2,'head'=8] {'x'}, dimensions={1}, use_global_device_ids=true | all-gather | bytes 1024000 | tf_op jit(solution)/shard_map/all_gather | solution.py:23
  42.5 2.2 pad_maximum_fusion
  44.8 3.7 %collective-permute-start = (bf16[2,384,640]{2,1,0:T(8,128)(2,1)}, bf16[2,384,640]{2,1,0:T(8,128)(2,1)}, u32[]{:S(2)}, u32[]{:S(2)}) collective-permute-start(bf16[2,384,640]{2,1,0:T(8,128)(2,1)} %pad_maximum_fusion), channel_id=1, source_target_pairs={{0,8},{8,16},{16,24},{24,32},{32,40},{40,48},{48,56},{56,64},{64,7... | collective-permute-start | bytes 2949128 | tf_op jit(solution)/shard_map/ppermute | solution.py:15
  48.5 5.6 %collective-permute-start.1 = (bf16[2,384,640]{2,1,0:T(8,128)(2,1)}, bf16[2,384,640]{2,1,0:T(8,128)(2,1)}, u32[]{:S(2)}, u32[]{:S(2)}) collective-permute-start(bf16[2,384,640]{2,1,0:T(8,128)(2,1)} %pad_maximum_fusion), channel_id=1, source_target_pairs={{0,16},{8,24},{16,32},{24,40},{32,48},{40,56},{48,64},{56,72},{64,... | collective-permute-start | bytes 2949128 | tf_op jit(solution)/shard_map/ppermute | solution.py:15
  54.1 2.3 collective-permute-start.2
  56.4 2.3 collective-permute-start.3
  58.6 0.6 dynamic_slice.18
  62.5 0.7 fusion.104
  63.2 0.6 fusion.99
  63.8 0.3 dynamic-update-slice.17
  64.0 0.6 fusion.100
  64.6 0.3 dynamic-update-slice.18
  64.9 0.6 fusion.101
  65.5 0.3 dynamic-update-slice.19
  65.8 0.6 fusion.102
  66.7 0.7 fusion.103
  67.6 0.4 dynamic-update-slice.22
  68.0 2.1 constant_dynamic-update-slice_fusion
  70.0 2.0 fusion.88
  72.1 15.4 %collective-permute-done.1 = bf16[2,384,640]{2,1,0:T(8,128)(2,1)} collective-permute-done((bf16[2,384,640]{2,1,0:T(8,128)(2,1)}, bf16[2,384,640]{2,1,0:T(8,128)(2,1)}, u32[]{:S(2)}, u32[]{:S(2)}) %collective-permute-start.1) | collective-permute-done | bytes 983072 | tf_op jit(solution)/shard_map/ppermute | solution.py:15
  87.5 2.0 fusion.87
  89.5 19.1 %collective-permute-done.2 = bf16[2,384,640]{2,1,0:T(8,128)(2,1)} collective-permute-done((bf16[2,384,640]{2,1,0:T(8,128)(2,1)}, bf16[2,384,640]{2,1,0:T(8,128)(2,1)}, u32[]{:S(2)}, u32[]{:S(2)}) %collective-permute-start.2) | collective-permute-done | bytes 983072 | tf_op jit(solution)/shard_map/ppermute | solution.py:15
  108.6 2.1 fusion.86
  110.7 12.3 %collective-permute-done.3 = bf16[2,384,640]{2,1,0:T(8,128)(2,1)} collective-permute-done((bf16[2,384,640]{2,1,0:T(8,128)(2,1)}, bf16[2,384,640]{2,1,0:T(8,128)(2,1)}, u32[]{:S(2)}, u32[]{:S(2)}) %collective-permute-start.3) | collective-permute-done | bytes 983072 | tf_op jit(solution)/shard_map/ppermute | solution.py:15
  123.0 2.1 fusion.85
  125.1 2.3 slice_dynamic-update-slice_fusion
  127.5 1.8 fusion.105
  129.3 0.6 fusion.5
  129.9 0.9 fusion.106
  130.8 0.6 fusion.7
  131.4 0.9 fusion.107
  132.3 0.6 fusion.9
  133.0 0.9 fusion.108
  133.8 0.6 fusion.11
  134.5 0.9 fusion.109
  135.3 0.6 fusion.13
  136.0 1.9 fusion.72
  137.8 1.9 fusion.66
  139.7 1.9 fusion.60
  141.6 1.8 fusion.54
  143.4 1.8 fusion.48
  145.3 5.7 %all-gather.5.cloned.1.call-done = bf16[640,5120]{0,1:T(8,128)(2,1)} async-done(((bf16[640,640]{0,1:T(8,128)(2,1)}), bf16[640,5120]{0,1:T(8,128)(2,1)}) %all-gather.5.cloned.1.call-update) | async-done | bytes 6553616 | tf_op jit(solution)/shard_map/all_gather | solution.py:23
  151.0 8.9 %convert_bitcast_fusion = bf16[8,384,640]{2,1,0:T(8,128)(2,1)} fusion(bf16[640,8,640]{0,2,1:T(8,128)(2,1)} %bitcast.54, bf16[384,640]{1,0:T(8,128)(2,1)S(1)} %fusion.48), kind=kOutput, calls=%fused_computation.10 | convolution fusion | flops 2518548480 | bytes 10977280 | tf_op jit(solution)/shard_map/rk,kgc->grc/dot_general | solution.py:82
  159.9 133.7 %reduce-scatter.2.cloned.1.call-done = bf16[1,384,640]{2,1,0:T(8,128)(2,1)} async-done(((bf16[8,384,640]{2,1,0:T(8,128)(2,1)}), bf16[1,384,640]{2,1,0:T(8,128)(2,1)}) %reduce-scatter.2.cloned.1.call-update) | async-done | bytes 491536 | tf_op jit(solution)/shard_map/reduce_scatter | solution.py:83
  (18 shorter events, 0.7 us)
Async XLA Ops:
  6.5 52.1 %copy-start.2 = (s32[64]{0:T(128)S(1)}, s32[64]{0:T(128)}, u32[]{:S(2)}) copy-start(s32[64]{0:T(128)} %param.14) | copy-start | bytes 772
  6.5 56.0 %copy-start.1 = (s32[64]{0:T(128)S(1)}, s32[64]{0:T(128)}, u32[]{:S(2)}) copy-start(s32[64]{0:T(128)} %param.15) | copy-start | bytes 772
  6.5 118.6 %all-gather.3.cloned.1.call-start = ((), (), s32[]{:S(2)}) async-start(), calls=%async_computation.1 | async-start | bytes 1474560 | tf_op jit(solution)/shard_map/all_gather | solution.py:23
  25.6 125.4 %all-gather.5.cloned.1.call-start = ((), (), s32[]{:S(2)}) async-start(), calls=%async_computation.2 | async-start | bytes 7372800 | tf_op jit(solution)/shard_map/all_gather | solution.py:23
  42.5 251.1 %reduce-scatter.2.cloned.1.call-start = ((), (), s32[]{:S(2)}) async-start(), calls=%async_computation.3 | async-start | bytes 4423680 | tf_op jit(solution)/shard_map/reduce_scatter | solution.py:83
  44.8 25.2 %collective-permute-start = (bf16[2,384,640]{2,1,0:T(8,128)(2,1)}, bf16[2,384,640]{2,1,0:T(8,128)(2,1)}, u32[]{:S(2)}, u32[]{:S(2)}) collective-permute-start(bf16[2,384,640]{2,1,0:T(8,128)(2,1)} %pad_maximum_fusion), channel_id=1, source_target_pairs={{0,8},{8,16},{16,24},{24,32},{32,40},{40,48},{48,56},{56,64},{64,7... | collective-permute-start | bytes 2949128 | tf_op jit(solution)/shard_map/ppermute | solution.py:15
  48.5 39.0 %collective-permute-start.1 = (bf16[2,384,640]{2,1,0:T(8,128)(2,1)}, bf16[2,384,640]{2,1,0:T(8,128)(2,1)}, u32[]{:S(2)}, u32[]{:S(2)}) collective-permute-start(bf16[2,384,640]{2,1,0:T(8,128)(2,1)} %pad_maximum_fusion), channel_id=1, source_target_pairs={{0,16},{8,24},{16,32},{24,40},{32,48},{40,56},{48,64},{56,72},{64,... | collective-permute-start | bytes 2949128 | tf_op jit(solution)/shard_map/ppermute | solution.py:15
  54.1 54.6 %collective-permute-start.2 = (bf16[2,384,640]{2,1,0:T(8,128)(2,1)}, bf16[2,384,640]{2,1,0:T(8,128)(2,1)}, u32[]{:S(2)}, u32[]{:S(2)}) collective-permute-start(bf16[2,384,640]{2,1,0:T(8,128)(2,1)} %pad_maximum_fusion), channel_id=1, source_target_pairs={{0,24},{8,32},{16,40},{24,48},{32,56},{40,64},{48,72},{56,80},{64,... | collective-permute-start | bytes 2949128 | tf_op jit(solution)/shard_map/ppermute | solution.py:15
  56.4 66.7 %collective-permute-start.3 = (bf16[2,384,640]{2,1,0:T(8,128)(2,1)}, bf16[2,384,640]{2,1,0:T(8,128)(2,1)}, u32[]{:S(2)}, u32[]{:S(2)}) collective-permute-start(bf16[2,384,640]{2,1,0:T(8,128)(2,1)} %pad_maximum_fusion), channel_id=1, source_target_pairs={{0,32},{8,40},{16,48},{24,56},{32,64},{40,72},{48,80},{56,88},{64,... | collective-permute-start | bytes 2949128 | tf_op jit(solution)/shard_map/ppermute | solution.py:15
  127.5 2.5 copy-start
Sparse Core Ops, SparseCore 0:
  25.7 39.1 all-gather.2
  67.0 83.9 all-gather.4
  160.0 133.5 reduce-scatter.1

commit v3 on v2

--- a/solution.py
+++ b/solution.py
@@ -7,28 +7,25 @@
 
 HD = 128
 WIN = 4
+FRAME_AXES = ("y", "x", "c")
+CHIP_AXES = ("y", "x")
 
 
-def from_behind(value, axis, steps):
-    count = lax.axis_size(axis)
-    initial, last = (max(0, -steps), min(count, count - steps))
-    return lax.ppermute(value, axis, [(source, source + steps) for source in range(initial, last)])
+def shift_frames(value, steps):
+    count = lax.axis_size(FRAME_AXES)
+    return lax.ppermute(value, FRAME_AXES, [(source, source + steps) for source in range(count - steps)])
 
 
-FRAME_AXES = ("y", "x", "c")
+def ring_gather(value, axis):
+    count = lax.axis_size(axis)
+    pieces = [value]
+    for step in range(1, count):
+        pieces.append(lax.ppermute(value, axis, [(source, (source + step) % count) for source in range(count)]))
+    return jnp.concatenate(pieces, axis=0)
 
 
-def gather_frames(value, axis):
-    for name in reversed(FRAME_AXES):
-        value = lax.all_gather(value, name, axis=axis, tiled=True)
-    return value
-
-
-def gather_text(text_keys, text_values):
-    width = text_keys.shape[1]
-    both = jnp.concatenate([text_keys, text_values], axis=1)
-    full = gather_frames(both, 0)
-    return full[:, :width], full[:, width:]
+def swap_cores(value):
+    return lax.ppermute(value, "c", [(0, 1), (1, 0)])
 
 
 def on_device(queries, keys, values, text_keys, text_values, out_weight, windows, lengths):
@@ -38,12 +35,24 @@
     groups = lax.axis_size("head")
     scale = 1.0 / math.sqrt(HD)
     position = lax.axis_index(FRAME_AXES)
-    text_k, text_v = gather_text(text_keys, text_values)
-    weight_all = gather_frames(out_weight, 1)
-    kv = jnp.stack([keys, values])
-    kv_list = [kv]
-    for step in range(1, WIN + 1):
-        kv_list.append(from_behind(kv, FRAME_AXES, step))
+    core = lax.axis_index("c")
+    first_core = core == 0
+
+    text_both = jnp.concatenate([text_keys, text_values], axis=1)
+    text_half = ring_gather(ring_gather(text_both, "x"), "y")
+    text_all = jnp.concatenate([text_half, swap_cores(text_half)], axis=0)
+    text_k, text_v = text_all[:, :width], text_all[:, width:]
+
+    weight_half = lax.all_gather(out_weight, CHIP_AXES, axis=1, tiled=True)
+    weight_pair = jnp.stack([weight_half, swap_cores(weight_half)])
+
+    own = jnp.stack([keys, values])
+    back2 = shift_frames(own, 2)
+    back4 = shift_frames(own, 4)
+    back1 = swap_cores(jnp.where(first_core, own, back2))
+    back3 = swap_cores(jnp.where(first_core, back2, back4))
+    kv_list = [own, back1, back2, back3, back4]
+
     token_ids = jnp.arange(rows, dtype=jnp.int32)
     own_window = windows[position]
     mask_list = []
@@ -78,17 +87,23 @@
         )
         head_outputs.append(attended.astype(jnp.bfloat16))
     attended_all = jnp.concatenate(head_outputs, axis=1)
-    w3 = weight_all.reshape(width, groups, weight_all.shape[1] // groups)
-    partial_out = jnp.einsum("rk,kgc->grc", attended_all, w3, preferred_element_type=jnp.float32)
+    ys = lax.axis_size("y")
+    xs = lax.axis_size("x")
+    block = out_weight.shape[1]
+    w5 = weight_pair.reshape(2, width, ys, xs, block)
+    partial_out = jnp.einsum("rk,ckyxn->yrcxn", attended_all, w5, preferred_element_type=jnp.float32)
+    partial_out = partial_out.reshape(groups, rows, -1)
     mixed = lax.psum_scatter(partial_out.astype(jnp.bfloat16), "head", scatter_dimension=0, tiled=True)
-    return mixed.reshape(rows, -1)
+    mixed = mixed.reshape(rows, 2, xs, block)
+    mixed = jnp.where(first_core, mixed, mixed[:, ::-1])
+    return mixed.transpose(0, 2, 1, 3).reshape(rows, -1)
 
 
 def solution(mesh):
-    frames = mesh.devices.shape[0]
+    frames, heads = mesh.devices.shape
     cores = 2
     xs = 4 if frames % (4 * cores) == 0 else 1
-    grid = mesh.devices.reshape(frames // (xs * cores), xs, cores, mesh.devices.shape[1])
+    grid = mesh.devices.reshape(frames // (xs * cores), xs, cores, heads)
     fine = jax.sharding.Mesh(grid, FRAME_AXES + ("head",))
     return jax.shard_map(
         on_device,

time: 301 us -> 246 us (0.82)
  waiting for transfers between devices: 186 us -> 106 us
  starting transfers between devices: 13.9 us -> 61 us
  blocking collectives: 35.1 us -> 0 us
  local copies, waits for them, and re-layouts: 15.5 us -> 27.7 us
  other arithmetic: 9.29 us -> 13.3 us
  matrix products: 23.5 us -> 20 us
    reduce_scatter x1, waiting for transfers between devices: 134 us -> 69.8 us  [on_device(): lax.psum_scatter(partial_out.astype(jnp.bfloat16), 'head', scatter_dimens...]
    ppermute x4 -> x16, starting transfers between devices: 13.8 us -> 61 us  [the longest x10 39.7 us: ring_gather(): lax.ppermute(value, axis, [(source, (source + step) % count) for source i...]
    ppermute x4 -> x16, waiting for transfers between devices: 46.8 us -> 0.04 us  [the longest x10 0.03 us: ring_gather(): lax.ppermute(value, axis, [(source, (source + step) % count) for source i...]
    all_gather x4 -> x0, blocking collectives: 35.1 us -> none  [gather_frames(): value = lax.all_gather(value, name, axis=axis, tiled=True)]
    all_gather x2 -> x1, waiting for transfers between devices: 5.69 us -> 36.1 us  [on_device(): weight_half = lax.all_gather(out_weight, CHIP_AXES, axis=1, tiled=True)]
    dot_general x5, matrix products: 5.33 us -> 11.7 us  [on_device(): lax.dot_general(query_h, key_h, (((1,), (1,)), ((), ())), preferred_eleme...]
    unnamed x16 -> x43, local copies, waits for them, and re-layouts: 11.6 us -> 17.2 us
    dot_general x5, matrix products: 9.29 us -> 3.72 us  [on_device(): jnp.dot(weights.astype(jnp.bfloat16), value_h, preferred_element_type=jnp...]
  transfers between devices with their start and end apart: 7 -> 18, of which waited for: 5 -> 2; matrix products, arithmetic and copies ran while one was open for 13% -> 18% of each run, Pallas kernels for 0% -> 0%
where the time goes in v3:
time: 246 us; the launch traced here: 245 us
  waiting for transfers between devices  106 us (43%)
  starting transfers between devices  61 us (25%)
  local copies, waits for them, and re-layouts  27.7 us (11%)
  matrix products  20 us (8%)
  between operations  17.1 us (7%)
  other arithmetic  13.3 us (5%)
    reduce_scatter x1, waiting for transfers between devices, on_device(): lax.psum_scatter(partial_out.astype(jnp.bfloat16), 'head', scatter_dimens...  69.8 us
    ppermute x10, starting transfers between devices, ring_gather(): lax.ppermute(value, axis, [(source, (source + step) % count) for source i...  39.7 us
    all_gather x1, waiting for transfers between devices, on_device(): weight_half = lax.all_gather(out_weight, CHIP_AXES, axis=1, tiled=True)  36.1 us
    unnamed x43, local copies, waits for them, and re-layouts  17.2 us
    ppermute x4, starting transfers between devices, swap_cores(): return lax.ppermute(value, 'c', [(0, 1), (1, 0)])  16.3 us
    dot_general x5, matrix products, on_device(): lax.dot_general(query_h, key_h, (((1,), (1,)), ((), ())), preferred_eleme...  11.7 us
    reduce_sum x5, other arithmetic, on_device(): total = jnp.sum(weights, axis=-1, keepdims=True)  5.22 us
    ppermute x2, starting transfers between devices, shift_frames(): lax.ppermute(value, FRAME_AXES, [(source, source + steps) for source in r...  5.06 us
  transfers between devices with their start and end apart: 18, of which 2 were waited for; matrix products, arithmetic and copies ran while one was open for 18% of the time, Pallas kernels for 0%

profile of v3, /device:TPU:1, one launch (start us, length us, event | category | flops | bytes accessed | tf_op | source)
XLA Modules:
  0.0 245.2 jit_solution(1290223051785092219)
XLA Ops:
  6.5 1.4 constant_dynamic-update-slice_fusion.13
  7.9 1.3 constant_dynamic-update-slice_fusion.12
  9.2 3.9 %collective-permute-start.5 = (bf16[8,1280]{1,0:T(8,128)(2,1)S(1)}, bf16[8,1280]{1,0:T(8,128)(2,1)S(1)}, u32[]{:S(2)}, u32[]{:S(2)}) collective-permute-start(bf16[8,1280]{1,0:T(8,128)(2,1)S(1)} %get-tuple-element.39), channel_id=1, source_target_pairs={{0,16},{16,32},{32,48},{48,0},{1,17},{17,33},{33,49},{49,1},{2,18}... | collective-permute-start | bytes 61448 | tf_op jit(solution)/shard_map/ppermute | solution.py:23
  13.2 4.4 %collective-permute-start.6 = (bf16[8,1280]{1,0:T(8,128)(2,1)S(1)}, bf16[8,1280]{1,0:T(8,128)(2,1)S(1)}, u32[]{:S(2)}, u32[]{:S(2)}) collective-permute-start(bf16[8,1280]{1,0:T(8,128)(2,1)S(1)} %get-tuple-element.39), channel_id=1, source_target_pairs={{0,32},{16,48},{32,0},{48,16},{1,33},{17,49},{33,1},{49,17},{2,34}... | collective-permute-start | bytes 61448 | tf_op jit(solution)/shard_map/ppermute | solution.py:23
  17.6 3.1 %collective-permute-start.7 = (bf16[8,1280]{1,0:T(8,128)(2,1)S(1)}, bf16[8,1280]{1,0:T(8,128)(2,1)S(1)}, u32[]{:S(2)}, u32[]{:S(2)}) collective-permute-start(bf16[8,1280]{1,0:T(8,128)(2,1)S(1)} %get-tuple-element.39), channel_id=1, source_target_pairs={{0,48},{16,0},{32,16},{48,32},{1,49},{17,1},{33,17},{49,33},{2,50}... | collective-permute-start | bytes 61448 | tf_op jit(solution)/shard_map/ppermute | solution.py:23
  20.6 2.2 pad_maximum_fusion
  22.9 2.3 collective-permute-start.1
  25.1 2.8 %collective-permute-start.3 = (bf16[2,384,640]{2,1,0:T(8,128)(2,1)}, bf16[2,384,640]{2,1,0:T(8,128)(2,1)S(1)}, u32[]{:S(2)}, u32[]{:S(2)}) collective-permute-start(bf16[2,384,640]{2,1,0:T(8,128)(2,1)} %pad_maximum_fusion), channel_id=1, source_target_pairs={{0,32},{8,40},{16,48},{24,56},{32,64},{40,72},{48,80},{56,88},{64,... | collective-permute-start | bytes 2949128 | tf_op jit(solution)/shard_map/ppermute | solution.py:16
  28.0 1.2 dynamic_slice.18
  32.5 1.5 fusion.112
  34.1 3.1 %collective-permute-start.8 = (bf16[32,1280]{1,0:T(8,128)(2,1)S(1)}, bf16[32,1280]{1,0:T(8,128)(2,1)S(1)}, u32[]{:S(2)}, u32[]{:S(2)}) collective-permute-start(bf16[32,1280]{1,0:T(8,128)(2,1)S(1)} %pad_maximum_fusion.1), channel_id=1, source_target_pairs={{0,64},{64,128},{128,192},{192,256},{256,320},{320,384},{384,448},... | collective-permute-start | bytes 245768 | tf_op jit(solution)/shard_map/ppermute | solution.py:23
  37.3 4.2 %collective-permute-start.9 = (bf16[32,1280]{1,0:T(8,128)(2,1)S(1)}, bf16[32,1280]{1,0:T(8,128)(2,1)S(1)}, u32[]{:S(2)}, u32[]{:S(2)}) collective-permute-start(bf16[32,1280]{1,0:T(8,128)(2,1)S(1)} %pad_maximum_fusion.1), channel_id=1, source_target_pairs={{0,128},{64,192},{128,256},{192,320},{256,384},{320,448},{384,0},{... | collective-permute-start | bytes 245768 | tf_op jit(solution)/shard_map/ppermute | solution.py:23
  41.5 4.6 %collective-permute-start.10 = (bf16[32,1280]{1,0:T(8,128)(2,1)S(1)}, bf16[32,1280]{1,0:T(8,128)(2,1)S(1)}, u32[]{:S(2)}, u32[]{:S(2)}) collective-permute-start(bf16[32,1280]{1,0:T(8,128)(2,1)S(1)} %pad_maximum_fusion.1), channel_id=1, source_target_pairs={{0,192},{64,256},{128,320},{192,384},{256,448},{320,0},{384,64},{4... | collective-permute-start | bytes 245768 | tf_op jit(solution)/shard_map/ppermute | solution.py:23
  48.0 3.5 %collective-permute-start.11 = (bf16[32,1280]{1,0:T(8,128)(2,1)S(1)}, bf16[32,1280]{1,0:T(8,128)(2,1)S(1)}, u32[]{:S(2)}, u32[]{:S(2)}) collective-permute-start(bf16[32,1280]{1,0:T(8,128)(2,1)S(1)} %pad_maximum_fusion.1), channel_id=1, source_target_pairs={{0,256},{64,320},{128,384},{192,448},{256,0},{320,64},{384,128},{4... | collective-permute-start | bytes 245768 | tf_op jit(solution)/shard_map/ppermute | solution.py:23
  51.5 0.7 constant_dynamic-update-slice_fusion.8
  52.2 4.9 %collective-permute-start.12 = (bf16[32,1280]{1,0:T(8,128)(2,1)S(1)}, bf16[32,1280]{1,0:T(8,128)(2,1)S(1)}, u32[]{:S(2)}, u32[]{:S(2)}) collective-permute-start(bf16[32,1280]{1,0:T(8,128)(2,1)S(1)} %pad_maximum_fusion.1), channel_id=1, source_target_pairs={{0,320},{64,384},{128,448},{192,0},{256,64},{320,128},{384,192},{4... | collective-permute-start | bytes 245768 | tf_op jit(solution)/shard_map/ppermute | solution.py:23
  57.8 5.0 %collective-permute-start.13 = (bf16[32,1280]{1,0:T(8,128)(2,1)S(1)}, bf16[32,1280]{1,0:T(8,128)(2,1)S(1)}, u32[]{:S(2)}, u32[]{:S(2)}) collective-permute-start(bf16[32,1280]{1,0:T(8,128)(2,1)S(1)} %pad_maximum_fusion.1), channel_id=1, source_target_pairs={{0,384},{64,448},{128,0},{192,64},{256,128},{320,192},{384,256},{4... | collective-permute-start | bytes 245768 | tf_op jit(solution)/shard_map/ppermute | solution.py:23
  63.4 3.0 %collective-permute-start.14 = (bf16[32,1280]{1,0:T(8,128)(2,1)S(1)}, bf16[32,1280]{1,0:T(8,128)(2,1)S(1)}, u32[]{:S(2)}, u32[]{:S(2)}) collective-permute-start(bf16[32,1280]{1,0:T(8,128)(2,1)S(1)} %pad_maximum_fusion.1), channel_id=1, source_target_pairs={{0,448},{64,0},{128,64},{192,128},{256,192},{320,256},{384,320},{4... | collective-permute-start | bytes 245768 | tf_op jit(solution)/shard_map/ppermute | solution.py:23
  67.1 0.7 constant_dynamic-update-slice_fusion.4
  68.5 1.5 broadcast_select_fusion
  70.0 5.7 %collective-permute-start.2 = (bf16[2,384,640]{2,1,0:T(8,128)(2,1)}, bf16[2,384,640]{2,1,0:T(8,128)(2,1)}, u32[]{:S(2)}, u32[]{:S(2)}) collective-permute-start(bf16[2,384,640]{2,1,0:T(8,128)(2,1)} %get-tuple-element.16), channel_id=1, source_target_pairs={{0,8},{8,0},{1,9},{9,1},{2,10},{10,2},{3,11},{11,3},{4,12},{12,4},... | collective-permute-start | bytes 2949128 | tf_op jit(solution)/shard_map/ppermute | solution.py:28
  76.3 1.9 collective-permute-start.15
  81.7 2.4 collective-permute-start.4
  85.3 2.0 constant_dynamic-update-slice_fusion.14
  87.3 1.3 fusion.95
  88.9 1.4 fusion.93
  90.4 1.5 slice_dynamic-update-slice_fusion
  92.0 1.6 copy-done.7
  93.6 0.9 fusion.113
  95.1 2.8 %fusion.114 = (f32[384]{0:T(512)S(1)}, f32[2432,384]{1,0:T(8,128)}) fusion(bf16[384,640]{1,0:T(8,128)(2,1)S(1)} %copy-done.9, bf16[2432,640]{1,0:T(8,128)(2,1)S(1)} %get-tuple-element.6, pred[2432]{0:T(1024)(128)(4,1)S(1)} %dynamic-update-slice.49), kind=kOutput, calls=%fused_computation.137 | convolution fusion | flops 241876608 | bytes 4461056 | tf_op jit(solution)/shard_map/dot_general | solution.py:75
  97.9 2.8 %fusion.115 = (f32[384]{0:T(512)S(1)}, f32[2432,384]{1,0:T(8,128)}) fusion(bf16[384,640]{1,0:T(8,128)(2,1)S(1)} %copy-done.9, bf16[2432,640]{1,0:T(8,128)(2,1)S(1)} %get-tuple-element.6, pred[2432]{0:T(1024)(128)(4,1)S(1)} %dynamic-update-slice.49), kind=kOutput, calls=%fused_computation.138 | convolution fusion | flops 241876608 | bytes 4461056 | tf_op jit(solution)/shard_map/dot_general | solution.py:75
  100.7 36.1 %all-gather.2.cloned.1.call-done = bf16[640,2560]{0,1:T(8,128)(2,1)} async-done(((bf16[640,80]{0,1:T(8,128)(2,1)}), bf16[640,2560]{0,1:T(8,128)(2,1)}) %all-gather.2.cloned.1.call-update) | async-done | bytes 3276816 | tf_op jit(solution)/shard_map/all_gather | solution.py:46
  136.8 6.3 %collective-permute-start = (bf16[640,2560]{0,1:T(8,128)(2,1)}, bf16[640,2560]{0,1:T(8,128)(2,1)S(1)}, u32[]{:S(2)}, u32[]{:S(2)}) collective-permute-start(bf16[640,2560]{0,1:T(8,128)(2,1)} %all-gather.2.cloned.1.call-done), channel_id=1, source_target_pairs={{0,8},{8,0},{1,9},{9,1},{2,10},{10,2},{3,11},{11,3},{4,12},{12,4},... | collective-permute-start | bytes 9830408 | tf_op jit(solution)/shard_map/ppermute | solution.py:28
  143.2 2.7 %fusion.11 = f32[384]{0:T(512)S(1)} fusion(f32[2432,384]{1,0:T(8,128)} %get-tuple-element.51, f32[384]{0:T(512)S(1)} %get-tuple-element.50), kind=kLoop, calls=%fused_computation.22 | loop fusion | flops 1867392 | bytes 3738624 | tf_op jit(solution)/shard_map/reduce_sum | solution.py:83
  146.5 2.5 %fusion.116 = (f32[384]{0:T(512)S(1)}, f32[2432,384]{1,0:T(8,128)S(1)}) fusion(bf16[384,640]{1,0:T(8,128)(2,1)S(1)} %copy-done.9, bf16[2432,640]{1,0:T(8,128)(2,1)} %copy-done.6, pred[2432]{0:T(1024)(128)(4,1)S(1)} %dynamic-update-slice.49), kind=kOutput, calls=%fused_computation.139 | convolution fusion | flops 241876608 | bytes 4461056 | tf_op jit(solution)/shard_map/dot_general | solution.py:75
  149.7 2.7 %fusion.117 = (f32[384]{0:T(512)S(1)}, f32[2432,384]{1,0:T(8,128)S(1)}) fusion(bf16[384,640]{1,0:T(8,128)(2,1)S(1)} %copy-done.9, bf16[2432,640]{1,0:T(8,128)(2,1)} %copy-done.6, pred[2432]{0:T(1024)(128)(4,1)S(1)} %dynamic-update-slice.49), kind=kOutput, calls=%fused_computation.140 | convolution fusion | flops 241876608 | bytes 4461056 | tf_op jit(solution)/shard_map/dot_general | solution.py:75
  153.0 0.7 fusion.78
  153.7 1.3 copy-done.3
  155.1 0.8 fusion.72
  155.8 0.7 fusion.66
  156.6 0.8 fusion.60
  157.3 0.7 fusion.54
  158.1 1.2 copy-done.10
  159.3 4.6 %convert_bitcast_fusion = bf16[8,384,2,4,80]{1,4,3,0,2:T(8,128)(2,1)S(1)} fusion(bf16[1,640,8,4,80]{1,4,3,2,0:T(8,128)(2,1)S(1)} %bitcast.66, bf16[1,640,8,4,80]{1,4,3,2,0:T(8,128)(2,1)S(1)} %bitcast.65, bf16[384,640]{1,0:T(8,128)(2,1)S(1)} %fusion.54), kind=kOutput, calls=%fused_computation.14 | convolution fusion | flops 2521825280 | bytes 10977280 | tf_op jit(solution)/shard_map/rk,ckyxn->yrcxn/dot_general | solution.py:94
  163.8 2.3 copy.9
  166.2 69.8 %reduce-scatter.2.cloned.1.call-done = bf16[1,384,640]{1,2,0:T(8,128)(2,1)} async-done(((bf16[8,384,640]{1,2,0:T(8,128)(2,1)}), bf16[1,384,640]{1,2,0:T(8,128)(2,1)}) %reduce-scatter.2.cloned.1.call-update) | async-done | bytes 491536 | tf_op jit(solution)/shard_map/reduce_scatter | solution.py:96
  236.0 1.3 fusion.91
  237.3 1.0 copy.11
  (69 shorter events, 13.0 us)
Async XLA Ops:
  6.5 61.9 %copy-start.5 = (bf16[384,640]{1,0:T(8,128)(2,1)S(1)}, bf16[384,640]{1,0:T(8,128)(2,1)}, u32[]{:S(2)}) copy-start(bf16[384,640]{1,0:T(8,128)(2,1)} %param.10) | copy-start | bytes 1474564
  6.5 61.9 %copy-start.4 = (bf16[384,640]{1,0:T(8,128)(2,1)S(1)}, bf16[384,640]{1,0:T(8,128)(2,1)}, u32[]{:S(2)}) copy-start(bf16[384,640]{1,0:T(8,128)(2,1)} %param.9) | copy-start | bytes 1474564
  6.5 130.3 %all-gather.2.cloned.1.call-start = ((), (), s32[]{:S(2)}) async-start(), calls=%async_computation.1 | async-start | bytes 3379200 | tf_op jit(solution)/shard_map/all_gather | solution.py:46
  9.2 24.8 %collective-permute-start.5 = (bf16[8,1280]{1,0:T(8,128)(2,1)S(1)}, bf16[8,1280]{1,0:T(8,128)(2,1)S(1)}, u32[]{:S(2)}, u32[]{:S(2)}) collective-permute-start(bf16[8,1280]{1,0:T(8,128)(2,1)S(1)} %get-tuple-element.39), channel_id=1, source_target_pairs={{0,16},{16,32},{32,48},{48,0},{1,17},{17,33},{33,49},{49,1},{2,18}... | collective-permute-start | bytes 61448 | tf_op jit(solution)/shard_map/ppermute | solution.py:23
  13.2 20.9 %collective-permute-start.6 = (bf16[8,1280]{1,0:T(8,128)(2,1)S(1)}, bf16[8,1280]{1,0:T(8,128)(2,1)S(1)}, u32[]{:S(2)}, u32[]{:S(2)}) collective-permute-start(bf16[8,1280]{1,0:T(8,128)(2,1)S(1)} %get-tuple-element.39), channel_id=1, source_target_pairs={{0,32},{16,48},{32,0},{48,16},{1,33},{17,49},{33,1},{49,17},{2,34}... | collective-permute-start | bytes 61448 | tf_op jit(solution)/shard_map/ppermute | solution.py:23
  17.6 16.5 %collective-permute-start.7 = (bf16[8,1280]{1,0:T(8,128)(2,1)S(1)}, bf16[8,1280]{1,0:T(8,128)(2,1)S(1)}, u32[]{:S(2)}, u32[]{:S(2)}) collective-permute-start(bf16[8,1280]{1,0:T(8,128)(2,1)S(1)} %get-tuple-element.39), channel_id=1, source_target_pairs={{0,48},{16,0},{32,16},{48,32},{1,49},{17,1},{33,17},{49,33},{2,50}... | collective-permute-start | bytes 61448 | tf_op jit(solution)/shard_map/ppermute | solution.py:23
  22.9 45.6 %collective-permute-start.1 = (bf16[2,384,640]{2,1,0:T(8,128)(2,1)}, bf16[2,384,640]{2,1,0:T(8,128)(2,1)S(1)}, u32[]{:S(2)}, u32[]{:S(2)}) collective-permute-start(bf16[2,384,640]{2,1,0:T(8,128)(2,1)} %pad_maximum_fusion), channel_id=1, source_target_pairs={{0,16},{8,24},{16,32},{24,40},{32,48},{40,56},{48,64},{56,72},{64,... | collective-permute-start | bytes 2949128 | tf_op jit(solution)/shard_map/ppermute | solution.py:16
  25.1 43.3 %collective-permute-start.3 = (bf16[2,384,640]{2,1,0:T(8,128)(2,1)}, bf16[2,384,640]{2,1,0:T(8,128)(2,1)S(1)}, u32[]{:S(2)}, u32[]{:S(2)}) collective-permute-start(bf16[2,384,640]{2,1,0:T(8,128)(2,1)} %pad_maximum_fusion), channel_id=1, source_target_pairs={{0,32},{8,40},{16,48},{24,56},{32,64},{40,72},{48,80},{56,88},{64,... | collective-permute-start | bytes 2949128 | tf_op jit(solution)/shard_map/ppermute | solution.py:16
  27.9 208.0 %reduce-scatter.2.cloned.1.call-start = ((), (), s32[]{:S(2)}) async-start(), calls=%async_computation.2 | async-start | bytes 4423680 | tf_op jit(solution)/shard_map/reduce_scatter | solution.py:96
  34.1 13.9 %collective-permute-start.8 = (bf16[32,1280]{1,0:T(8,128)(2,1)S(1)}, bf16[32,1280]{1,0:T(8,128)(2,1)S(1)}, u32[]{:S(2)}, u32[]{:S(2)}) collective-permute-start(bf16[32,1280]{1,0:T(8,128)(2,1)S(1)} %pad_maximum_fusion.1), channel_id=1, source_target_pairs={{0,64},{64,128},{128,192},{192,256},{256,320},{320,384},{384,448},... | collective-permute-start | bytes 245768 | tf_op jit(solution)/shard_map/ppermute | solution.py:23
  37.3 15.0 %collective-permute-start.9 = (bf16[32,1280]{1,0:T(8,128)(2,1)S(1)}, bf16[32,1280]{1,0:T(8,128)(2,1)S(1)}, u32[]{:S(2)}, u32[]{:S(2)}) collective-permute-start(bf16[32,1280]{1,0:T(8,128)(2,1)S(1)} %pad_maximum_fusion.1), channel_id=1, source_target_pairs={{0,128},{64,192},{128,256},{192,320},{256,384},{320,448},{384,0},{... | collective-permute-start | bytes 245768 | tf_op jit(solution)/shard_map/ppermute | solution.py:23
  41.5 16.3 %collective-permute-start.10 = (bf16[32,1280]{1,0:T(8,128)(2,1)S(1)}, bf16[32,1280]{1,0:T(8,128)(2,1)S(1)}, u32[]{:S(2)}, u32[]{:S(2)}) collective-permute-start(bf16[32,1280]{1,0:T(8,128)(2,1)S(1)} %pad_maximum_fusion.1), channel_id=1, source_target_pairs={{0,192},{64,256},{128,320},{192,384},{256,448},{320,0},{384,64},{4... | collective-permute-start | bytes 245768 | tf_op jit(solution)/shard_map/ppermute | solution.py:23
  48.0 15.4 %collective-permute-start.11 = (bf16[32,1280]{1,0:T(8,128)(2,1)S(1)}, bf16[32,1280]{1,0:T(8,128)(2,1)S(1)}, u32[]{:S(2)}, u32[]{:S(2)}) collective-permute-start(bf16[32,1280]{1,0:T(8,128)(2,1)S(1)} %pad_maximum_fusion.1), channel_id=1, source_target_pairs={{0,256},{64,320},{128,384},{192,448},{256,0},{320,64},{384,128},{4... | collective-permute-start | bytes 245768 | tf_op jit(solution)/shard_map/ppermute | solution.py:23
  52.2 14.9 %collective-permute-start.12 = (bf16[32,1280]{1,0:T(8,128)(2,1)S(1)}, bf16[32,1280]{1,0:T(8,128)(2,1)S(1)}, u32[]{:S(2)}, u32[]{:S(2)}) collective-permute-start(bf16[32,1280]{1,0:T(8,128)(2,1)S(1)} %pad_maximum_fusion.1), channel_id=1, source_target_pairs={{0,320},{64,384},{128,448},{192,0},{256,64},{320,128},{384,192},{4... | collective-permute-start | bytes 245768 | tf_op jit(solution)/shard_map/ppermute | solution.py:23
  57.8 10.0 %collective-permute-start.13 = (bf16[32,1280]{1,0:T(8,128)(2,1)S(1)}, bf16[32,1280]{1,0:T(8,128)(2,1)S(1)}, u32[]{:S(2)}, u32[]{:S(2)}) collective-permute-start(bf16[32,1280]{1,0:T(8,128)(2,1)S(1)} %pad_maximum_fusion.1), channel_id=1, source_target_pairs={{0,384},{64,448},{128,0},{192,64},{256,128},{320,192},{384,256},{4... | collective-permute-start | bytes 245768 | tf_op jit(solution)/shard_map/ppermute | solution.py:23
  63.4 12.2 %collective-permute-start.14 = (bf16[32,1280]{1,0:T(8,128)(2,1)S(1)}, bf16[32,1280]{1,0:T(8,128)(2,1)S(1)}, u32[]{:S(2)}, u32[]{:S(2)}) collective-permute-start(bf16[32,1280]{1,0:T(8,128)(2,1)S(1)} %pad_maximum_fusion.1), channel_id=1, source_target_pairs={{0,448},{64,0},{128,64},{192,128},{256,192},{320,256},{384,320},{4... | collective-permute-start | bytes 245768 | tf_op jit(solution)/shard_map/ppermute | solution.py:23
  70.0 17.4 %collective-permute-start.2 = (bf16[2,384,640]{2,1,0:T(8,128)(2,1)}, bf16[2,384,640]{2,1,0:T(8,128)(2,1)}, u32[]{:S(2)}, u32[]{:S(2)}) collective-permute-start(bf16[2,384,640]{2,1,0:T(8,128)(2,1)} %get-tuple-element.16), channel_id=1, source_target_pairs={{0,8},{8,0},{1,9},{9,1},{2,10},{10,2},{3,11},{11,3},{4,12},{12,4},... | collective-permute-start | bytes 2949128 | tf_op jit(solution)/shard_map/ppermute | solution.py:28
  76.3 9.0 %collective-permute-start.15 = (bf16[256,1280]{1,0:T(8,128)(2,1)}, bf16[256,1280]{1,0:T(8,128)(2,1)}, u32[]{:S(2)}, u32[]{:S(2)}) collective-permute-start(bf16[256,1280]{1,0:T(8,128)(2,1)} %get-tuple-element.17), channel_id=1, source_target_pairs={{0,8},{8,0},{1,9},{9,1},{2,10},{10,2},{3,11},{11,3},{4,12},{12,4},... | collective-permute-start | bytes 1966088 | tf_op jit(solution)/shard_map/ppermute | solution.py:28
  81.7 7.2 %collective-permute-start.4 = (bf16[2,384,640]{2,1,0:T(8,128)(2,1)}, bf16[2,384,640]{2,1,0:T(8,128)(2,1)}, u32[]{:S(2)}, u32[]{:S(2)}) collective-permute-start(bf16[2,384,640]{2,1,0:T(8,128)(2,1)} %get-tuple-element.15), channel_id=1, source_target_pairs={{0,8},{8,0},{1,9},{9,1},{2,10},{10,2},{3,11},{11,3},{4,12},{12,4},... | collective-permute-start | bytes 2949128 | tf_op jit(solution)/shard_map/ppermute | solution.py:28
  88.9 4.7 %copy-start.9 = (bf16[384,640]{1,0:T(8,128)(2,1)S(1)}, bf16[384,640]{1,0:T(8,128)(2,1)}, u32[]{:S(2)}) copy-start(bf16[384,640]{1,0:T(8,128)(2,1)} %param.8) | copy-start | bytes 1474564
  92.0 1.6 copy-start.7
  93.6 4.3 %copy-start.6 = (bf16[2432,640]{1,0:T(8,128)(2,1)}, bf16[2432,640]{1,0:T(8,128)(2,1)S(1)}, u32[]{:S(2)}) copy-start(bf16[2432,640]{1,0:T(8,128)(2,1)S(1)} %get-tuple-element.6) | copy-start | bytes 9338884
  94.5 3.4 %copy-start.1 = (f32[2432,384]{1,0:T(8,128)}, f32[2432,384]{1,0:T(8,128)S(1)}, u32[]{:S(2)}) copy-start(f32[2432,384]{1,0:T(8,128)S(1)} %get-tuple-element.49) | copy-start | bytes 11206660
  136.8 9.0 %copy-start = (f32[2432,384]{1,0:T(8,128)S(1)}, f32[2432,384]{1,0:T(8,128)}, u32[]{:S(2)}) copy-start(f32[2432,384]{1,0:T(8,128)} %get-tuple-element.53) | copy-start | bytes 11206660
  136.8 21.2 %collective-permute-start = (bf16[640,2560]{0,1:T(8,128)(2,1)}, bf16[640,2560]{0,1:T(8,128)(2,1)S(1)}, u32[]{:S(2)}, u32[]{:S(2)}) collective-permute-start(bf16[640,2560]{0,1:T(8,128)(2,1)} %all-gather.2.cloned.1.call-done), channel_id=1, source_target_pairs={{0,8},{8,0},{1,9},{9,1},{2,10},{10,2},{3,11},{11,3},{4,12},{12,4},... | collective-permute-start | bytes 9830408 | tf_op jit(solution)/shard_map/ppermute | solution.py:28
  149.7 3.3 %copy-start.2 = (f32[2432,384]{1,0:T(8,128)S(1)}, f32[2432,384]{1,0:T(8,128)}, u32[]{:S(2)}) copy-start(f32[2432,384]{1,0:T(8,128)} %copy-done.1) | copy-start | bytes 11206660
  149.7 3.3 %copy-start.8 = (bf16[2432,640]{1,0:T(8,128)(2,1)S(1)}, bf16[2432,640]{1,0:T(8,128)(2,1)}, u32[]{:S(2)}) copy-start(bf16[2432,640]{1,0:T(8,128)(2,1)} %copy-done.7) | copy-start | bytes 9338884
  153.0 2.1 copy-start.3
  157.3 1.9 copy-start.10
Sparse Core Ops, SparseCore 0:
  28.1 108.7 all-gather.1
  166.3 69.6 reduce-scatter.1

commit v4 on v3

--- a/solution.py
+++ b/solution.py
@@ -39,11 +39,17 @@
     first_core = core == 0
 
     text_both = jnp.concatenate([text_keys, text_values], axis=1)
-    text_half = ring_gather(ring_gather(text_both, "x"), "y")
+    tokens = text_both.shape[0]
+    chips = lax.axis_size(CHIP_AXES)
+    block = out_weight.shape[1]
+    text_cols = text_both.reshape(width, -1)
+    packed = jnp.concatenate([out_weight, text_cols], axis=1)
+    packed = lax.all_gather(packed, CHIP_AXES, axis=1, tiled=True).reshape(width, chips, -1)
+    weight_half = packed[:, :, :block].reshape(width, chips * block)
+    text_half = packed[:, :, block:].reshape(tokens, -1, chips, text_cols.shape[1])
+    text_half = text_half.transpose(2, 0, 1, 3).reshape(chips * tokens, 2 * width)
     text_all = jnp.concatenate([text_half, swap_cores(text_half)], axis=0)
     text_k, text_v = text_all[:, :width], text_all[:, width:]
-
-    weight_half = lax.all_gather(out_weight, CHIP_AXES, axis=1, tiled=True)
     weight_pair = jnp.stack([weight_half, swap_cores(weight_half)])
 
     own = jnp.stack([keys, values])
@@ -89,7 +95,6 @@
     attended_all = jnp.concatenate(head_outputs, axis=1)
     ys = lax.axis_size("y")
     xs = lax.axis_size("x")
-    block = out_weight.shape[1]
     w5 = weight_pair.reshape(2, width, ys, xs, block)
     partial_out = jnp.einsum("rk,ckyxn->yrcxn", attended_all, w5, preferred_element_type=jnp.float32)
     partial_out = partial_out.reshape(groups, rows, -1)

time: 246 us -> 249 us (1.012)
  starting transfers between devices: 61 us -> 24.9 us
  waiting for transfers between devices: 106 us -> 138 us
  matrix products: 20 us -> 26.7 us
    ppermute x10 -> x0, starting transfers between devices: 39.7 us -> none  [ring_gather(): lax.ppermute(value, axis, [(source, (source + step) % count) for source i...]
    ppermute x2, waiting for transfers between devices: 0.01 us -> 35.4 us  [shift_frames(): lax.ppermute(value, FRAME_AXES, [(source, source + steps) for source in r...]
    reduce_scatter x1, waiting for transfers between devices: 69.8 us -> 54.1 us  [on_device(): lax.psum_scatter(partial_out.astype(jnp.bfloat16), 'head', scatter_dimens...]
    all_gather x1, waiting for transfers between devices: 36.1 us -> 48.6 us  [on_device(): lax.all_gather(packed, CHIP_AXES, axis=1, tiled=True)]
    unnamed x43 -> x23, local copies, waits for them, and re-layouts: 17.2 us -> 8.98 us
    reshape x0 -> x3, local copies, waits for them, and re-layouts: none -> 6.82 us  [the longest x1 6.55 us: on_device(): text_half.transpose(2, 0, 1, 3).reshape(chips * tokens, 2 * width)]
    dot_general x5, matrix products: 3.72 us -> 9.23 us  [on_device(): jnp.dot(weights.astype(jnp.bfloat16), value_h, preferred_element_type=jnp...]
    slice x0 -> x3, local copies, waits for them, and re-layouts: none -> 4.92 us  [the longest x2 4.63 us: on_device(): packed[:, :, block:].reshape(tokens, -1, chips, text_cols.shape[1])]
  transfers between devices with their start and end apart: 18 -> 8, of which waited for: 2 -> 4; matrix products, arithmetic and copies ran while one was open for 18% -> 23% of each run, Pallas kernels for 0% -> 0%
where the time goes in v4:
time: 249 us; the launch traced here: 248 us
  waiting for transfers between devices  138 us (55%)
  local copies, waits for them, and re-layouts  26.9 us (11%)
  matrix products  26.7 us (11%)
  starting transfers between devices  24.9 us (10%)
  between operations  16.9 us (7%)
  other arithmetic  15 us (6%)
    reduce_scatter x1, waiting for transfers between devices, on_device(): lax.psum_scatter(partial_out.astype(jnp.bfloat16), 'head', scatter_dimens...  54.1 us
    all_gather x1, waiting for transfers between devices, on_device(): lax.all_gather(packed, CHIP_AXES, axis=1, tiled=True)  48.6 us
    ppermute x2, waiting for transfers between devices, shift_frames(): lax.ppermute(value, FRAME_AXES, [(source, source + steps) for source in r...  35.4 us
    ppermute x4, starting transfers between devices, swap_cores(): return lax.ppermute(value, 'c', [(0, 1), (1, 0)])  16.5 us
    dot_general x5, matrix products, on_device(): lax.dot_general(query_h, key_h, (((1,), (1,)), ((), ())), preferred_eleme...  12.7 us
    dot_general x5, matrix products, on_device(): jnp.dot(weights.astype(jnp.bfloat16), value_h, preferred_element_type=jnp...  9.23 us
    unnamed x23, local copies, waits for them, and re-layouts  8.98 us
    ppermute x2, starting transfers between devices, shift_frames(): lax.ppermute(value, FRAME_AXES, [(source, source + steps) for source in r...  8.35 us
  transfers between devices with their start and end apart: 8, of which 4 were waited for; matrix products, arithmetic and copies ran while one was open for 23% of the time, Pallas kernels for 0%

profile of v4, /device:TPU:1, one launch (start us, length us, event | category | flops | bytes accessed | tf_op | source)
XLA Modules:
  0.0 248.4 jit_solution(2321284656506221694)
XLA Ops:
  6.5 0.7 pad_maximum_fusion.2
  7.6 1.6 pad_maximum_fusion.1
  9.3 2.2 pad_maximum_fusion
  11.5 4.0 %collective-permute-start.1 = (bf16[2,384,640]{2,1,0:T(8,128)(2,1)}, bf16[2,384,640]{2,1,0:T(8,128)(2,1)S(1)}, u32[]{:S(2)}, u32[]{:S(2)}) collective-permute-start(bf16[2,384,640]{2,1,0:T(8,128)(2,1)} %pad_maximum_fusion), channel_id=1, source_target_pairs={{0,16},{8,24},{16,32},{24,40},{32,48},{40,56},{48,64},{56,72},{64,... | collective-permute-start | bytes 2949128 | tf_op jit(solution)/shard_map/ppermute | solution.py:16
  15.5 4.4 %collective-permute-start.3 = (bf16[2,384,640]{2,1,0:T(8,128)(2,1)}, bf16[2,384,640]{2,1,0:T(8,128)(2,1)S(1)}, u32[]{:S(2)}, u32[]{:S(2)}) collective-permute-start(bf16[2,384,640]{2,1,0:T(8,128)(2,1)} %pad_maximum_fusion), channel_id=1, source_target_pairs={{0,32},{8,40},{16,48},{24,56},{32,64},{40,72},{48,80},{56,88},{64,... | collective-permute-start | bytes 2949128 | tf_op jit(solution)/shard_map/ppermute | solution.py:16
  19.9 13.3 %collective-permute-done.1 = bf16[2,384,640]{2,1,0:T(8,128)(2,1)S(1)} collective-permute-done((bf16[2,384,640]{2,1,0:T(8,128)(2,1)}, bf16[2,384,640]{2,1,0:T(8,128)(2,1)S(1)}, u32[]{:S(2)}, u32[]{:S(2)}) %collective-permute-start.1) | collective-permute-done | bytes 983072 | tf_op jit(solution)/shard_map/ppermute | solution.py:16
  33.2 22.1 %collective-permute-done.3 = bf16[2,384,640]{2,1,0:T(8,128)(2,1)S(1)} collective-permute-done((bf16[2,384,640]{2,1,0:T(8,128)(2,1)}, bf16[2,384,640]{2,1,0:T(8,128)(2,1)S(1)}, u32[]{:S(2)}, u32[]{:S(2)}) %collective-permute-start.3) | collective-permute-done | bytes 983072 | tf_op jit(solution)/shard_map/ppermute | solution.py:16
  55.3 2.7 %broadcast_select_fusion = (bf16[2,384,640]{2,1,0:T(8,128)(2,1)}, bf16[2,384,640]{2,1,0:T(8,128)(2,1)}) fusion(bf16[2,384,640]{2,1,0:T(8,128)(2,1)S(1)} %collective-permute-done.1, bf16[2,384,640]{2,1,0:T(8,128)(2,1)S(1)} %collective-permute-done.3, pred[]{:T(512)S(6)} %eq.3, bf16[1,384,640]{2,1,0:T(8,128)(2,1)} %bitcast.70, bf16[1,384,640]{2,1,0:T(8,128)(2,1)} %bitcast.68), kind=kLoop, calls=%fused_computation.56 | loop fusion | flops 1474560 | bytes 4915201 | tf_op jit(solution)/shard_map/jit(_where)/select_n | solution.py:59
  58.0 6.8 %collective-permute-start.2 = (bf16[2,384,640]{2,1,0:T(8,128)(2,1)}, bf16[2,384,640]{2,1,0:T(8,128)(2,1)}, u32[]{:S(2)}, u32[]{:S(2)}) collective-permute-start(bf16[2,384,640]{2,1,0:T(8,128)(2,1)} %get-tuple-element.16), channel_id=1, source_target_pairs={{0,8},{8,0},{1,9},{9,1},{2,10},{10,2},{3,11},{11,3},{4,12},{12,4},... | collective-permute-start | bytes 2949128 | tf_op jit(solution)/shard_map/ppermute | solution.py:28
  68.6 0.7 fusion.112
  69.3 0.7 fusion.106
  70.2 0.6 fusion.107
  71.1 1.9 collective-permute-start.4
  73.0 0.6 fusion.108
  73.9 0.6 fusion.109
  74.8 0.6 fusion.110
  76.0 1.1 constant_dynamic-update-slice_fusion.2
  77.0 2.2 fusion.95
  79.3 1.0 fusion.94
  80.3 48.6 %all-gather.2.cloned.1.call-done = bf16[640,3072]{0,1:T(8,128)(2,1)} async-done(((bf16[640,96]{0,1:T(8,128)(2,1)}), bf16[640,3072]{0,1:T(8,128)(2,1)}) %all-gather.2.cloned.1.call-update) | async-done | bytes 3932176 | tf_op jit(solution)/shard_map/all_gather | solution.py:47
  128.9 1.1 slice.113
  130.1 3.5 %copy.10 = bf16[640,32,16]{2,0,1:T(8,128)(2,1)} copy(bf16[640,32,16]{0,2,1:T(8,128)(2,1)S(1)} %slice.113) | data formatting | bytes 1310720 | tf_op jit(solution)/shard_map/slice | solution.py:49
  133.5 6.5 %reshape.53 = bf16[256,1280]{1,0:T(8,128)(2,1)S(1)} reshape(bf16[32,8,80,16]{3,2,1,0:T(8,128)(2,1)} %bitcast.65) | data formatting | bytes 1310720 | tf_op jit(solution)/shard_map/reshape | solution.py:50
  140.1 5.6 %collective-permute-start.5 = (bf16[256,1280]{1,0:T(8,128)(2,1)S(1)}, bf16[256,1280]{1,0:T(8,128)(2,1)S(1)}, u32[]{:S(2)}, u32[]{:S(2)}) collective-permute-start(bf16[256,1280]{1,0:T(8,128)(2,1)S(1)} %reshape.53), channel_id=1, source_target_pairs={{0,8},{8,0},{1,9},{9,1},{2,10},{10,2},{3,11},{11,3},{4,12},{12,4},... | collective-permute-start | bytes 1966088 | tf_op jit(solution)/shard_map/ppermute | solution.py:28
  145.7 2.2 fusion.93
  147.9 1.1 fusion.92
  149.3 2.2 collective-permute-start
  151.6 1.2 slice_dynamic-update-slice_fusion
  152.9 2.5 %fusion.113 = (f32[384]{0:T(512)S(1)}, f32[2432,384]{1,0:T(8,128)S(1)}) fusion(bf16[384,640]{1,0:T(8,128)(2,1)S(1)} %copy-done.3, bf16[2432,640]{1,0:T(8,128)(2,1)} %get-tuple-element.6, pred[2432]{0:T(1024)(128)(4,1)S(1)} %dynamic-update-slice.24), kind=kOutput, calls=%fused_computation.112 | convolution fusion | flops 241876608 | bytes 4461056 | tf_op jit(solution)/shard_map/dot_general | solution.py:81
  155.4 2.5 %fusion.114 = (f32[384]{0:T(512)S(1)}, f32[2432,384]{1,0:T(8,128)S(1)}) fusion(bf16[384,640]{1,0:T(8,128)(2,1)S(1)} %copy-done.3, bf16[2432,640]{1,0:T(8,128)(2,1)} %get-tuple-element.6, pred[2432]{0:T(1024)(128)(4,1)S(1)} %dynamic-update-slice.24), kind=kOutput, calls=%fused_computation.113 | convolution fusion | flops 241876608 | bytes 4461056 | tf_op jit(solution)/shard_map/dot_general | solution.py:81
  158.0 2.5 %fusion.115 = (f32[384]{0:T(512)S(1)}, f32[2432,384]{1,0:T(8,128)S(1)}) fusion(bf16[384,640]{1,0:T(8,128)(2,1)S(1)} %copy-done.3, bf16[2432,640]{1,0:T(8,128)(2,1)} %get-tuple-element.6, pred[2432]{0:T(1024)(128)(4,1)S(1)} %dynamic-update-slice.24), kind=kOutput, calls=%fused_computation.114 | convolution fusion | flops 241876608 | bytes 4461056 | tf_op jit(solution)/shard_map/dot_general | solution.py:81
  160.5 0.6 fusion.9
  161.1 0.6 fusion.11
  161.8 0.6 fusion.13
  162.4 2.5 %fusion.116 = (f32[384]{0:T(512)S(1)}, f32[2432,384]{1,0:T(8,128)S(1)}) fusion(bf16[384,640]{1,0:T(8,128)(2,1)S(1)} %copy-done.3, bf16[2432,640]{1,0:T(8,128)(2,1)} %get-tuple-element.6, pred[2432]{0:T(1024)(128)(4,1)S(1)} %dynamic-update-slice.24), kind=kOutput, calls=%fused_computation.115 | convolution fusion | flops 241876608 | bytes 4461056 | tf_op jit(solution)/shard_map/dot_general | solution.py:81
  164.9 0.6 fusion.15
  165.6 2.5 %fusion.117 = (f32[384]{0:T(512)S(1)}, f32[2432,384]{1,0:T(8,128)S(1)}) fusion(bf16[384,640]{1,0:T(8,128)(2,1)S(1)} %copy-done.3, bf16[2432,640]{1,0:T(8,128)(2,1)} %get-tuple-element.6, pred[2432]{0:T(1024)(128)(4,1)S(1)} %dynamic-update-slice.24), kind=kOutput, calls=%fused_computation.116 | convolution fusion | flops 241876608 | bytes 4461056 | tf_op jit(solution)/shard_map/dot_general | solution.py:81
  168.1 0.6 fusion.17
  168.7 1.8 fusion.78
  170.6 1.9 fusion.72
  172.4 1.9 fusion.66
  174.3 1.8 fusion.60
  176.1 1.8 fusion.54
  178.0 4.8 %convert_bitcast_fusion = bf16[8,384,2,4,80]{1,4,3,0,2:T(8,128)(2,1)S(1)} fusion(bf16[1,640,8,4,80]{1,4,3,2,0:T(8,128)(2,1)S(1)} %bitcast.77, bf16[1,640,8,4,80]{1,4,3,2,0:T(8,128)(2,1)S(1)} %bitcast.74, bf16[384,640]{1,0:T(8,128)(2,1)S(1)} %fusion.54), kind=kOutput, calls=%fused_computation.14 | convolution fusion | flops 2521825280 | bytes 10977280 | tf_op jit(solution)/shard_map/rk,ckyxn->yrcxn/dot_general | solution.py:99
  182.8 2.3 copy.11
  185.1 54.1 %reduce-scatter.2.cloned.1.call-done = bf16[1,384,640]{1,2,0:T(8,128)(2,1)} async-done(((bf16[8,384,640]{1,2,0:T(8,128)(2,1)}), bf16[1,384,640]{1,2,0:T(8,128)(2,1)}) %reduce-scatter.2.cloned.1.call-update) | async-done | bytes 491536 | tf_op jit(solution)/shard_map/reduce_scatter | solution.py:101
  239.2 1.4 fusion.91
  240.6 1.0 copy.13
  (35 shorter events, 2.9 us)
Async XLA Ops:
  6.5 122.4 %all-gather.2.cloned.1.call-start = ((), (), s32[]{:S(2)}) async-start(), calls=%async_computation.1 | async-start | bytes 4055040 | tf_op jit(solution)/shard_map/all_gather | solution.py:47
  7.4 57.3 %copy-start.5 = (s32[64]{0:T(128)S(1)}, s32[64]{0:T(128)}, u32[]{:S(2)}) copy-start(s32[64]{0:T(128)} %param.14) | copy-start | bytes 772
  7.5 61.2 %copy-start.4 = (s32[64]{0:T(128)S(1)}, s32[64]{0:T(128)}, u32[]{:S(2)}) copy-start(s32[64]{0:T(128)} %param.15) | copy-start | bytes 772
  7.6 68.4 %copy-start = (bf16[384,640]{1,0:T(8,128)(2,1)S(1)}, bf16[384,640]{1,0:T(8,128)(2,1)}, u32[]{:S(2)}) copy-start(bf16[384,640]{1,0:T(8,128)(2,1)} %param.9) | copy-start | bytes 1474564
  7.6 68.4 %copy-start.1 = (bf16[384,640]{1,0:T(8,128)(2,1)S(1)}, bf16[384,640]{1,0:T(8,128)(2,1)}, u32[]{:S(2)}) copy-start(bf16[384,640]{1,0:T(8,128)(2,1)} %param.10) | copy-start | bytes 1474564
  9.3 229.9 %reduce-scatter.2.cloned.1.call-start = ((), (), s32[]{:S(2)}) async-start(), calls=%async_computation.2 | async-start | bytes 4423680 | tf_op jit(solution)/shard_map/reduce_scatter | solution.py:101
  11.5 21.7 %collective-permute-start.1 = (bf16[2,384,640]{2,1,0:T(8,128)(2,1)}, bf16[2,384,640]{2,1,0:T(8,128)(2,1)S(1)}, u32[]{:S(2)}, u32[]{:S(2)}) collective-permute-start(bf16[2,384,640]{2,1,0:T(8,128)(2,1)} %pad_maximum_fusion), channel_id=1, source_target_pairs={{0,16},{8,24},{16,32},{24,40},{32,48},{40,56},{48,64},{56,72},{64,... | collective-permute-start | bytes 2949128 | tf_op jit(solution)/shard_map/ppermute | solution.py:16
  15.5 39.8 %collective-permute-start.3 = (bf16[2,384,640]{2,1,0:T(8,128)(2,1)}, bf16[2,384,640]{2,1,0:T(8,128)(2,1)S(1)}, u32[]{:S(2)}, u32[]{:S(2)}) collective-permute-start(bf16[2,384,640]{2,1,0:T(8,128)(2,1)} %pad_maximum_fusion), channel_id=1, source_target_pairs={{0,32},{8,40},{16,48},{24,56},{32,64},{40,72},{48,80},{56,88},{64,... | collective-permute-start | bytes 2949128 | tf_op jit(solution)/shard_map/ppermute | solution.py:16
  58.0 19.1 %collective-permute-start.2 = (bf16[2,384,640]{2,1,0:T(8,128)(2,1)}, bf16[2,384,640]{2,1,0:T(8,128)(2,1)}, u32[]{:S(2)}, u32[]{:S(2)}) collective-permute-start(bf16[2,384,640]{2,1,0:T(8,128)(2,1)} %get-tuple-element.16), channel_id=1, source_target_pairs={{0,8},{8,0},{1,9},{9,1},{2,10},{10,2},{3,11},{11,3},{4,12},{12,4},... | collective-permute-start | bytes 2949128 | tf_op jit(solution)/shard_map/ppermute | solution.py:28
  71.1 74.6 %collective-permute-start.4 = (bf16[2,384,640]{2,1,0:T(8,128)(2,1)}, bf16[2,384,640]{2,1,0:T(8,128)(2,1)}, u32[]{:S(2)}, u32[]{:S(2)}) collective-permute-start(bf16[2,384,640]{2,1,0:T(8,128)(2,1)} %get-tuple-element.15), channel_id=1, source_target_pairs={{0,8},{8,0},{1,9},{9,1},{2,10},{10,2},{3,11},{11,3},{4,12},{12,4},... | collective-permute-start | bytes 2949128 | tf_op jit(solution)/shard_map/ppermute | solution.py:28
  140.1 8.9 %copy-start.2 = (bf16[640,3072]{0,1:T(8,128)(2,1)S(1)}, bf16[640,3072]{0,1:T(8,128)(2,1)}, u32[]{:S(2)}) copy-start(bf16[640,3072]{0,1:T(8,128)(2,1)} %all-gather.2.cloned.1.call-done) | copy-start | bytes 11796484
  140.1 11.5 %collective-permute-start.5 = (bf16[256,1280]{1,0:T(8,128)(2,1)S(1)}, bf16[256,1280]{1,0:T(8,128)(2,1)S(1)}, u32[]{:S(2)}, u32[]{:S(2)}) collective-permute-start(bf16[256,1280]{1,0:T(8,128)(2,1)S(1)} %reshape.53), channel_id=1, source_target_pairs={{0,8},{8,0},{1,9},{9,1},{2,10},{10,2},{3,11},{11,3},{4,12},{12,4},... | collective-permute-start | bytes 1966088 | tf_op jit(solution)/shard_map/ppermute | solution.py:28
  149.3 3.6 %copy-start.3 = (bf16[384,640]{1,0:T(8,128)(2,1)S(1)}, bf16[384,640]{1,0:T(8,128)(2,1)}, u32[]{:S(2)}) copy-start(bf16[384,640]{1,0:T(8,128)(2,1)} %param.8) | copy-start | bytes 1474564
  149.3 28.7 %collective-permute-start = (bf16[640,2560]{0,1:T(8,128)(2,1)S(1)}, bf16[640,2560]{0,1:T(8,128)(2,1)S(1)}, u32[]{:S(2)}, u32[]{:S(2)}) collective-permute-start(bf16[640,2560]{0,1:T(8,128)(2,1)S(1)} %bitcast.73), channel_id=1, source_target_pairs={{0,8},{8,0},{1,9},{9,1},{2,10},{10,2},{3,11},{11,3},{4,12},{12,4},... | collective-permute-start | bytes 9830408 | tf_op jit(solution)/shard_map/ppermute | solution.py:28
Sparse Core Ops, SparseCore 0:
  10.5 118.3 all-gather.1
  185.2 53.9 reduce-scatter.1

commit v5 on v3

--- a/solution.py
+++ b/solution.py
@@ -38,14 +38,6 @@
     core = lax.axis_index("c")
     first_core = core == 0
 
-    text_both = jnp.concatenate([text_keys, text_values], axis=1)
-    text_half = ring_gather(ring_gather(text_both, "x"), "y")
-    text_all = jnp.concatenate([text_half, swap_cores(text_half)], axis=0)
-    text_k, text_v = text_all[:, :width], text_all[:, width:]
-
-    weight_half = lax.all_gather(out_weight, CHIP_AXES, axis=1, tiled=True)
-    weight_pair = jnp.stack([weight_half, swap_cores(weight_half)])
-
     own = jnp.stack([keys, values])
     back2 = shift_frames(own, 2)
     back4 = shift_frames(own, 4)
@@ -61,35 +53,55 @@
         usable = (step <= own_window) & (source >= 0)
         source_len = lengths[jnp.maximum(source, 0)]
         mask_list.append(usable & (token_ids < source_len))
-    mask_list.append(jnp.ones((text_k.shape[0],), bool))
     key_mask = jnp.concatenate(mask_list)
-    all_keys = jnp.concatenate([p[0] for p in kv_list] + [text_k], axis=0)
-    all_values = jnp.concatenate([p[1] for p in kv_list] + [text_v], axis=0)
+    all_keys = jnp.concatenate([p[0] for p in kv_list], axis=0)
+    all_values = jnp.concatenate([p[1] for p in kv_list], axis=0)
+    frame_parts = []
+    for head_index in range(local_heads):
+        lower = head_index * HD
+        query_h = queries[:, lower : lower + HD]
+        scores = lax.dot_general(
+            query_h, all_keys[:, lower : lower + HD], (((1,), (1,)), ((), ())),
+            preferred_element_type=jnp.float32) * scale
+        scores = jnp.where(key_mask[None, :], scores, -jnp.inf)
+        top_f = jnp.max(scores, axis=-1, keepdims=True)
+        weights = jnp.exp(scores - top_f)
+        total_f = jnp.sum(weights, axis=-1, keepdims=True)
+        acc_f = jnp.dot(weights.astype(jnp.bfloat16), all_values[:, lower : lower + HD],
+                        preferred_element_type=jnp.float32)
+        frame_parts.append((top_f, total_f, acc_f))
+
+    chips = lax.axis_size(CHIP_AXES)
+    block = out_weight.shape[1]
+    tokens = text_keys.shape[0]
+    packed = jnp.concatenate([out_weight, text_keys.T, text_values.T], axis=1)
+    packed = lax.all_gather(packed, CHIP_AXES, axis=1, tiled=True)
+    packed, frame_parts = lax.optimization_barrier((packed, frame_parts))
+    pair = jnp.stack([packed, swap_cores(packed)]).reshape(2, width, chips, -1)
+    weight_pair = pair[:, :, :, :block]
+    text_kt = pair[:, :, :, block : block + tokens].transpose(1, 0, 2, 3).reshape(width, -1)
+    text_vt = pair[:, :, :, block + tokens :].transpose(1, 0, 2, 3).reshape(width, -1)
+
     head_outputs = []
     for head_index in range(local_heads):
         lower = head_index * HD
         query_h = queries[:, lower : lower + HD]
-        key_h = all_keys[:, lower : lower + HD]
-        value_h = all_values[:, lower : lower + HD]
-        scores = (
-            lax.dot_general(
-                query_h, key_h, (((1,), (1,)), ((), ())), preferred_element_type=jnp.float32
-            )
-            * scale
-        )
-        scores = jnp.where(key_mask[None, :], scores, -jnp.inf)
-        top = jnp.max(scores, axis=-1, keepdims=True)
-        weights = jnp.exp(scores - top)
-        total = jnp.sum(weights, axis=-1, keepdims=True)
-        attended = (
-            jnp.dot(weights.astype(jnp.bfloat16), value_h, preferred_element_type=jnp.float32)
-            / total
-        )
+        top_f, total_f, acc_f = frame_parts[head_index]
+        scores_t = jnp.dot(query_h, text_kt[lower : lower + HD], preferred_element_type=jnp.float32) * scale
+        top_t = jnp.max(scores_t, axis=-1, keepdims=True)
+        weights_t = jnp.exp(scores_t - top_t)
+        total_t = jnp.sum(weights_t, axis=-1, keepdims=True)
+        acc_t = lax.dot_general(
+            weights_t.astype(jnp.bfloat16), text_vt[lower : lower + HD], (((1,), (1,)), ((), ())),
+            preferred_element_type=jnp.float32)
+        top = jnp.maximum(top_f, top_t)
+        keep_f = jnp.exp(top_f - top)
+        keep_t = jnp.exp(top_t - top)
+        attended = (acc_f * keep_f + acc_t * keep_t) / (total_f * keep_f + total_t * keep_t)
         head_outputs.append(attended.astype(jnp.bfloat16))
     attended_all = jnp.concatenate(head_outputs, axis=1)
     ys = lax.axis_size("y")
     xs = lax.axis_size("x")
-    block = out_weight.shape[1]
     w5 = weight_pair.reshape(2, width, ys, xs, block)
     partial_out = jnp.einsum("rk,ckyxn->yrcxn", attended_all, w5, preferred_element_type=jnp.float32)
     partial_out = partial_out.reshape(groups, rows, -1)

time: 246 us -> 217 us (0.88)
  starting transfers between devices: 61 us -> 22.7 us
  waiting for transfers between devices: 106 us -> 136 us
  local copies, waits for them, and re-layouts: 27.7 us -> 10.2 us
  matrix products: 20 us -> 14.3 us
  other arithmetic: 13.3 us -> 16.6 us
    ppermute x10 -> x0, starting transfers between devices: 39.7 us -> none  [ring_gather(): lax.ppermute(value, axis, [(source, (source + step) % count) for source i...]
    ppermute x2, waiting for transfers between devices: 0.01 us -> 33.7 us  [shift_frames(): lax.ppermute(value, FRAME_AXES, [(source, source + steps) for source in r...]
    reduce_scatter x1, waiting for transfers between devices: 69.8 us -> 54 us  [on_device(): lax.psum_scatter(partial_out.astype(jnp.bfloat16), 'head', scatter_dimens...]
    unnamed x43 -> x20, local copies, waits for them, and re-layouts: 17.2 us -> 4.89 us
    ppermute x4 -> x3, waiting for transfers between devices: 0.01 us -> 6.6 us  [swap_cores(): return lax.ppermute(value, 'c', [(0, 1), (1, 0)])]
    dot_general x10 -> x20, matrix products: 15.4 us -> 9.99 us  [the longest x5 3.57 us: on_device(): lax.dot_general(query_h, all_keys[:, lower:lower + HD], (((1,), (1,)), ((...]
    all_gather x1, waiting for transfers between devices: 36.1 us -> 41.5 us  [on_device(): packed = lax.all_gather(packed, CHIP_AXES, axis=1, tiled=True)]
    concatenate x3 -> x1, local copies, waits for them, and re-layouts: 4.19 us -> 0.16 us  [on_device(): all_values = jnp.concatenate([p[1] for p in kv_list], axis=0)]
  transfers between devices with their start and end apart: 18 -> 7, of which waited for: 2 -> 5; matrix products, arithmetic and copies ran while one was open for 18% -> 10% of each run, Pallas kernels for 0% -> 0%
where the time goes in v5:
time: 217 us; the launch traced here: 216 us
  waiting for transfers between devices  136 us (63%)
  starting transfers between devices  22.7 us (10%)
  other arithmetic  16.6 us (8%)
  between operations  16.5 us (8%)
  matrix products  14.3 us (7%)
  local copies, waits for them, and re-layouts  10.2 us (5%)
    reduce_scatter x1, waiting for transfers between devices, on_device(): lax.psum_scatter(partial_out.astype(jnp.bfloat16), 'head', scatter_dimens...  54 us
    all_gather x1, waiting for transfers between devices, on_device(): packed = lax.all_gather(packed, CHIP_AXES, axis=1, tiled=True)  41.5 us
    ppermute x2, waiting for transfers between devices, shift_frames(): lax.ppermute(value, FRAME_AXES, [(source, source + steps) for source in r...  33.7 us
    ppermute x3, starting transfers between devices, swap_cores(): return lax.ppermute(value, 'c', [(0, 1), (1, 0)])  14.1 us
    ppermute x2, starting transfers between devices, shift_frames(): lax.ppermute(value, FRAME_AXES, [(source, source + steps) for source in r...  8.5 us
    ppermute x3, waiting for transfers between devices, swap_cores(): return lax.ppermute(value, 'c', [(0, 1), (1, 0)])  6.6 us
    unnamed x20, local copies, waits for them, and re-layouts  4.89 us
  transfers between devices with their start and end apart: 7, of which 5 were waited for; matrix products, arithmetic and copies ran while one was open for 10% of the time, Pallas kernels for 0%

profile of v5, /device:TPU:1, one launch (start us, length us, event | category | flops | bytes accessed | tf_op | source)
XLA Modules:
  0.0 216.2 jit_solution(3334961082568300724)
XLA Ops:
  6.5 2.2 %pad_maximum_fusion = bf16[2,384,640]{2,1,0:T(8,128)(2,1)} fusion(bf16[1,384,640]{2,1,0:T(8,128)(2,1)} %bitcast.94, bf16[1,384,640]{2,1,0:T(8,128)(2,1)} %bitcast.92), kind=kLoop, calls=%fused_computation.71 | loop fusion | flops 491520 | bytes 1966080 | tf_op jit(solution)/shard_map/stack | solution.py:41
  8.8 4.1 %collective-permute-start = (bf16[2,384,640]{2,1,0:T(8,128)(2,1)}, bf16[2,384,640]{2,1,0:T(8,128)(2,1)S(1)}, u32[]{:S(2)}, u32[]{:S(2)}) collective-permute-start(bf16[2,384,640]{2,1,0:T(8,128)(2,1)} %pad_maximum_fusion), channel_id=1, source_target_pairs={{0,16},{8,24},{16,32},{24,40},{32,48},{40,56},{48,64},{56,72},{64,... | collective-permute-start | bytes 2949128 | tf_op jit(solution)/shard_map/ppermute | solution.py:16
  12.9 4.4 %collective-permute-start.2 = (bf16[2,384,640]{2,1,0:T(8,128)(2,1)}, bf16[2,384,640]{2,1,0:T(8,128)(2,1)S(1)}, u32[]{:S(2)}, u32[]{:S(2)}) collective-permute-start(bf16[2,384,640]{2,1,0:T(8,128)(2,1)} %pad_maximum_fusion), channel_id=1, source_target_pairs={{0,32},{8,40},{16,48},{24,56},{32,64},{40,72},{48,80},{56,88},{64,... | collective-permute-start | bytes 2949128 | tf_op jit(solution)/shard_map/ppermute | solution.py:16
  17.3 1.6 pad_maximum_fusion.2
  19.0 11.3 %collective-permute-done = bf16[2,384,640]{2,1,0:T(8,128)(2,1)S(1)} collective-permute-done((bf16[2,384,640]{2,1,0:T(8,128)(2,1)}, bf16[2,384,640]{2,1,0:T(8,128)(2,1)S(1)}, u32[]{:S(2)}, u32[]{:S(2)}) %collective-permute-start) | collective-permute-done | bytes 983072 | tf_op jit(solution)/shard_map/ppermute | solution.py:16
  30.3 22.4 %collective-permute-done.2 = bf16[2,384,640]{2,1,0:T(8,128)(2,1)S(1)} collective-permute-done((bf16[2,384,640]{2,1,0:T(8,128)(2,1)}, bf16[2,384,640]{2,1,0:T(8,128)(2,1)S(1)}, u32[]{:S(2)}, u32[]{:S(2)}) %collective-permute-start.2) | collective-permute-done | bytes 983072 | tf_op jit(solution)/shard_map/ppermute | solution.py:16
  52.7 2.7 %broadcast_select_fusion = (bf16[2,384,640]{2,1,0:T(8,128)(2,1)}, bf16[2,384,640]{2,1,0:T(8,128)(2,1)}) fusion(bf16[2,384,640]{2,1,0:T(8,128)(2,1)S(1)} %collective-permute-done, bf16[2,384,640]{2,1,0:T(8,128)(2,1)S(1)} %collective-permute-done.2, pred[]{:T(512)S(6)} %eq.3, bf16[1,384,640]{2,1,0:T(8,128)(2,1)} %bitcast.95, bf16[1,384,640]{2,1,0:T(8,128)(2,1)} %bitcast.93), kind=kLoop, calls=%fused_computation.72 | loop fusion | flops 1474560 | bytes 4915201 | tf_op jit(solution)/shard_map/jit(_where)/select_n | solution.py:45
  55.3 6.8 %collective-permute-start.1 = (bf16[2,384,640]{2,1,0:T(8,128)(2,1)}, bf16[2,384,640]{2,1,0:T(8,128)(2,1)}, u32[]{:S(2)}, u32[]{:S(2)}) collective-permute-start(bf16[2,384,640]{2,1,0:T(8,128)(2,1)} %get-tuple-element.63), channel_id=1, source_target_pairs={{0,8},{8,0},{1,9},{9,1},{2,10},{10,2},{3,11},{11,3},{4,12},{12,4},... | collective-permute-start | bytes 2949128 | tf_op jit(solution)/shard_map/ppermute | solution.py:28
  62.2 0.6 dynamic_slice.18
  65.6 0.7 fusion.131
  66.2 0.6 fusion.104
  67.1 0.6 fusion.105
  67.9 1.9 collective-permute-start.3
  69.8 0.6 fusion.106
  70.7 0.6 fusion.107
  71.5 0.6 fusion.108
  72.5 1.3 fusion.77
  74.0 1.3 fusion.75
  75.6 0.7 fusion.136
  76.3 0.5 fusion.15
  76.8 0.7 fusion.135
  77.5 0.5 fusion.13
  78.1 0.7 fusion.134
  78.8 0.5 fusion.11
  79.3 0.7 fusion.133
  80.0 0.5 fusion.9
  80.5 0.7 fusion.132
  81.3 0.5 fusion.7
  81.8 0.6 fusion.16
  82.4 0.6 fusion.18
  83.0 0.6 fusion.20
  83.6 0.6 fusion.22
  84.2 0.6 fusion.24
  84.8 41.5 %all-gather.2.cloned.1.call-done = bf16[640,3072]{0,1:T(8,128)(2,1)} async-done(((bf16[640,96]{0,1:T(8,128)(2,1)}), bf16[640,3072]{0,1:T(8,128)(2,1)}) %all-gather.2.cloned.1.call-update) | async-done | bytes 3932176 | tf_op jit(solution)/shard_map/all_gather | solution.py:78
  126.3 5.5 %collective-permute-start.4 = (bf16[640,3072]{0,1:T(8,128)(2,1)}, bf16[640,3072]{0,1:T(8,128)(2,1)S(1)}, u32[]{:S(2)}, u32[]{:S(2)}) collective-permute-start(bf16[640,3072]{0,1:T(8,128)(2,1)} %all-gather.2.cloned.1.call-done), channel_id=1, source_target_pairs={{0,8},{8,0},{1,9},{9,1},{2,10},{10,2},{3,11},{11,3},{4,12},{12,4},... | collective-permute-start | bytes 11796488 | tf_op jit(solution)/shard_map/ppermute | solution.py:28
  131.8 6.6 %collective-permute-done.4 = bf16[640,3072]{0,1:T(8,128)(2,1)S(1)} collective-permute-done((bf16[640,3072]{0,1:T(8,128)(2,1)}, bf16[640,3072]{0,1:T(8,128)(2,1)S(1)}, u32[]{:S(2)}, u32[]{:S(2)}) %collective-permute-start.4) | collective-permute-done | bytes 3932192 | tf_op jit(solution)/shard_map/ppermute | solution.py:28
  138.4 1.4 fusion.63
  139.8 0.9 copy-done
  140.7 0.8 fusion
  144.6 0.4 fusion.44
  145.0 0.4 fusion.46
  145.4 0.4 fusion.48
  145.8 0.4 fusion.50
  146.2 4.3 %convert_bitcast_fusion = bf16[8,384,2,4,80]{1,4,3,0,2:T(8,128)(2,1)S(1)} fusion(bf16[2,640,8,4,80]{1,4,3,2,0:T(8,128)(2,1)S(1)} %bitcast.91, bf16[384,640]{1,0:T(8,128)(2,1)S(1)} %fusion.50), kind=kOutput, calls=%fused_computation.5 | convolution fusion | flops 2518548480 | bytes 10977280 | tf_op jit(solution)/shard_map/rk,ckyxn->yrcxn/dot_general | solution.py:106
  150.5 2.3 %copy.9 = bf16[8,384,2,4,80]{1,4,3,2,0:T(8,128)(2,1)} copy(bf16[8,384,2,4,80]{1,4,3,0,2:T(8,128)(2,1)S(1)} %convert_bitcast_fusion) | data formatting | bytes 7864320 | tf_op jit(solution)/shard_map/convert_element_type | solution.py:108
  152.9 54.0 %reduce-scatter.2.cloned.1.call-done = bf16[1,384,640]{1,2,0:T(8,128)(2,1)} async-done(((bf16[8,384,640]{1,2,0:T(8,128)(2,1)}), bf16[1,384,640]{1,2,0:T(8,128)(2,1)}) %reduce-scatter.2.cloned.1.call-update) | async-done | bytes 491536 | tf_op jit(solution)/shard_map/reduce_scatter | solution.py:108
  206.9 1.4 fusion.64
  208.3 1.0 copy.11
  (55 shorter events, 4.9 us)
Async XLA Ops:
  6.5 119.8 %all-gather.2.cloned.1.call-start = ((), (), s32[]{:S(2)}) async-start(), calls=%async_computation.1 | async-start | bytes 4055040 | tf_op jit(solution)/shard_map/all_gather | solution.py:78
  8.8 53.4 %copy-start.5 = (s32[64]{0:T(128)S(1)}, s32[64]{0:T(128)}, u32[]{:S(2)}) copy-start(s32[64]{0:T(128)} %param.14) | copy-start | bytes 772
  8.8 56.8 %copy-start.4 = (s32[64]{0:T(128)S(1)}, s32[64]{0:T(128)}, u32[]{:S(2)}) copy-start(s32[64]{0:T(128)} %param.15) | copy-start | bytes 772
  8.8 63.6 %copy-start.1 = (bf16[384,640]{1,0:T(8,128)(2,1)S(1)}, bf16[384,640]{1,0:T(8,128)(2,1)}, u32[]{:S(2)}) copy-start(bf16[384,640]{1,0:T(8,128)(2,1)} %param.9) | copy-start | bytes 1474564
  8.8 63.6 %copy-start.2 = (bf16[384,640]{1,0:T(8,128)(2,1)S(1)}, bf16[384,640]{1,0:T(8,128)(2,1)}, u32[]{:S(2)}) copy-start(bf16[384,640]{1,0:T(8,128)(2,1)} %param.10) | copy-start | bytes 1474564
  8.8 21.5 %collective-permute-start = (bf16[2,384,640]{2,1,0:T(8,128)(2,1)}, bf16[2,384,640]{2,1,0:T(8,128)(2,1)S(1)}, u32[]{:S(2)}, u32[]{:S(2)}) collective-permute-start(bf16[2,384,640]{2,1,0:T(8,128)(2,1)} %pad_maximum_fusion), channel_id=1, source_target_pairs={{0,16},{8,24},{16,32},{24,40},{32,48},{40,56},{48,64},{56,72},{64,... | collective-permute-start | bytes 2949128 | tf_op jit(solution)/shard_map/ppermute | solution.py:16
  12.9 39.7 %collective-permute-start.2 = (bf16[2,384,640]{2,1,0:T(8,128)(2,1)}, bf16[2,384,640]{2,1,0:T(8,128)(2,1)S(1)}, u32[]{:S(2)}, u32[]{:S(2)}) collective-permute-start(bf16[2,384,640]{2,1,0:T(8,128)(2,1)} %pad_maximum_fusion), channel_id=1, source_target_pairs={{0,32},{8,40},{16,48},{24,56},{32,64},{40,72},{48,80},{56,88},{64,... | collective-permute-start | bytes 2949128 | tf_op jit(solution)/shard_map/ppermute | solution.py:16
  18.9 188.0 %reduce-scatter.2.cloned.1.call-start = ((), (), s32[]{:S(2)}) async-start(), calls=%async_computation.2 | async-start | bytes 4423680 | tf_op jit(solution)/shard_map/reduce_scatter | solution.py:108
  55.3 17.2 %collective-permute-start.1 = (bf16[2,384,640]{2,1,0:T(8,128)(2,1)}, bf16[2,384,640]{2,1,0:T(8,128)(2,1)}, u32[]{:S(2)}, u32[]{:S(2)}) collective-permute-start(bf16[2,384,640]{2,1,0:T(8,128)(2,1)} %get-tuple-element.63), channel_id=1, source_target_pairs={{0,8},{8,0},{1,9},{9,1},{2,10},{10,2},{3,11},{11,3},{4,12},{12,4},... | collective-permute-start | bytes 2949128 | tf_op jit(solution)/shard_map/ppermute | solution.py:28
  67.9 6.1 %collective-permute-start.3 = (bf16[2,384,640]{2,1,0:T(8,128)(2,1)}, bf16[2,384,640]{2,1,0:T(8,128)(2,1)}, u32[]{:S(2)}, u32[]{:S(2)}) collective-permute-start(bf16[2,384,640]{2,1,0:T(8,128)(2,1)} %get-tuple-element.62), channel_id=1, source_target_pairs={{0,8},{8,0},{1,9},{9,1},{2,10},{10,2},{3,11},{11,3},{4,12},{12,4},... | collective-permute-start | bytes 2949128 | tf_op jit(solution)/shard_map/ppermute | solution.py:28
  73.9 1.7 copy-start.3
  126.3 12.1 %collective-permute-start.4 = (bf16[640,3072]{0,1:T(8,128)(2,1)}, bf16[640,3072]{0,1:T(8,128)(2,1)S(1)}, u32[]{:S(2)}, u32[]{:S(2)}) collective-permute-start(bf16[640,3072]{0,1:T(8,128)(2,1)} %all-gather.2.cloned.1.call-done), channel_id=1, source_target_pairs={{0,8},{8,0},{1,9},{9,1},{2,10},{10,2},{3,11},{11,3},{4,12},{12,4},... | collective-permute-start | bytes 11796488 | tf_op jit(solution)/shard_map/ppermute | solution.py:28
  138.4 2.3 %copy-start = (bf16[640,3072]{0,1:T(8,128)(2,1)S(1)}, bf16[640,3072]{0,1:T(8,128)(2,1)}, u32[]{:S(2)}) copy-start(bf16[640,3072]{0,1:T(8,128)(2,1)} %all-gather.2.cloned.1.call-done) | copy-start | bytes 11796484
Sparse Core Ops, SparseCore 0:
  19.0 107.2 all-gather.1
  153.0 53.8 reduce-scatter.1

commit v6 on v5

--- a/solution.py
+++ b/solution.py
@@ -16,12 +16,21 @@
     return lax.ppermute(value, FRAME_AXES, [(source, source + steps) for source in range(count - steps)])
 
 
-def ring_gather(value, axis):
-    count = lax.axis_size(axis)
-    pieces = [value]
-    for step in range(1, count):
-        pieces.append(lax.ppermute(value, axis, [(source, (source + step) % count) for source in range(count)]))
-    return jnp.concatenate(pieces, axis=0)
+def relay_back(value, chips_back):
+    ys, xs, cs = (lax.axis_size(name) for name in FRAME_AXES)
+    count = ys * xs * cs
+    first, second = [], []
+    for y in range(ys):
+        for x in range(xs):
+            for c in range(cs):
+                source = (y * xs + x) * cs + c
+                middle = (y * xs + (x - 1) % xs) * cs + c
+                first.append((source, middle))
+                target = source + chips_back * cs
+                if target < count:
+                    second.append((middle, target))
+    hop = lax.ppermute(value, FRAME_AXES, first)
+    return lax.ppermute(hop, FRAME_AXES, second)
 
 
 def swap_cores(value):
@@ -40,7 +49,7 @@
 
     own = jnp.stack([keys, values])
     back2 = shift_frames(own, 2)
-    back4 = shift_frames(own, 4)
+    back4 = relay_back(own, 2)
     back1 = swap_cores(jnp.where(first_core, own, back2))
     back3 = swap_cores(jnp.where(first_core, back2, back4))
     kv_list = [own, back1, back2, back3, back4]

time: 217 us -> 219 us (level)
  starting transfers between devices: 22.7 us -> 26.5 us
    ppermute x2 -> x1, waiting for transfers between devices: 33.7 us -> 0.01 us  [shift_frames(): lax.ppermute(value, FRAME_AXES, [(source, source + steps) for source in r...]
    ppermute x0 -> x2, waiting for transfers between devices: none -> 32.1 us  [the longest x1 16.7 us: relay_back(): hop = lax.ppermute(value, FRAME_AXES, first)]
    ppermute x0 -> x2, starting transfers between devices: none -> 10.7 us  [the longest x1 5.36 us: relay_back(): return lax.ppermute(hop, FRAME_AXES, second)]
    ppermute x2 -> x1, starting transfers between devices: 8.5 us -> 1.35 us  [shift_frames(): lax.ppermute(value, FRAME_AXES, [(source, source + steps) for source in r...]
  transfers between devices with their start and end apart: 7 -> 8, of which waited for: 5 -> 5; matrix products, arithmetic and copies ran while one was open for 10% -> 10% of each run, Pallas kernels for 0% -> 0%
where the time goes in v6:
time: 219 us
  waiting for transfers between devices  134 us (61%)
  starting transfers between devices  26.5 us (12%)
  other arithmetic  16.6 us (8%)
  between operations  16.6 us (8%)
  matrix products  14.3 us (7%)
  local copies, waits for them, and re-layouts  10.2 us (5%)
    reduce_scatter x1, waiting for transfers between devices, on_device(): lax.psum_scatter(partial_out.astype(jnp.bfloat16), 'head', scatter_dimens...  54 us
    all_gather x1, waiting for transfers between devices, on_device(): packed = lax.all_gather(packed, CHIP_AXES, axis=1, tiled=True)  41.8 us
    ppermute x1, waiting for transfers between devices, relay_back(): hop = lax.ppermute(value, FRAME_AXES, first)  16.7 us
    ppermute x1, waiting for transfers between devices, relay_back(): return lax.ppermute(hop, FRAME_AXES, second)  15.4 us
    ppermute x3, starting transfers between devices, swap_cores(): return lax.ppermute(value, 'c', [(0, 1), (1, 0)])  14.4 us
    ppermute x3, waiting for transfers between devices, swap_cores(): return lax.ppermute(value, 'c', [(0, 1), (1, 0)])  6.42 us
    ppermute x1, starting transfers between devices, relay_back(): return lax.ppermute(hop, FRAME_AXES, second)  5.36 us
    ppermute x1, starting transfers between devices, relay_back(): hop = lax.ppermute(value, FRAME_AXES, first)  5.35 us
  transfers between devices with their start and end apart: 8, of which 5 were waited for; matrix products, arithmetic and copies ran while one was open for 10% of the time, Pallas kernels for 0%

profile of v6, /device:TPU:1, one launch (start us, length us, event | category | flops | bytes accessed | tf_op | source)
XLA Modules:
  0.0 218.5 jit_solution(1085650684667911366)
XLA Ops:
  6.5 2.2 %pad_maximum_fusion = bf16[2,384,640]{2,1,0:T(8,128)(2,1)} fusion(bf16[1,384,640]{2,1,0:T(8,128)(2,1)} %bitcast.94, bf16[1,384,640]{2,1,0:T(8,128)(2,1)} %bitcast.92), kind=kLoop, calls=%fused_computation.71 | loop fusion | flops 491520 | bytes 1966080 | tf_op jit(solution)/shard_map/stack | solution.py:50
  8.8 5.3 %collective-permute-start.2 = (bf16[2,384,640]{2,1,0:T(8,128)(2,1)}, bf16[2,384,640]{2,1,0:T(8,128)(2,1)}, u32[]{:S(2)}, u32[]{:S(2)}) collective-permute-start(bf16[2,384,640]{2,1,0:T(8,128)(2,1)} %pad_maximum_fusion), channel_id=1, source_target_pairs={{0,48},{8,56},{16,0},{24,8},{32,16},{40,24},{48,32},{56,40},{64,11... | collective-permute-start | bytes 2949128 | tf_op jit(solution)/shard_map/ppermute | solution.py:32
  14.2 1.4 collective-permute-start
  15.5 16.7 %collective-permute-done.2 = bf16[2,384,640]{2,1,0:T(8,128)(2,1)} collective-permute-done((bf16[2,384,640]{2,1,0:T(8,128)(2,1)}, bf16[2,384,640]{2,1,0:T(8,128)(2,1)}, u32[]{:S(2)}, u32[]{:S(2)}) %collective-permute-start.2) | collective-permute-done | bytes 983072 | tf_op jit(solution)/shard_map/ppermute | solution.py:32
  32.2 5.4 %collective-permute-start.3 = (bf16[2,384,640]{2,1,0:T(8,128)(2,1)}, bf16[2,384,640]{2,1,0:T(8,128)(2,1)S(1)}, u32[]{:S(2)}, u32[]{:S(2)}) collective-permute-start(bf16[2,384,640]{2,1,0:T(8,128)(2,1)} %collective-permute-done.2), channel_id=1, source_target_pairs={{48,32},{56,40},{0,48},{8,56},{16,64},{24,72},{32,80},{40,88},{112... | collective-permute-start | bytes 2949128 | tf_op jit(solution)/shard_map/ppermute | solution.py:33
  37.6 1.6 pad_maximum_fusion.2
  39.2 15.4 %collective-permute-done.3 = bf16[2,384,640]{2,1,0:T(8,128)(2,1)S(1)} collective-permute-done((bf16[2,384,640]{2,1,0:T(8,128)(2,1)}, bf16[2,384,640]{2,1,0:T(8,128)(2,1)S(1)}, u32[]{:S(2)}, u32[]{:S(2)}) %collective-permute-start.3) | collective-permute-done | bytes 983072 | tf_op jit(solution)/shard_map/ppermute | solution.py:33
  54.6 2.7 %broadcast_select_fusion = (bf16[2,384,640]{2,1,0:T(8,128)(2,1)}, bf16[2,384,640]{2,1,0:T(8,128)(2,1)}) fusion(bf16[2,384,640]{2,1,0:T(8,128)(2,1)S(1)} %collective-permute-done, bf16[2,384,640]{2,1,0:T(8,128)(2,1)S(1)} %collective-permute-done.3, pred[]{:T(512)S(6)} %eq.3, bf16[1,384,640]{2,1,0:T(8,128)(2,1)} %bitcast.95, bf16[1,384,640]{2,1,0:T(8,128)(2,1)} %bitcast.93), kind=kLoop, calls=%fused_computation.72 | loop fusion | flops 1474560 | bytes 4915201 | tf_op jit(solution)/shard_map/jit(_where)/select_n | solution.py:54
  57.3 7.1 %collective-permute-start.1 = (bf16[2,384,640]{2,1,0:T(8,128)(2,1)}, bf16[2,384,640]{2,1,0:T(8,128)(2,1)}, u32[]{:S(2)}, u32[]{:S(2)}) collective-permute-start(bf16[2,384,640]{2,1,0:T(8,128)(2,1)} %get-tuple-element.63), channel_id=1, source_target_pairs={{0,8},{8,0},{1,9},{9,1},{2,10},{10,2},{3,11},{11,3},{4,12},{12,4},... | collective-permute-start | bytes 2949128 | tf_op jit(solution)/shard_map/ppermute | solution.py:37
  64.4 0.6 dynamic_slice.18
  67.8 0.7 fusion.131
  68.5 0.6 fusion.104
  69.4 0.6 fusion.105
  70.2 1.9 collective-permute-start.4
  72.1 0.6 fusion.106
  73.0 0.6 fusion.107
  73.8 0.6 fusion.108
  74.8 1.3 fusion.77
  76.3 1.3 fusion.75
  77.8 0.7 fusion.136
  78.5 0.5 fusion.15
  79.1 0.7 fusion.135
  79.8 0.5 fusion.13
  80.3 0.7 fusion.134
  81.0 0.5 fusion.11
  81.5 0.7 fusion.133
  82.3 0.5 fusion.9
  82.8 0.7 fusion.132
  83.5 0.5 fusion.7
  84.0 0.6 fusion.16
  84.6 0.6 fusion.18
  85.2 0.6 fusion.20
  85.9 0.6 fusion.22
  86.5 0.6 fusion.24
  87.1 41.8 %all-gather.2.cloned.1.call-done = bf16[640,3072]{0,1:T(8,128)(2,1)} async-done(((bf16[640,96]{0,1:T(8,128)(2,1)}), bf16[640,3072]{0,1:T(8,128)(2,1)}) %all-gather.2.cloned.1.call-update) | async-done | bytes 3932176 | tf_op jit(solution)/shard_map/all_gather | solution.py:87
  128.9 5.5 %collective-permute-start.5 = (bf16[640,3072]{0,1:T(8,128)(2,1)}, bf16[640,3072]{0,1:T(8,128)(2,1)S(1)}, u32[]{:S(2)}, u32[]{:S(2)}) collective-permute-start(bf16[640,3072]{0,1:T(8,128)(2,1)} %all-gather.2.cloned.1.call-done), channel_id=1, source_target_pairs={{0,8},{8,0},{1,9},{9,1},{2,10},{10,2},{3,11},{11,3},{4,12},{12,4},... | collective-permute-start | bytes 11796488 | tf_op jit(solution)/shard_map/ppermute | solution.py:37
  134.3 6.4 %collective-permute-done.5 = bf16[640,3072]{0,1:T(8,128)(2,1)S(1)} collective-permute-done((bf16[640,3072]{0,1:T(8,128)(2,1)}, bf16[640,3072]{0,1:T(8,128)(2,1)S(1)}, u32[]{:S(2)}, u32[]{:S(2)}) %collective-permute-start.5) | collective-permute-done | bytes 3932192 | tf_op jit(solution)/shard_map/ppermute | solution.py:37
  140.8 1.4 fusion.63
  142.1 0.9 copy-done
  143.1 0.8 fusion
  147.4 0.4 fusion.46
  147.8 0.4 fusion.48
  148.2 0.4 fusion.50
  148.6 4.3 %convert_bitcast_fusion = bf16[8,384,2,4,80]{1,4,3,0,2:T(8,128)(2,1)S(1)} fusion(bf16[2,640,8,4,80]{1,4,3,2,0:T(8,128)(2,1)S(1)} %bitcast.91, bf16[384,640]{1,0:T(8,128)(2,1)S(1)} %fusion.50), kind=kOutput, calls=%fused_computation.5 | convolution fusion | flops 2518548480 | bytes 10977280 | tf_op jit(solution)/shard_map/rk,ckyxn->yrcxn/dot_general | solution.py:115
  152.9 2.3 %copy.9 = bf16[8,384,2,4,80]{1,4,3,2,0:T(8,128)(2,1)} copy(bf16[8,384,2,4,80]{1,4,3,0,2:T(8,128)(2,1)S(1)} %convert_bitcast_fusion) | data formatting | bytes 7864320 | tf_op jit(solution)/shard_map/convert_element_type | solution.py:117
  155.2 54.0 %reduce-scatter.2.cloned.1.call-done = bf16[1,384,640]{1,2,0:T(8,128)(2,1)} async-done(((bf16[8,384,640]{1,2,0:T(8,128)(2,1)}), bf16[1,384,640]{1,2,0:T(8,128)(2,1)}) %reduce-scatter.2.cloned.1.call-update) | async-done | bytes 491536 | tf_op jit(solution)/shard_map/reduce_scatter | solution.py:117
  209.3 1.4 fusion.64
  210.7 1.0 copy.11
  (57 shorter events, 5.3 us)
Async XLA Ops:
  6.5 122.3 %all-gather.2.cloned.1.call-start = ((), (), s32[]{:S(2)}) async-start(), calls=%async_computation.1 | async-start | bytes 4055040 | tf_op jit(solution)/shard_map/all_gather | solution.py:87
  8.8 55.6 %copy-start.5 = (s32[64]{0:T(128)S(1)}, s32[64]{0:T(128)}, u32[]{:S(2)}) copy-start(s32[64]{0:T(128)} %param.14) | copy-start | bytes 772
  8.8 59.0 %copy-start.4 = (s32[64]{0:T(128)S(1)}, s32[64]{0:T(128)}, u32[]{:S(2)}) copy-start(s32[64]{0:T(128)} %param.15) | copy-start | bytes 772
  8.8 65.9 %copy-start.1 = (bf16[384,640]{1,0:T(8,128)(2,1)S(1)}, bf16[384,640]{1,0:T(8,128)(2,1)}, u32[]{:S(2)}) copy-start(bf16[384,640]{1,0:T(8,128)(2,1)} %param.9) | copy-start | bytes 1474564
  8.8 65.9 %copy-start.2 = (bf16[384,640]{1,0:T(8,128)(2,1)S(1)}, bf16[384,640]{1,0:T(8,128)(2,1)}, u32[]{:S(2)}) copy-start(bf16[384,640]{1,0:T(8,128)(2,1)} %param.10) | copy-start | bytes 1474564
  8.8 23.4 %collective-permute-start.2 = (bf16[2,384,640]{2,1,0:T(8,128)(2,1)}, bf16[2,384,640]{2,1,0:T(8,128)(2,1)}, u32[]{:S(2)}, u32[]{:S(2)}) collective-permute-start(bf16[2,384,640]{2,1,0:T(8,128)(2,1)} %pad_maximum_fusion), channel_id=1, source_target_pairs={{0,48},{8,56},{16,0},{24,8},{32,16},{40,24},{48,32},{56,40},{64,11... | collective-permute-start | bytes 2949128 | tf_op jit(solution)/shard_map/ppermute | solution.py:32
  14.2 25.1 %collective-permute-start = (bf16[2,384,640]{2,1,0:T(8,128)(2,1)}, bf16[2,384,640]{2,1,0:T(8,128)(2,1)S(1)}, u32[]{:S(2)}, u32[]{:S(2)}) collective-permute-start(bf16[2,384,640]{2,1,0:T(8,128)(2,1)} %pad_maximum_fusion), channel_id=1, source_target_pairs={{0,16},{8,24},{16,32},{24,40},{32,48},{40,56},{48,64},{56,72},{64,... | collective-permute-start | bytes 2949128 | tf_op jit(solution)/shard_map/ppermute | solution.py:16
  32.2 22.4 %collective-permute-start.3 = (bf16[2,384,640]{2,1,0:T(8,128)(2,1)}, bf16[2,384,640]{2,1,0:T(8,128)(2,1)S(1)}, u32[]{:S(2)}, u32[]{:S(2)}) collective-permute-start(bf16[2,384,640]{2,1,0:T(8,128)(2,1)} %collective-permute-done.2), channel_id=1, source_target_pairs={{48,32},{56,40},{0,48},{8,56},{16,64},{24,72},{32,80},{40,88},{112... | collective-permute-start | bytes 2949128 | tf_op jit(solution)/shard_map/ppermute | solution.py:33
  39.2 170.1 %reduce-scatter.2.cloned.1.call-start = ((), (), s32[]{:S(2)}) async-start(), calls=%async_computation.2 | async-start | bytes 4423680 | tf_op jit(solution)/shard_map/reduce_scatter | solution.py:117
  57.3 17.5 %collective-permute-start.1 = (bf16[2,384,640]{2,1,0:T(8,128)(2,1)}, bf16[2,384,640]{2,1,0:T(8,128)(2,1)}, u32[]{:S(2)}, u32[]{:S(2)}) collective-permute-start(bf16[2,384,640]{2,1,0:T(8,128)(2,1)} %get-tuple-element.63), channel_id=1, source_target_pairs={{0,8},{8,0},{1,9},{9,1},{2,10},{10,2},{3,11},{11,3},{4,12},{12,4},... | collective-permute-start | bytes 2949128 | tf_op jit(solution)/shard_map/ppermute | solution.py:37
  70.2 6.1 %collective-permute-start.4 = (bf16[2,384,640]{2,1,0:T(8,128)(2,1)}, bf16[2,384,640]{2,1,0:T(8,128)(2,1)}, u32[]{:S(2)}, u32[]{:S(2)}) collective-permute-start(bf16[2,384,640]{2,1,0:T(8,128)(2,1)} %get-tuple-element.62), channel_id=1, source_target_pairs={{0,8},{8,0},{1,9},{9,1},{2,10},{10,2},{3,11},{11,3},{4,12},{12,4},... | collective-permute-start | bytes 2949128 | tf_op jit(solution)/shard_map/ppermute | solution.py:37
  76.1 1.7 copy-start.3
  128.9 11.9 %collective-permute-start.5 = (bf16[640,3072]{0,1:T(8,128)(2,1)}, bf16[640,3072]{0,1:T(8,128)(2,1)S(1)}, u32[]{:S(2)}, u32[]{:S(2)}) collective-permute-start(bf16[640,3072]{0,1:T(8,128)(2,1)} %all-gather.2.cloned.1.call-done), channel_id=1, source_target_pairs={{0,8},{8,0},{1,9},{9,1},{2,10},{10,2},{3,11},{11,3},{4,12},{12,4},... | collective-permute-start | bytes 11796488 | tf_op jit(solution)/shard_map/ppermute | solution.py:37
  140.8 2.3 %copy-start = (bf16[640,3072]{0,1:T(8,128)(2,1)S(1)}, bf16[640,3072]{0,1:T(8,128)(2,1)}, u32[]{:S(2)}) copy-start(bf16[640,3072]{0,1:T(8,128)(2,1)} %all-gather.2.cloned.1.call-done) | copy-start | bytes 11796484
Sparse Core Ops, SparseCore 0:
  39.3 89.5 all-gather.1
  155.4 53.8 reduce-scatter.1

commit v7 on v6

--- a/solution.py
+++ b/solution.py
@@ -9,6 +9,7 @@
 WIN = 4
 FRAME_AXES = ("y", "x", "c")
 CHIP_AXES = ("y", "x")
+GATHER_SPARE = 8
 
 
 def shift_frames(value, steps):
@@ -83,13 +84,14 @@
     chips = lax.axis_size(CHIP_AXES)
     block = out_weight.shape[1]
     tokens = text_keys.shape[0]
-    packed = jnp.concatenate([out_weight, text_keys.T, text_values.T], axis=1)
-    packed = lax.all_gather(packed, CHIP_AXES, axis=1, tiled=True)
+    spare = jnp.zeros((width, GATHER_SPARE), out_weight.dtype)
+    packed = jnp.concatenate([out_weight, text_keys.T, text_values.T, spare], axis=1)
+    packed = lax.all_gather(lax.all_gather(packed, "y", axis=1, tiled=True), "x", axis=1, tiled=True)
     packed, frame_parts = lax.optimization_barrier((packed, frame_parts))
     pair = jnp.stack([packed, swap_cores(packed)]).reshape(2, width, chips, -1)
     weight_pair = pair[:, :, :, :block]
     text_kt = pair[:, :, :, block : block + tokens].transpose(1, 0, 2, 3).reshape(width, -1)
-    text_vt = pair[:, :, :, block + tokens :].transpose(1, 0, 2, 3).reshape(width, -1)
+    text_vt = pair[:, :, :, block + tokens : block + 2 * tokens].transpose(1, 0, 2, 3).reshape(width, -1)
 
     head_outputs = []
     for head_index in range(local_heads):
@@ -111,8 +113,8 @@
     attended_all = jnp.concatenate(head_outputs, axis=1)
     ys = lax.axis_size("y")
     xs = lax.axis_size("x")
-    w5 = weight_pair.reshape(2, width, ys, xs, block)
-    partial_out = jnp.einsum("rk,ckyxn->yrcxn", attended_all, w5, preferred_element_type=jnp.float32)
+    w5 = weight_pair.reshape(2, width, xs, ys, block)
+    partial_out = jnp.einsum("rk,ckxyn->yrcxn", attended_all, w5, preferred_element_type=jnp.float32)
     partial_out = partial_out.reshape(groups, rows, -1)
     mixed = lax.psum_scatter(partial_out.astype(jnp.bfloat16), "head", scatter_dimension=0, tiled=True)
     mixed = mixed.reshape(rows, 2, xs, block)

time: 219 us -> 207 us (0.945)
  waiting for transfers between devices: 134 us -> 126 us
  starting transfers between devices: 26.5 us -> 23.2 us
    ppermute x1, waiting for transfers between devices: 15.4 us -> 0.01 us  [relay_back(): return lax.ppermute(hop, FRAME_AXES, second)]
    all_gather x1 -> x2, waiting for transfers between devices: 41.8 us -> 47.2 us  [the longest x1 28.8 us: on_device(): lax.all_gather(lax.all_gather(packed, 'y', axis=1, tiled=True), 'x', axis...]
    ppermute x3, starting transfers between devices: 14.4 us -> 11.2 us  [swap_cores(): return lax.ppermute(value, 'c', [(0, 1), (1, 0)])]
    reduce_scatter x1, waiting for transfers between devices: 54 us -> 56.6 us  [on_device(): lax.psum_scatter(partial_out.astype(jnp.bfloat16), 'head', scatter_dimens...]
  transfers between devices with their start and end apart: 8 -> 9, of which waited for: 5 -> 5; matrix products, arithmetic and copies ran while one was open for 10% -> 10% of each run, Pallas kernels for 0% -> 0%
where the time goes in v7:
time: 207 us; the launch traced here: 206 us
  waiting for transfers between devices  126 us (61%)
  starting transfers between devices  23.2 us (11%)
  between operations  16.7 us (8%)
  other arithmetic  15.9 us (8%)
  matrix products  14.3 us (7%)
  local copies, waits for them, and re-layouts  10.8 us (5%)
    reduce_scatter x1, waiting for transfers between devices, on_device(): lax.psum_scatter(partial_out.astype(jnp.bfloat16), 'head', scatter_dimens...  56.6 us
    all_gather x1, waiting for transfers between devices, on_device(): lax.all_gather(lax.all_gather(packed, 'y', axis=1, tiled=True), 'x', axis...  28.8 us
    all_gather x1, waiting for transfers between devices, on_device(): lax.all_gather(packed, 'y', axis=1, tiled=True)  18.3 us
    ppermute x1, waiting for transfers between devices, relay_back(): hop = lax.ppermute(value, FRAME_AXES, first)  14.8 us
    ppermute x3, starting transfers between devices, swap_cores(): return lax.ppermute(value, 'c', [(0, 1), (1, 0)])  11.2 us
    ppermute x3, waiting for transfers between devices, swap_cores(): return lax.ppermute(value, 'c', [(0, 1), (1, 0)])  6.89 us
    ppermute x1, starting transfers between devices, relay_back(): return lax.ppermute(hop, FRAME_AXES, second)  5.36 us
    ppermute x1, starting transfers between devices, relay_back(): hop = lax.ppermute(value, FRAME_AXES, first)  5.21 us
  transfers between devices with their start and end apart: 9, of which 5 were waited for; matrix products, arithmetic and copies ran while one was open for 10% of the time, Pallas kernels for 0%

profile of v7, /device:TPU:1, one launch (start us, length us, event | category | flops | bytes accessed | tf_op | source)
XLA Modules:
  0.0 206.5 jit_solution(6002830714241544566)
XLA Ops:
  6.5 2.4 %pad_maximum_fusion = bf16[2,384,640]{2,1,0:T(8,128)(2,1)} fusion(bf16[1,384,640]{2,1,0:T(8,128)(2,1)} %bitcast.94, bf16[1,384,640]{2,1,0:T(8,128)(2,1)} %bitcast.92), kind=kLoop, calls=%fused_computation.71 | loop fusion | flops 491520 | bytes 1966080 | tf_op jit(solution)/shard_map/stack | solution.py:51
  8.9 5.2 %collective-permute-start.2 = (bf16[2,384,640]{2,1,0:T(8,128)(2,1)}, bf16[2,384,640]{2,1,0:T(8,128)(2,1)}, u32[]{:S(2)}, u32[]{:S(2)}) collective-permute-start(bf16[2,384,640]{2,1,0:T(8,128)(2,1)} %pad_maximum_fusion), channel_id=1, source_target_pairs={{0,48},{8,56},{16,0},{24,8},{32,16},{40,24},{48,32},{56,40},{64,11... | collective-permute-start | bytes 2949128 | tf_op jit(solution)/shard_map/ppermute | solution.py:33
  14.2 1.7 maximum_maximum_fusion
  15.9 1.4 collective-permute-start
  17.3 14.8 %collective-permute-done.2 = bf16[2,384,640]{2,1,0:T(8,128)(2,1)} collective-permute-done((bf16[2,384,640]{2,1,0:T(8,128)(2,1)}, bf16[2,384,640]{2,1,0:T(8,128)(2,1)}, u32[]{:S(2)}, u32[]{:S(2)}) %collective-permute-start.2) | collective-permute-done | bytes 983072 | tf_op jit(solution)/shard_map/ppermute | solution.py:33
  32.2 5.4 %collective-permute-start.3 = (bf16[2,384,640]{2,1,0:T(8,128)(2,1)}, bf16[2,384,640]{2,1,0:T(8,128)(2,1)S(1)}, u32[]{:S(2)}, u32[]{:S(2)}) collective-permute-start(bf16[2,384,640]{2,1,0:T(8,128)(2,1)} %collective-permute-done.2), channel_id=1, source_target_pairs={{48,32},{56,40},{0,48},{8,56},{16,64},{24,72},{32,80},{40,88},{112... | collective-permute-start | bytes 2949128 | tf_op jit(solution)/shard_map/ppermute | solution.py:34
  37.5 18.3 %all-gather.3.cloned.1.call-done = bf16[640,832]{0,1:T(8,128)(2,1)} async-done(((bf16[640,104]{0,1:T(8,128)(2,1)}), bf16[640,832]{0,1:T(8,128)(2,1)}) %all-gather.3.cloned.1.call-update) | async-done | bytes 1064976 | tf_op jit(solution)/shard_map/all_gather | solution.py:89
  56.0 1.5 broadcast_select_fusion
  57.5 6.5 %collective-permute-start.1 = (bf16[2,384,640]{2,1,0:T(8,128)(2,1)}, bf16[2,384,640]{2,1,0:T(8,128)(2,1)}, u32[]{:S(2)}, u32[]{:S(2)}) collective-permute-start(bf16[2,384,640]{2,1,0:T(8,128)(2,1)} %get-tuple-element.63), channel_id=1, source_target_pairs={{0,8},{8,0},{1,9},{9,1},{2,10},{10,2},{3,11},{11,3},{4,12},{12,4},... | collective-permute-start | bytes 2949128 | tf_op jit(solution)/shard_map/ppermute | solution.py:38
  64.1 0.6 dynamic_slice.18
  67.9 0.7 fusion.131
  68.6 0.6 fusion.104
  69.5 0.7 fusion.105
  70.5 1.9 collective-permute-start.4
  72.4 0.6 fusion.106
  73.3 0.7 fusion.107
  74.2 0.7 fusion.108
  75.2 1.3 fusion.77
  76.7 1.5 fusion.75
  78.4 0.7 fusion.136
  79.1 0.5 fusion.15
  79.6 0.7 fusion.135
  80.3 0.5 fusion.13
  80.9 0.7 fusion.134
  81.6 0.5 fusion.11
  82.1 0.7 fusion.133
  82.8 0.5 fusion.9
  83.3 0.7 fusion.132
  84.1 0.5 fusion.7
  84.6 0.6 fusion.16
  85.2 0.6 fusion.18
  85.8 0.6 fusion.20
  86.4 0.6 fusion.22
  87.0 0.6 fusion.24
  87.7 28.8 %all-gather.5.cloned.1.call-done = bf16[640,3328]{0,1:T(8,128)(2,1)} async-done(((bf16[640,832]{0,1:T(8,128)(2,1)}), bf16[640,3328]{0,1:T(8,128)(2,1)}) %all-gather.5.cloned.1.call-update) | async-done | bytes 4259856 | tf_op jit(solution)/shard_map/all_gather | solution.py:89
  116.5 2.8 %collective-permute-start.5 = (bf16[640,3328]{0,1:T(8,128)(2,1)}, bf16[640,3328]{0,1:T(8,128)(2,1)S(1)}, u32[]{:S(2)}, u32[]{:S(2)}) collective-permute-start(bf16[640,3328]{0,1:T(8,128)(2,1)} %all-gather.5.cloned.1.call-done), channel_id=1, source_target_pairs={{0,8},{8,0},{1,9},{9,1},{2,10},{10,2},{3,11},{11,3},{4,12},{12,4},... | collective-permute-start | bytes 12779528 | tf_op jit(solution)/shard_map/ppermute | solution.py:38
  119.3 6.9 %collective-permute-done.5 = bf16[640,3328]{0,1:T(8,128)(2,1)S(1)} collective-permute-done((bf16[640,3328]{0,1:T(8,128)(2,1)}, bf16[640,3328]{0,1:T(8,128)(2,1)S(1)}, u32[]{:S(2)}, u32[]{:S(2)}) %collective-permute-start.5) | collective-permute-done | bytes 4259872 | tf_op jit(solution)/shard_map/ppermute | solution.py:38
  126.1 1.3 fusion.63
  127.5 1.1 copy-done
  128.6 0.9 fusion
  132.9 0.4 fusion.46
  133.3 0.4 fusion.48
  133.7 0.4 fusion.50
  134.1 4.3 %convert_bitcast_fusion = bf16[8,384,2,4,80]{1,4,0,3,2:T(8,128)(2,1)S(1)} fusion(bf16[2,640,4,8,80]{1,4,3,2,0:T(8,128)(2,1)S(1)} %bitcast.91, bf16[384,640]{1,0:T(8,128)(2,1)S(1)} %fusion.50), kind=kOutput, calls=%fused_computation.5 | convolution fusion | flops 2518548480 | bytes 10977280 | tf_op jit(solution)/shard_map/rk,ckxyn->yrcxn/dot_general | solution.py:117
  138.4 2.5 %copy.9 = bf16[8,384,2,4,80]{1,4,3,2,0:T(8,128)(2,1)} copy(bf16[8,384,2,4,80]{1,4,0,3,2:T(8,128)(2,1)S(1)} %convert_bitcast_fusion) | data formatting | bytes 7864320 | tf_op jit(solution)/shard_map/convert_element_type | solution.py:119
  140.9 56.6 %reduce-scatter.2.cloned.1.call-done = bf16[1,384,640]{1,2,0:T(8,128)(2,1)} async-done(((bf16[8,384,640]{1,2,0:T(8,128)(2,1)}), bf16[1,384,640]{1,2,0:T(8,128)(2,1)}) %reduce-scatter.2.cloned.1.call-update) | async-done | bytes 491536 | tf_op jit(solution)/shard_map/reduce_scatter | solution.py:119
  197.5 1.4 fusion.64
  198.9 1.0 copy.11
  (62 shorter events, 5.4 us)
Async XLA Ops:
  6.5 49.4 %copy-start.1 = (bf16[384,640]{1,0:T(8,128)(2,1)S(1)}, bf16[384,640]{1,0:T(8,128)(2,1)}, u32[]{:S(2)}) copy-start(bf16[384,640]{1,0:T(8,128)(2,1)} %param.9) | copy-start | bytes 1474564
  6.5 49.4 %copy-start.2 = (bf16[384,640]{1,0:T(8,128)(2,1)S(1)}, bf16[384,640]{1,0:T(8,128)(2,1)}, u32[]{:S(2)}) copy-start(bf16[384,640]{1,0:T(8,128)(2,1)} %param.10) | copy-start | bytes 1474564
  6.5 49.3 %all-gather.3.cloned.1.call-start = ((), (), s32[]{:S(2)}) async-start(), calls=%async_computation.1 | async-start | bytes 1198080 | tf_op jit(solution)/shard_map/all_gather | solution.py:89
  8.9 23.3 %collective-permute-start.2 = (bf16[2,384,640]{2,1,0:T(8,128)(2,1)}, bf16[2,384,640]{2,1,0:T(8,128)(2,1)}, u32[]{:S(2)}, u32[]{:S(2)}) collective-permute-start(bf16[2,384,640]{2,1,0:T(8,128)(2,1)} %pad_maximum_fusion), channel_id=1, source_target_pairs={{0,48},{8,56},{16,0},{24,8},{32,16},{40,24},{48,32},{56,40},{64,11... | collective-permute-start | bytes 2949128 | tf_op jit(solution)/shard_map/ppermute | solution.py:33
  15.9 100.6 %all-gather.5.cloned.1.call-start = ((), (), s32[]{:S(2)}) async-start(), calls=%async_computation.2 | async-start | bytes 5324800 | tf_op jit(solution)/shard_map/all_gather | solution.py:89
  15.9 40.0 %collective-permute-start = (bf16[2,384,640]{2,1,0:T(8,128)(2,1)}, bf16[2,384,640]{2,1,0:T(8,128)(2,1)S(1)}, u32[]{:S(2)}, u32[]{:S(2)}) collective-permute-start(bf16[2,384,640]{2,1,0:T(8,128)(2,1)} %pad_maximum_fusion), channel_id=1, source_target_pairs={{0,16},{8,24},{16,32},{24,40},{32,48},{40,56},{48,64},{56,72},{64,... | collective-permute-start | bytes 2949128 | tf_op jit(solution)/shard_map/ppermute | solution.py:17
  32.2 23.8 %collective-permute-start.3 = (bf16[2,384,640]{2,1,0:T(8,128)(2,1)}, bf16[2,384,640]{2,1,0:T(8,128)(2,1)S(1)}, u32[]{:S(2)}, u32[]{:S(2)}) collective-permute-start(bf16[2,384,640]{2,1,0:T(8,128)(2,1)} %collective-permute-done.2), channel_id=1, source_target_pairs={{48,32},{56,40},{0,48},{8,56},{16,64},{24,72},{32,80},{40,88},{112... | collective-permute-start | bytes 2949128 | tf_op jit(solution)/shard_map/ppermute | solution.py:34
  55.9 8.2 %copy-start.5 = (s32[64]{0:T(128)S(1)}, s32[64]{0:T(128)}, u32[]{:S(2)}) copy-start(s32[64]{0:T(128)} %param.14) | copy-start | bytes 772
  55.9 12.0 %copy-start.4 = (s32[64]{0:T(128)S(1)}, s32[64]{0:T(128)}, u32[]{:S(2)}) copy-start(s32[64]{0:T(128)} %param.15) | copy-start | bytes 772
  55.9 141.6 %reduce-scatter.2.cloned.1.call-start = ((), (), s32[]{:S(2)}) async-start(), calls=%async_computation.3 | async-start | bytes 4423680 | tf_op jit(solution)/shard_map/reduce_scatter | solution.py:119
  57.5 17.7 %collective-permute-start.1 = (bf16[2,384,640]{2,1,0:T(8,128)(2,1)}, bf16[2,384,640]{2,1,0:T(8,128)(2,1)}, u32[]{:S(2)}, u32[]{:S(2)}) collective-permute-start(bf16[2,384,640]{2,1,0:T(8,128)(2,1)} %get-tuple-element.63), channel_id=1, source_target_pairs={{0,8},{8,0},{1,9},{9,1},{2,10},{10,2},{3,11},{11,3},{4,12},{12,4},... | collective-permute-start | bytes 2949128 | tf_op jit(solution)/shard_map/ppermute | solution.py:38
  70.5 6.3 %collective-permute-start.4 = (bf16[2,384,640]{2,1,0:T(8,128)(2,1)}, bf16[2,384,640]{2,1,0:T(8,128)(2,1)}, u32[]{:S(2)}, u32[]{:S(2)}) collective-permute-start(bf16[2,384,640]{2,1,0:T(8,128)(2,1)} %get-tuple-element.62), channel_id=1, source_target_pairs={{0,8},{8,0},{1,9},{9,1},{2,10},{10,2},{3,11},{11,3},{4,12},{12,4},... | collective-permute-start | bytes 2949128 | tf_op jit(solution)/shard_map/ppermute | solution.py:38
  76.5 1.8 copy-start.3
  116.5 9.6 %collective-permute-start.5 = (bf16[640,3328]{0,1:T(8,128)(2,1)}, bf16[640,3328]{0,1:T(8,128)(2,1)S(1)}, u32[]{:S(2)}, u32[]{:S(2)}) collective-permute-start(bf16[640,3328]{0,1:T(8,128)(2,1)} %all-gather.5.cloned.1.call-done), channel_id=1, source_target_pairs={{0,8},{8,0},{1,9},{9,1},{2,10},{10,2},{3,11},{11,3},{4,12},{12,4},... | collective-permute-start | bytes 12779528 | tf_op jit(solution)/shard_map/ppermute | solution.py:38
  126.1 2.4 %copy-start = (bf16[640,3328]{0,1:T(8,128)(2,1)S(1)}, bf16[640,3328]{0,1:T(8,128)(2,1)}, u32[]{:S(2)}) copy-start(bf16[640,3328]{0,1:T(8,128)(2,1)} %all-gather.5.cloned.1.call-done) | copy-start | bytes 12779524
Sparse Core Ops, SparseCore 0:
  16.0 39.8 all-gather.2
  58.0 58.4 all-gather.4
  141.0 56.4 reduce-scatter.1

commit v8 on v7

--- a/solution.py
+++ b/solution.py
@@ -88,10 +88,13 @@
     packed = jnp.concatenate([out_weight, text_keys.T, text_values.T, spare], axis=1)
     packed = lax.all_gather(lax.all_gather(packed, "y", axis=1, tiled=True), "x", axis=1, tiled=True)
     packed, frame_parts = lax.optimization_barrier((packed, frame_parts))
-    pair = jnp.stack([packed, swap_cores(packed)]).reshape(2, width, chips, -1)
-    weight_pair = pair[:, :, :, :block]
-    text_kt = pair[:, :, :, block : block + tokens].transpose(1, 0, 2, 3).reshape(width, -1)
-    text_vt = pair[:, :, :, block + tokens : block + 2 * tokens].transpose(1, 0, 2, 3).reshape(width, -1)
+    packed = packed.reshape(width, chips, -1)
+    text_own = packed[:, :, block : block + 2 * tokens]
+    text_pair = jnp.stack([text_own, swap_cores(text_own)])
+    text_kt = text_pair[:, :, :, :tokens].transpose(1, 0, 2, 3).reshape(width, -1)
+    text_vt = text_pair[:, :, :, tokens:].transpose(1, 0, 2, 3).reshape(width, -1)
+    weight_own = packed[:, :, :block]
+    weight_pair = jnp.stack([weight_own, swap_cores(weight_own)])
 
     head_outputs = []
     for head_index in range(local_heads):

time: 207 us -> 203 us (0.981)
  waiting for transfers between devices: 126 us -> 119 us
  local copies, waits for them, and re-layouts: 10.8 us -> 13.1 us
    ppermute x3 -> x4, waiting for transfers between devices: 6.89 us -> 0.83 us  [swap_cores(): return lax.ppermute(value, 'c', [(0, 1), (1, 0)])]
    slice x0 -> x1, local copies, waits for them, and re-layouts: none -> 2.22 us  [on_device(): weight_own = packed[:, :, :block]]
    ppermute x3 -> x4, starting transfers between devices: 11.2 us -> 13.1 us  [swap_cores(): return lax.ppermute(value, 'c', [(0, 1), (1, 0)])]
    unnamed x20 -> x18, local copies, waits for them, and re-layouts: 5.12 us -> 4.06 us
  transfers between devices with their start and end apart: 9 -> 10, of which waited for: 5 -> 5; matrix products, arithmetic and copies ran while one was open for 10% -> 14% of each run, Pallas kernels for 0% -> 0%
where the time goes in v8:
time: 203 us
  waiting for transfers between devices  119 us (59%)
  starting transfers between devices  25.1 us (12%)
  between operations  16.8 us (8%)
  matrix products  14.5 us (7%)
  other arithmetic  13.9 us (7%)
  local copies, waits for them, and re-layouts  13.1 us (6%)
    reduce_scatter x1, waiting for transfers between devices, on_device(): lax.psum_scatter(partial_out.astype(jnp.bfloat16), 'head', scatter_dimens...  56.4 us
    all_gather x1, waiting for transfers between devices, on_device(): lax.all_gather(lax.all_gather(packed, 'y', axis=1, tiled=True), 'x', axis...  28.8 us
    all_gather x1, waiting for transfers between devices, on_device(): lax.all_gather(packed, 'y', axis=1, tiled=True)  18.3 us
    ppermute x1, waiting for transfers between devices, relay_back(): hop = lax.ppermute(value, FRAME_AXES, first)  14.8 us
    ppermute x4, starting transfers between devices, swap_cores(): return lax.ppermute(value, 'c', [(0, 1), (1, 0)])  13.1 us
    ppermute x1, starting transfers between devices, relay_back(): return lax.ppermute(hop, FRAME_AXES, second)  5.36 us
    ppermute x1, starting transfers between devices, relay_back(): hop = lax.ppermute(value, FRAME_AXES, first)  5.21 us
    dot_general x1, matrix products, on_device(): jnp.einsum('rk,ckxyn->yrcxn', attended_all, w5, preferred_element_type=jn...  4.52 us
  transfers between devices with their start and end apart: 10, of which 5 were waited for; matrix products, arithmetic and copies ran while one was open for 14% of the time, Pallas kernels for 0%

profile of v8, /device:TPU:1, one launch (start us, length us, event | category | flops | bytes accessed | tf_op | source)
XLA Modules:
  0.0 202.7 jit_solution(15236489433286057938)
XLA Ops:
  6.5 2.4 %pad_maximum_fusion = bf16[2,384,640]{2,1,0:T(8,128)(2,1)} fusion(bf16[1,384,640]{2,1,0:T(8,128)(2,1)} %bitcast.91, bf16[1,384,640]{2,1,0:T(8,128)(2,1)} %bitcast.89), kind=kLoop, calls=%fused_computation.72 | loop fusion | flops 491520 | bytes 1966080 | tf_op jit(solution)/shard_map/stack | solution.py:51
  8.9 5.2 %collective-permute-start.2 = (bf16[2,384,640]{2,1,0:T(8,128)(2,1)}, bf16[2,384,640]{2,1,0:T(8,128)(2,1)}, u32[]{:S(2)}, u32[]{:S(2)}) collective-permute-start(bf16[2,384,640]{2,1,0:T(8,128)(2,1)} %pad_maximum_fusion), channel_id=1, source_target_pairs={{0,48},{8,56},{16,0},{24,8},{32,16},{40,24},{48,32},{56,40},{64,11... | collective-permute-start | bytes 2949128 | tf_op jit(solution)/shard_map/ppermute | solution.py:33
  14.2 1.7 maximum_maximum_fusion
  15.9 1.4 collective-permute-start
  17.3 14.8 %collective-permute-done.2 = bf16[2,384,640]{2,1,0:T(8,128)(2,1)} collective-permute-done((bf16[2,384,640]{2,1,0:T(8,128)(2,1)}, bf16[2,384,640]{2,1,0:T(8,128)(2,1)}, u32[]{:S(2)}, u32[]{:S(2)}) %collective-permute-start.2) | collective-permute-done | bytes 983072 | tf_op jit(solution)/shard_map/ppermute | solution.py:33
  32.2 5.4 %collective-permute-start.3 = (bf16[2,384,640]{2,1,0:T(8,128)(2,1)}, bf16[2,384,640]{2,1,0:T(8,128)(2,1)S(1)}, u32[]{:S(2)}, u32[]{:S(2)}) collective-permute-start(bf16[2,384,640]{2,1,0:T(8,128)(2,1)} %collective-permute-done.2), channel_id=1, source_target_pairs={{48,32},{56,40},{0,48},{8,56},{16,64},{24,72},{32,80},{40,88},{112... | collective-permute-start | bytes 2949128 | tf_op jit(solution)/shard_map/ppermute | solution.py:34
  37.5 18.3 %all-gather.3.cloned.1.call-done = bf16[640,832]{0,1:T(8,128)(2,1)} async-done(((bf16[640,104]{0,1:T(8,128)(2,1)}), bf16[640,832]{0,1:T(8,128)(2,1)}) %all-gather.3.cloned.1.call-update) | async-done | bytes 1064976 | tf_op jit(solution)/shard_map/all_gather | solution.py:89
  56.0 1.5 broadcast_select_fusion
  57.5 6.5 %collective-permute-start.1 = (bf16[2,384,640]{2,1,0:T(8,128)(2,1)}, bf16[2,384,640]{2,1,0:T(8,128)(2,1)}, u32[]{:S(2)}, u32[]{:S(2)}) collective-permute-start(bf16[2,384,640]{2,1,0:T(8,128)(2,1)} %get-tuple-element.65), channel_id=1, source_target_pairs={{0,8},{8,0},{1,9},{9,1},{2,10},{10,2},{3,11},{11,3},{4,12},{12,4},... | collective-permute-start | bytes 2949128 | tf_op jit(solution)/shard_map/ppermute | solution.py:38
  64.1 0.6 dynamic_slice.18
  67.9 0.7 fusion.137
  68.6 0.6 fusion.109
  69.5 0.7 fusion.110
  70.5 1.9 collective-permute-start.4
  72.4 0.6 fusion.111
  73.3 0.7 fusion.112
  74.2 0.7 fusion.113
  75.2 1.3 fusion.82
  76.7 1.5 fusion.80
  78.4 0.7 fusion.142
  79.1 0.5 fusion.18
  79.6 0.7 fusion.141
  80.3 0.5 fusion.16
  80.9 0.7 fusion.140
  81.6 0.5 fusion.14
  82.1 0.7 fusion.139
  82.8 0.5 fusion.12
  83.3 0.7 fusion.138
  84.1 0.5 fusion.10
  84.6 0.6 fusion.21
  85.2 0.6 fusion.23
  85.8 0.6 fusion.25
  86.4 0.6 fusion.27
  87.0 0.6 fusion.29
  87.7 28.8 %all-gather.5.cloned.1.call-done = bf16[640,3328]{0,1:T(8,128)(2,1)} async-done(((bf16[640,832]{0,1:T(8,128)(2,1)}), bf16[640,3328]{0,1:T(8,128)(2,1)}) %all-gather.5.cloned.1.call-update) | async-done | bytes 4259856 | tf_op jit(solution)/shard_map/all_gather | solution.py:89
  116.5 1.2 slice_bitcast_fusion.8
  117.7 2.6 %collective-permute-start.6 = (bf16[640,32,16]{0,2,1:T(8,128)(2,1)S(1)}, bf16[640,32,16]{0,2,1:T(8,128)(2,1)S(1)}, u32[]{:S(2)}, u32[]{:S(2)}) collective-permute-start(bf16[640,32,16]{0,2,1:T(8,128)(2,1)S(1)} %get-tuple-element.53), channel_id=1, source_target_pairs={{0,8},{8,0},{1,9},{9,1},{2,10},{10,2},{3,11},{11,3},{4,12},{12,4},... | collective-permute-start | bytes 1966088 | tf_op jit(solution)/shard_map/ppermute | solution.py:38
  120.3 2.2 %slice.211 = bf16[640,32,80]{0,2,1:T(8,128)(2,1)S(1)} slice(bf16[640,32,104]{0,2,1:T(8,128)(2,1)} %bitcast.94), slice={[0:640], [0:32], [0:80]} | slice | bytes 6553600 | tf_op jit(solution)/shard_map/slice | solution.py:96
  122.5 2.1 %collective-permute-start.5 = (bf16[640,32,80]{0,2,1:T(8,128)(2,1)S(1)}, bf16[640,32,80]{0,2,1:T(8,128)(2,1)S(1)}, u32[]{:S(2)}, u32[]{:S(2)}) collective-permute-start(bf16[640,32,80]{0,2,1:T(8,128)(2,1)S(1)} %slice.211), channel_id=1, source_target_pairs={{0,8},{8,0},{1,9},{9,1},{2,10},{10,2},{3,11},{11,3},{4,12},{12,4},... | collective-permute-start | bytes 9830408 | tf_op jit(solution)/shard_map/ppermute | solution.py:38
  128.2 0.4 fusion.51
  128.6 0.4 fusion.53
  129.0 0.4 fusion.55
  129.4 0.8 collective-permute-done.5
  130.2 4.5 %convert_bitcast_fusion = bf16[8,384,2,4,80]{1,4,0,3,2:T(8,128)(2,1)S(1)} fusion(bf16[1,640,4,8,80]{1,4,3,2,0:T(8,128)(2,1)S(1)} %bitcast.111, bf16[1,640,4,8,80]{1,4,3,2,0:T(8,128)(2,1)S(1)} %bitcast.95, bf16[384,640]{1,0:T(8,128)(2,1)S(1)} %fusion.55), kind=kOutput, calls=%fused_computation.4 | convolution fusion | flops 2521825280 | bytes 10977280 | tf_op jit(solution)/shard_map/rk,ckxyn->yrcxn/dot_general | solution.py:120
  134.8 2.5 %copy.9 = bf16[8,384,2,4,80]{1,4,3,2,0:T(8,128)(2,1)} copy(bf16[8,384,2,4,80]{1,4,0,3,2:T(8,128)(2,1)S(1)} %convert_bitcast_fusion) | data formatting | bytes 7864320 | tf_op jit(solution)/shard_map/convert_element_type | solution.py:122
  137.3 56.4 %reduce-scatter.2.cloned.1.call-done = bf16[1,384,640]{1,2,0:T(8,128)(2,1)} async-done(((bf16[8,384,640]{1,2,0:T(8,128)(2,1)}), bf16[1,384,640]{1,2,0:T(8,128)(2,1)}) %reduce-scatter.2.cloned.1.call-update) | async-done | bytes 491536 | tf_op jit(solution)/shard_map/reduce_scatter | solution.py:122
  193.7 1.4 fusion.69
  195.1 1.0 copy.11
  (63 shorter events, 5.5 us)
Async XLA Ops:
  6.5 49.4 %copy-start = (bf16[384,640]{1,0:T(8,128)(2,1)S(1)}, bf16[384,640]{1,0:T(8,128)(2,1)}, u32[]{:S(2)}) copy-start(bf16[384,640]{1,0:T(8,128)(2,1)} %param.9) | copy-start | bytes 1474564
  6.5 49.4 %copy-start.1 = (bf16[384,640]{1,0:T(8,128)(2,1)S(1)}, bf16[384,640]{1,0:T(8,128)(2,1)}, u32[]{:S(2)}) copy-start(bf16[384,640]{1,0:T(8,128)(2,1)} %param.10) | copy-start | bytes 1474564
  6.5 49.3 %all-gather.3.cloned.1.call-start = ((), (), s32[]{:S(2)}) async-start(), calls=%async_computation.1 | async-start | bytes 1198080 | tf_op jit(solution)/shard_map/all_gather | solution.py:89
  8.9 23.3 %collective-permute-start.2 = (bf16[2,384,640]{2,1,0:T(8,128)(2,1)}, bf16[2,384,640]{2,1,0:T(8,128)(2,1)}, u32[]{:S(2)}, u32[]{:S(2)}) collective-permute-start(bf16[2,384,640]{2,1,0:T(8,128)(2,1)} %pad_maximum_fusion), channel_id=1, source_target_pairs={{0,48},{8,56},{16,0},{24,8},{32,16},{40,24},{48,32},{56,40},{64,11... | collective-permute-start | bytes 2949128 | tf_op jit(solution)/shard_map/ppermute | solution.py:33
  15.9 100.6 %all-gather.5.cloned.1.call-start = ((), (), s32[]{:S(2)}) async-start(), calls=%async_computation.2 | async-start | bytes 5324800 | tf_op jit(solution)/shard_map/all_gather | solution.py:89
  15.9 40.0 %collective-permute-start = (bf16[2,384,640]{2,1,0:T(8,128)(2,1)}, bf16[2,384,640]{2,1,0:T(8,128)(2,1)S(1)}, u32[]{:S(2)}, u32[]{:S(2)}) collective-permute-start(bf16[2,384,640]{2,1,0:T(8,128)(2,1)} %pad_maximum_fusion), channel_id=1, source_target_pairs={{0,16},{8,24},{16,32},{24,40},{32,48},{40,56},{48,64},{56,72},{64,... | collective-permute-start | bytes 2949128 | tf_op jit(solution)/shard_map/ppermute | solution.py:17
  32.2 23.8 %collective-permute-start.3 = (bf16[2,384,640]{2,1,0:T(8,128)(2,1)}, bf16[2,384,640]{2,1,0:T(8,128)(2,1)S(1)}, u32[]{:S(2)}, u32[]{:S(2)}) collective-permute-start(bf16[2,384,640]{2,1,0:T(8,128)(2,1)} %collective-permute-done.2), channel_id=1, source_target_pairs={{48,32},{56,40},{0,48},{8,56},{16,64},{24,72},{32,80},{40,88},{112... | collective-permute-start | bytes 2949128 | tf_op jit(solution)/shard_map/ppermute | solution.py:34
  55.9 8.2 %copy-start.4 = (s32[64]{0:T(128)S(1)}, s32[64]{0:T(128)}, u32[]{:S(2)}) copy-start(s32[64]{0:T(128)} %param.14) | copy-start | bytes 772
  55.9 12.0 %copy-start.3 = (s32[64]{0:T(128)S(1)}, s32[64]{0:T(128)}, u32[]{:S(2)}) copy-start(s32[64]{0:T(128)} %param.15) | copy-start | bytes 772
  55.9 137.8 %reduce-scatter.2.cloned.1.call-start = ((), (), s32[]{:S(2)}) async-start(), calls=%async_computation.3 | async-start | bytes 4423680 | tf_op jit(solution)/shard_map/reduce_scatter | solution.py:122
  57.5 17.7 %collective-permute-start.1 = (bf16[2,384,640]{2,1,0:T(8,128)(2,1)}, bf16[2,384,640]{2,1,0:T(8,128)(2,1)}, u32[]{:S(2)}, u32[]{:S(2)}) collective-permute-start(bf16[2,384,640]{2,1,0:T(8,128)(2,1)} %get-tuple-element.65), channel_id=1, source_target_pairs={{0,8},{8,0},{1,9},{9,1},{2,10},{10,2},{3,11},{11,3},{4,12},{12,4},... | collective-permute-start | bytes 2949128 | tf_op jit(solution)/shard_map/ppermute | solution.py:38
  70.5 6.3 %collective-permute-start.4 = (bf16[2,384,640]{2,1,0:T(8,128)(2,1)}, bf16[2,384,640]{2,1,0:T(8,128)(2,1)}, u32[]{:S(2)}, u32[]{:S(2)}) collective-permute-start(bf16[2,384,640]{2,1,0:T(8,128)(2,1)} %get-tuple-element.64), channel_id=1, source_target_pairs={{0,8},{8,0},{1,9},{9,1},{2,10},{10,2},{3,11},{11,3},{4,12},{12,4},... | collective-permute-start | bytes 2949128 | tf_op jit(solution)/shard_map/ppermute | solution.py:38
  76.5 1.8 copy-start.2
  117.7 6.9 %collective-permute-start.6 = (bf16[640,32,16]{0,2,1:T(8,128)(2,1)S(1)}, bf16[640,32,16]{0,2,1:T(8,128)(2,1)S(1)}, u32[]{:S(2)}, u32[]{:S(2)}) collective-permute-start(bf16[640,32,16]{0,2,1:T(8,128)(2,1)S(1)} %get-tuple-element.53), channel_id=1, source_target_pairs={{0,8},{8,0},{1,9},{9,1},{2,10},{10,2},{3,11},{11,3},{4,12},{12,4},... | collective-permute-start | bytes 1966088 | tf_op jit(solution)/shard_map/ppermute | solution.py:38
  122.5 7.7 %collective-permute-start.5 = (bf16[640,32,80]{0,2,1:T(8,128)(2,1)S(1)}, bf16[640,32,80]{0,2,1:T(8,128)(2,1)S(1)}, u32[]{:S(2)}, u32[]{:S(2)}) collective-permute-start(bf16[640,32,80]{0,2,1:T(8,128)(2,1)S(1)} %slice.211), channel_id=1, source_target_pairs={{0,8},{8,0},{1,9},{9,1},{2,10},{10,2},{3,11},{11,3},{4,12},{12,4},... | collective-permute-start | bytes 9830408 | tf_op jit(solution)/shard_map/ppermute | solution.py:38
Sparse Core Ops, SparseCore 0:
  16.0 39.8 all-gather.2
  58.0 58.4 all-gather.4
  137.4 56.2 reduce-scatter.1

commit v9 on v8

--- a/solution.py
+++ b/solution.py
@@ -51,8 +51,7 @@
     own = jnp.stack([keys, values])
     back2 = shift_frames(own, 2)
     back4 = relay_back(own, 2)
-    back1 = swap_cores(jnp.where(first_core, own, back2))
-    back3 = swap_cores(jnp.where(first_core, back2, back4))
+    back1, back3 = swap_cores(jnp.where(first_core, jnp.stack([own, back2]), jnp.stack([back2, back4])))
     kv_list = [own, back1, back2, back3, back4]
 
     token_ids = jnp.arange(rows, dtype=jnp.int32)

time: 203 us -> 228 us (1.12)
  waiting for transfers between devices: 119 us -> 145 us
    ppermute x1, waiting for transfers between devices: 0.01 us -> 16.1 us  [relay_back(): return lax.ppermute(hop, FRAME_AXES, second)]
    all_gather x1, waiting for transfers between devices: 28.8 us -> 36.9 us  [on_device(): lax.all_gather(lax.all_gather(packed, 'y', axis=1, tiled=True), 'x', axis...]
    ppermute x4 -> x3, starting transfers between devices: 13.1 us -> 11.7 us  [swap_cores(): return lax.ppermute(value, 'c', [(0, 1), (1, 0)])]
    unnamed x18 -> x22, local copies, waits for them, and re-layouts: 4.06 us -> 4.97 us
  transfers between devices with their start and end apart: 10 -> 9, of which waited for: 5 -> 6; matrix products, arithmetic and copies ran while one was open for 14% -> 13% of each run, Pallas kernels for 0% -> 0%
where the time goes in v9:
time: 228 us; the launch traced here: 227 us
  waiting for transfers between devices  145 us (64%)
  starting transfers between devices  23.7 us (10%)
  between operations  16.7 us (7%)
  matrix products  14.5 us (6%)
  local copies, waits for them, and re-layouts  14 us (6%)
  other arithmetic  13 us (6%)
    reduce_scatter x1, waiting for transfers between devices, on_device(): lax.psum_scatter(partial_out.astype(jnp.bfloat16), 'head', scatter_dimens...  56.4 us
    all_gather x1, waiting for transfers between devices, on_device(): lax.all_gather(lax.all_gather(packed, 'y', axis=1, tiled=True), 'x', axis...  36.9 us
    all_gather x1, waiting for transfers between devices, on_device(): lax.all_gather(packed, 'y', axis=1, tiled=True)  18.3 us
    ppermute x1, waiting for transfers between devices, relay_back(): hop = lax.ppermute(value, FRAME_AXES, first)  16.7 us
    ppermute x1, waiting for transfers between devices, relay_back(): return lax.ppermute(hop, FRAME_AXES, second)  16.1 us
    ppermute x3, starting transfers between devices, swap_cores(): return lax.ppermute(value, 'c', [(0, 1), (1, 0)])  11.7 us
    ppermute x1, starting transfers between devices, relay_back(): return lax.ppermute(hop, FRAME_AXES, second)  5.36 us
    ppermute x1, starting transfers between devices, relay_back(): hop = lax.ppermute(value, FRAME_AXES, first)  5.21 us
  transfers between devices with their start and end apart: 9, of which 6 were waited for; matrix products, arithmetic and copies ran while one was open for 13% of the time, Pallas kernels for 0%

profile of v9, /device:TPU:1, one launch (start us, length us, event | category | flops | bytes accessed | tf_op | source)
XLA Modules:
  0.0 227.2 jit_solution(6308222422223797731)
XLA Ops:
  6.5 2.3 %fusion.135 = (bf16[1,2,384,640]{3,2,1,0:T(8,128)(2,1)S(1)}, bf16[2,384,640]{2,1,0:T(8,128)(2,1)}) fusion(bf16[1,384,640]{2,1,0:T(8,128)(2,1)} %bitcast.100, bf16[1,384,640]{2,1,0:T(8,128)(2,1)} %bitcast.99), kind=kLoop, calls=%fused_computation.187 | loop fusion | flops 491520 | bytes 2949120 | tf_op jit(solution)/shard_map/stack | solution.py:54
  8.9 5.2 %collective-permute-start.1 = (bf16[2,384,640]{2,1,0:T(8,128)(2,1)}, bf16[2,384,640]{2,1,0:T(8,128)(2,1)}, u32[]{:S(2)}, u32[]{:S(2)}) collective-permute-start(bf16[2,384,640]{2,1,0:T(8,128)(2,1)} %get-tuple-element.65), channel_id=1, source_target_pairs={{0,48},{8,56},{16,0},{24,8},{32,16},{40,24},{48,32},{56,40},{64,11... | collective-permute-start | bytes 2949128 | tf_op jit(solution)/shard_map/ppermute | solution.py:33
  14.1 1.4 collective-permute-start
  15.4 16.7 %collective-permute-done.1 = bf16[2,384,640]{2,1,0:T(8,128)(2,1)} collective-permute-done((bf16[2,384,640]{2,1,0:T(8,128)(2,1)}, bf16[2,384,640]{2,1,0:T(8,128)(2,1)}, u32[]{:S(2)}, u32[]{:S(2)}) %collective-permute-start.1) | collective-permute-done | bytes 983072 | tf_op jit(solution)/shard_map/ppermute | solution.py:33
  32.1 5.4 %collective-permute-start.2 = (bf16[2,384,640]{2,1,0:T(8,128)(2,1)}, bf16[2,384,640]{2,1,0:T(8,128)(2,1)S(1)}, u32[]{:S(2)}, u32[]{:S(2)}) collective-permute-start(bf16[2,384,640]{2,1,0:T(8,128)(2,1)} %collective-permute-done.1), channel_id=1, source_target_pairs={{48,32},{56,40},{0,48},{8,56},{16,64},{24,72},{32,80},{40,88},{112... | collective-permute-start | bytes 2949128 | tf_op jit(solution)/shard_map/ppermute | solution.py:34
  37.6 0.7 maximum_maximum_fusion
  38.4 16.1 %collective-permute-done.2 = bf16[2,384,640]{2,1,0:T(8,128)(2,1)S(1)} collective-permute-done((bf16[2,384,640]{2,1,0:T(8,128)(2,1)}, bf16[2,384,640]{2,1,0:T(8,128)(2,1)S(1)}, u32[]{:S(2)}, u32[]{:S(2)}) %collective-permute-start.2) | collective-permute-done | bytes 983072 | tf_op jit(solution)/shard_map/ppermute | solution.py:34
  54.6 1.6 maximum_select_fusion
  56.2 7.0 %collective-permute-start.3 = (bf16[2,2,384,640]{3,2,1,0:T(8,128)(2,1)}, bf16[2,2,384,640]{3,2,1,0:T(8,128)(2,1)}, u32[]{:S(2)}, u32[]{:S(2)}) collective-permute-start(bf16[2,2,384,640]{3,2,1,0:T(8,128)(2,1)} %maximum_select_fusion), channel_id=1, source_target_pairs={{0,8},{8,0},{1,9},{9,1},{2,10},{10,2},{3,11},{11,3},{4,12},{12,4},... | collective-permute-start | bytes 5898248 | tf_op jit(solution)/shard_map/ppermute | solution.py:38
  63.3 18.3 %all-gather.3.cloned.1.call-done = bf16[640,832]{0,1:T(8,128)(2,1)} async-done(((bf16[640,104]{0,1:T(8,128)(2,1)}), bf16[640,832]{0,1:T(8,128)(2,1)}) %all-gather.3.cloned.1.call-update) | async-done | bytes 1064976 | tf_op jit(solution)/shard_map/all_gather | solution.py:88
  81.7 0.6 dynamic_slice.18
  85.5 0.7 fusion.138
  86.2 0.6 fusion.109
  87.1 0.7 fusion.110
  88.0 0.6 fusion.111
  88.9 0.7 fusion.112
  89.9 0.7 fusion.113
  90.8 1.1 constant_dynamic-update-slice_fusion
  91.9 1.3 fusion.82
  93.4 1.3 fusion.80
  94.9 0.7 fusion.143
  95.6 0.5 fusion.18
  96.2 0.7 fusion.142
  96.9 0.5 fusion.16
  97.4 0.7 fusion.141
  98.1 0.5 fusion.14
  98.6 0.7 fusion.140
  99.4 0.5 fusion.12
  99.9 0.7 fusion.139
  100.6 0.5 fusion.10
  101.1 0.6 fusion.21
  101.7 0.6 fusion.23
  102.4 0.6 fusion.25
  103.0 0.6 fusion.27
  103.6 0.6 fusion.29
  104.2 36.9 %all-gather.5.cloned.1.call-done = bf16[640,3328]{0,1:T(8,128)(2,1)} async-done(((bf16[640,832]{0,1:T(8,128)(2,1)}), bf16[640,3328]{0,1:T(8,128)(2,1)}) %all-gather.5.cloned.1.call-update) | async-done | bytes 4259856 | tf_op jit(solution)/shard_map/all_gather | solution.py:88
  141.1 1.2 slice_bitcast_fusion.8
  142.3 2.6 %collective-permute-start.5 = (bf16[640,32,16]{0,2,1:T(8,128)(2,1)S(1)}, bf16[640,32,16]{0,2,1:T(8,128)(2,1)S(1)}, u32[]{:S(2)}, u32[]{:S(2)}) collective-permute-start(bf16[640,32,16]{0,2,1:T(8,128)(2,1)S(1)} %get-tuple-element.53), channel_id=1, source_target_pairs={{0,8},{8,0},{1,9},{9,1},{2,10},{10,2},{3,11},{11,3},{4,12},{12,4},... | collective-permute-start | bytes 1966088 | tf_op jit(solution)/shard_map/ppermute | solution.py:38
  144.9 2.2 slice.219
  147.1 2.1 collective-permute-start.4
  153.2 0.4 fusion.53
  153.6 0.4 fusion.55
  154.0 0.8 collective-permute-done.4
  154.8 4.5 %convert_bitcast_fusion = bf16[8,384,2,4,80]{1,4,0,3,2:T(8,128)(2,1)S(1)} fusion(bf16[1,640,4,8,80]{1,4,3,2,0:T(8,128)(2,1)S(1)} %bitcast.115, bf16[1,640,4,8,80]{1,4,3,2,0:T(8,128)(2,1)S(1)} %bitcast.97, bf16[384,640]{1,0:T(8,128)(2,1)S(1)} %fusion.55), kind=kOutput, calls=%fused_computation.4 | convolution fusion | flops 2521825280 | bytes 10977280 | tf_op jit(solution)/shard_map/rk,ckxyn->yrcxn/dot_general | solution.py:119
  159.3 2.5 %copy.9 = bf16[8,384,2,4,80]{1,4,3,2,0:T(8,128)(2,1)} copy(bf16[8,384,2,4,80]{1,4,0,3,2:T(8,128)(2,1)S(1)} %convert_bitcast_fusion) | data formatting | bytes 7864320 | tf_op jit(solution)/shard_map/convert_element_type | solution.py:121
  161.9 56.4 %reduce-scatter.2.cloned.1.call-done = bf16[1,384,640]{1,2,0:T(8,128)(2,1)} async-done(((bf16[8,384,640]{1,2,0:T(8,128)(2,1)}), bf16[1,384,640]{1,2,0:T(8,128)(2,1)}) %reduce-scatter.2.cloned.1.call-update) | async-done | bytes 491536 | tf_op jit(solution)/shard_map/reduce_scatter | solution.py:121
  218.2 1.4 fusion.69
  219.7 1.0 copy.11
  (65 shorter events, 5.8 us)
Async XLA Ops:
  6.5 31.0 %copy-start.5 = (bf16[8,640]{1,0:T(8,128)(2,1)S(1)}, bf16[8,640]{1,0:T(8,128)(2,1)}, u32[]{:S(2)}) copy-start(bf16[8,640]{1,0:T(8,128)(2,1)} %param.11) | copy-start | bytes 30724
  6.5 31.0 %copy-start.4 = (bf16[8,640]{1,0:T(8,128)(2,1)S(1)}, bf16[8,640]{1,0:T(8,128)(2,1)}, u32[]{:S(2)}) copy-start(bf16[8,640]{1,0:T(8,128)(2,1)} %param.12) | copy-start | bytes 30724
  6.5 31.0 %copy-start.2 = (bf16[640,80]{0,1:T(8,128)(2,1)S(1)}, bf16[640,80]{0,1:T(8,128)(2,1)}, u32[]{:S(2)}) copy-start(bf16[640,80]{0,1:T(8,128)(2,1)} %param.13) | copy-start | bytes 307204
  6.5 75.0 %all-gather.3.cloned.1.call-start = ((), (), s32[]{:S(2)}) async-start(), calls=%async_computation.1 | async-start | bytes 1198080 | tf_op jit(solution)/shard_map/all_gather | solution.py:88
  8.9 23.3 %collective-permute-start.1 = (bf16[2,384,640]{2,1,0:T(8,128)(2,1)}, bf16[2,384,640]{2,1,0:T(8,128)(2,1)}, u32[]{:S(2)}, u32[]{:S(2)}) collective-permute-start(bf16[2,384,640]{2,1,0:T(8,128)(2,1)} %get-tuple-element.65), channel_id=1, source_target_pairs={{0,48},{8,56},{16,0},{24,8},{32,16},{40,24},{48,32},{56,40},{64,11... | collective-permute-start | bytes 2949128 | tf_op jit(solution)/shard_map/ppermute | solution.py:33
  14.1 24.3 %collective-permute-start = (bf16[2,384,640]{2,1,0:T(8,128)(2,1)}, bf16[2,384,640]{2,1,0:T(8,128)(2,1)S(1)}, u32[]{:S(2)}, u32[]{:S(2)}) collective-permute-start(bf16[2,384,640]{2,1,0:T(8,128)(2,1)} %get-tuple-element.65), channel_id=1, source_target_pairs={{0,16},{8,24},{16,32},{24,40},{32,48},{40,56},{48,64},{56,72},{64,... | collective-permute-start | bytes 2949128 | tf_op jit(solution)/shard_map/ppermute | solution.py:17
  32.1 22.4 %collective-permute-start.2 = (bf16[2,384,640]{2,1,0:T(8,128)(2,1)}, bf16[2,384,640]{2,1,0:T(8,128)(2,1)S(1)}, u32[]{:S(2)}, u32[]{:S(2)}) collective-permute-start(bf16[2,384,640]{2,1,0:T(8,128)(2,1)} %collective-permute-done.1), channel_id=1, source_target_pairs={{48,32},{56,40},{0,48},{8,56},{16,64},{24,72},{32,80},{40,88},{112... | collective-permute-start | bytes 2949128 | tf_op jit(solution)/shard_map/ppermute | solution.py:34
  38.4 102.7 %all-gather.5.cloned.1.call-start = ((), (), s32[]{:S(2)}) async-start(), calls=%async_computation.2 | async-start | bytes 5324800 | tf_op jit(solution)/shard_map/all_gather | solution.py:88
  54.5 27.1 %copy-start.6 = (s32[64]{0:T(128)S(1)}, s32[64]{0:T(128)}, u32[]{:S(2)}) copy-start(s32[64]{0:T(128)} %param.14) | copy-start | bytes 772
  54.6 31.0 %copy-start.3 = (s32[64]{0:T(128)S(1)}, s32[64]{0:T(128)}, u32[]{:S(2)}) copy-start(s32[64]{0:T(128)} %param.15) | copy-start | bytes 772
  54.6 36.2 %copy-start.1 = (bf16[384,640]{1,0:T(8,128)(2,1)S(1)}, bf16[384,640]{1,0:T(8,128)(2,1)}, u32[]{:S(2)}) copy-start(bf16[384,640]{1,0:T(8,128)(2,1)} %param.9) | copy-start | bytes 1474564
  56.2 35.7 %collective-permute-start.3 = (bf16[2,2,384,640]{3,2,1,0:T(8,128)(2,1)}, bf16[2,2,384,640]{3,2,1,0:T(8,128)(2,1)}, u32[]{:S(2)}, u32[]{:S(2)}) collective-permute-start(bf16[2,2,384,640]{3,2,1,0:T(8,128)(2,1)} %maximum_select_fusion), channel_id=1, source_target_pairs={{0,8},{8,0},{1,9},{9,1},{2,10},{10,2},{3,11},{11,3},{4,12},{12,4},... | collective-permute-start | bytes 5898248 | tf_op jit(solution)/shard_map/ppermute | solution.py:38
  81.6 136.7 %reduce-scatter.2.cloned.1.call-start = ((), (), s32[]{:S(2)}) async-start(), calls=%async_computation.3 | async-start | bytes 4423680 | tf_op jit(solution)/shard_map/reduce_scatter | solution.py:121
  93.2 1.7 copy-start
  142.3 6.9 %collective-permute-start.5 = (bf16[640,32,16]{0,2,1:T(8,128)(2,1)S(1)}, bf16[640,32,16]{0,2,1:T(8,128)(2,1)S(1)}, u32[]{:S(2)}, u32[]{:S(2)}) collective-permute-start(bf16[640,32,16]{0,2,1:T(8,128)(2,1)S(1)} %get-tuple-element.53), channel_id=1, source_target_pairs={{0,8},{8,0},{1,9},{9,1},{2,10},{10,2},{3,11},{11,3},{4,12},{12,4},... | collective-permute-start | bytes 1966088 | tf_op jit(solution)/shard_map/ppermute | solution.py:38
  147.1 7.7 %collective-permute-start.4 = (bf16[640,32,80]{0,2,1:T(8,128)(2,1)S(1)}, bf16[640,32,80]{0,2,1:T(8,128)(2,1)S(1)}, u32[]{:S(2)}, u32[]{:S(2)}) collective-permute-start(bf16[640,32,80]{0,2,1:T(8,128)(2,1)S(1)} %slice.219), channel_id=1, source_target_pairs={{0,8},{8,0},{1,9},{9,1},{2,10},{10,2},{3,11},{11,3},{4,12},{12,4},... | collective-permute-start | bytes 9830408 | tf_op jit(solution)/shard_map/ppermute | solution.py:38
Sparse Core Ops, SparseCore 0:
  38.5 43.0 all-gather.2
  83.6 57.3 all-gather.4
  162.0 56.2 reduce-scatter.1

commit v10 on v8

--- a/solution.py
+++ b/solution.py
@@ -86,7 +86,7 @@
     tokens = text_keys.shape[0]
     spare = jnp.zeros((width, GATHER_SPARE), out_weight.dtype)
     packed = jnp.concatenate([out_weight, text_keys.T, text_values.T, spare], axis=1)
-    packed = lax.all_gather(lax.all_gather(packed, "y", axis=1, tiled=True), "x", axis=1, tiled=True)
+    packed = lax.all_gather(lax.all_gather(packed, "x", axis=1, tiled=True), "y", axis=1, tiled=True)
     packed, frame_parts = lax.optimization_barrier((packed, frame_parts))
     packed = packed.reshape(width, chips, -1)
     text_own = packed[:, :, block : block + 2 * tokens]
@@ -116,8 +116,8 @@
     attended_all = jnp.concatenate(head_outputs, axis=1)
     ys = lax.axis_size("y")
     xs = lax.axis_size("x")
-    w5 = weight_pair.reshape(2, width, xs, ys, block)
-    partial_out = jnp.einsum("rk,ckxyn->yrcxn", attended_all, w5, preferred_element_type=jnp.float32)
+    w5 = weight_pair.reshape(2, width, ys, xs, block)
+    partial_out = jnp.einsum("rk,ckyxn->yrcxn", attended_all, w5, preferred_element_type=jnp.float32)
     partial_out = partial_out.reshape(groups, rows, -1)
     mixed = lax.psum_scatter(partial_out.astype(jnp.bfloat16), "head", scatter_dimension=0, tiled=True)
     mixed = mixed.reshape(rows, 2, xs, block)

time: 203 us -> 219 us (1.079)
  blocking collectives: 0 us -> 27 us
  waiting for transfers between devices: 119 us -> 109 us
    all_gather x0 -> x1, blocking collectives: none -> 27 us  [on_device(): lax.all_gather(packed, 'x', axis=1, tiled=True)]
    all_gather x2 -> x1, waiting for transfers between devices: 47.2 us -> 36.5 us  [on_device(): lax.all_gather(lax.all_gather(packed, 'x', axis=1, tiled=True), 'y', axis...]
  transfers between devices with their start and end apart: 10 -> 9, of which waited for: 5 -> 4; matrix products, arithmetic and copies ran while one was open for 14% -> 13% of each run, Pallas kernels for 0% -> 0%
where the time goes in v10:
time: 219 us
  waiting for transfers between devices  109 us (50%)
  blocking collectives  27 us (12%)
  starting transfers between devices  25.6 us (12%)
  between operations  17.1 us (8%)
  matrix products  14.5 us (7%)
  other arithmetic  13 us (6%)
  local copies, waits for them, and re-layouts  12.8 us (6%)
    reduce_scatter x1, waiting for transfers between devices, on_device(): lax.psum_scatter(partial_out.astype(jnp.bfloat16), 'head', scatter_dimens...  55 us
    all_gather x1, waiting for transfers between devices, on_device(): lax.all_gather(lax.all_gather(packed, 'x', axis=1, tiled=True), 'y', axis...  36.5 us
    all_gather x1, blocking collectives, on_device(): lax.all_gather(packed, 'x', axis=1, tiled=True)  27 us
    ppermute x1, waiting for transfers between devices, relay_back(): hop = lax.ppermute(value, FRAME_AXES, first)  16.6 us
    ppermute x4, starting transfers between devices, swap_cores(): return lax.ppermute(value, 'c', [(0, 1), (1, 0)])  13.6 us
    ppermute x1, starting transfers between devices, relay_back(): return lax.ppermute(hop, FRAME_AXES, second)  5.36 us
    ppermute x1, starting transfers between devices, relay_back(): hop = lax.ppermute(value, FRAME_AXES, first)  5.21 us
    dot_general x1, matrix products, on_device(): jnp.einsum('rk,ckyxn->yrcxn', attended_all, w5, preferred_element_type=jn...  4.52 us
  transfers between devices with their start and end apart: 9, of which 4 were waited for; matrix products, arithmetic and copies ran while one was open for 13% of the time, Pallas kernels for 0%

profile of v10, /device:TPU:1, one launch (start us, length us, event | category | flops | bytes accessed | tf_op | source)
XLA Modules:
  0.0 218.9 jit_solution(17559375766864371503)
XLA Ops:
  6.5 2.3 %pad_maximum_fusion = bf16[2,384,640]{2,1,0:T(8,128)(2,1)} fusion(bf16[1,384,640]{2,1,0:T(8,128)(2,1)} %bitcast.91, bf16[1,384,640]{2,1,0:T(8,128)(2,1)} %bitcast.89), kind=kLoop, calls=%fused_computation.72 | loop fusion | flops 491520 | bytes 1966080 | tf_op jit(solution)/shard_map/stack | solution.py:51
  8.9 5.2 %collective-permute-start.2 = (bf16[2,384,640]{2,1,0:T(8,128)(2,1)}, bf16[2,384,640]{2,1,0:T(8,128)(2,1)}, u32[]{:S(2)}, u32[]{:S(2)}) collective-permute-start(bf16[2,384,640]{2,1,0:T(8,128)(2,1)} %pad_maximum_fusion), channel_id=1, source_target_pairs={{0,48},{8,56},{16,0},{24,8},{32,16},{40,24},{48,32},{56,40},{64,11... | collective-permute-start | bytes 2949128 | tf_op jit(solution)/shard_map/ppermute | solution.py:33
  14.1 1.4 collective-permute-start
  15.5 16.6 %collective-permute-done.2 = bf16[2,384,640]{2,1,0:T(8,128)(2,1)} collective-permute-done((bf16[2,384,640]{2,1,0:T(8,128)(2,1)}, bf16[2,384,640]{2,1,0:T(8,128)(2,1)}, u32[]{:S(2)}, u32[]{:S(2)}) %collective-permute-start.2) | collective-permute-done | bytes 983072 | tf_op jit(solution)/shard_map/ppermute | solution.py:33
  32.1 5.4 %collective-permute-start.3 = (bf16[2,384,640]{2,1,0:T(8,128)(2,1)}, bf16[2,384,640]{2,1,0:T(8,128)(2,1)S(1)}, u32[]{:S(2)}, u32[]{:S(2)}) collective-permute-start(bf16[2,384,640]{2,1,0:T(8,128)(2,1)} %collective-permute-done.2), channel_id=1, source_target_pairs={{48,32},{56,40},{0,48},{8,56},{16,64},{24,72},{32,80},{40,88},{112... | collective-permute-start | bytes 2949128 | tf_op jit(solution)/shard_map/ppermute | solution.py:34
  37.5 1.0 maximum_maximum_fusion
  38.5 27.0 %all_gather.6 = bf16[640,416]{0,1:T(8,128)(2,1)} all-gather(bf16[640,104]{0,1:T(8,128)(2,1)S(1)} %maximum_maximum_fusion), channel_id=1, replica_groups=mesh['y'=8,'x'=4,'c'=2,'head'=8] {'x'}, dimensions={1}, use_global_device_ids=true | all-gather | bytes 665600 | tf_op jit(solution)/shard_map/all_gather | solution.py:89
  65.7 1.5 broadcast_select_fusion
  67.2 7.0 %collective-permute-start.1 = (bf16[2,384,640]{2,1,0:T(8,128)(2,1)}, bf16[2,384,640]{2,1,0:T(8,128)(2,1)}, u32[]{:S(2)}, u32[]{:S(2)}) collective-permute-start(bf16[2,384,640]{2,1,0:T(8,128)(2,1)} %get-tuple-element.65), channel_id=1, source_target_pairs={{0,8},{8,0},{1,9},{9,1},{2,10},{10,2},{3,11},{11,3},{4,12},{12,4},... | collective-permute-start | bytes 2949128 | tf_op jit(solution)/shard_map/ppermute | solution.py:38
  74.3 0.6 dynamic_slice.18
  78.1 0.7 fusion.137
  78.8 0.7 fusion.109
  79.7 0.6 fusion.110
  80.5 1.9 collective-permute-start.4
  82.4 0.6 fusion.111
  83.3 0.7 fusion.112
  84.3 0.7 fusion.113
  85.3 1.3 fusion.82
  86.8 1.3 fusion.80
  88.3 0.7 fusion.142
  89.0 0.5 fusion.18
  89.5 0.7 fusion.141
  90.3 0.5 fusion.16
  90.8 0.7 fusion.140
  91.5 0.5 fusion.14
  92.0 0.7 fusion.139
  92.7 0.5 fusion.12
  93.3 0.7 fusion.138
  94.0 0.5 fusion.10
  94.5 0.6 fusion.21
  95.1 0.6 fusion.23
  95.7 0.6 fusion.25
  96.3 0.6 fusion.27
  97.0 0.6 fusion.29
  97.6 36.5 %all-gather.2.cloned.1.call-done = bf16[640,3328]{0,1:T(8,128)(2,1)} async-done(((bf16[640,416]{0,1:T(8,128)(2,1)}), bf16[640,3328]{0,1:T(8,128)(2,1)}) %all-gather.2.cloned.1.call-update) | async-done | bytes 4259856 | tf_op jit(solution)/shard_map/all_gather | solution.py:89
  134.0 1.2 slice_bitcast_fusion.8
  135.2 2.6 %collective-permute-start.6 = (bf16[640,32,16]{0,2,1:T(8,128)(2,1)S(1)}, bf16[640,32,16]{0,2,1:T(8,128)(2,1)S(1)}, u32[]{:S(2)}, u32[]{:S(2)}) collective-permute-start(bf16[640,32,16]{0,2,1:T(8,128)(2,1)S(1)} %get-tuple-element.53), channel_id=1, source_target_pairs={{0,8},{8,0},{1,9},{9,1},{2,10},{10,2},{3,11},{11,3},{4,12},{12,4},... | collective-permute-start | bytes 1966088 | tf_op jit(solution)/shard_map/ppermute | solution.py:38
  137.8 2.2 %slice.211 = bf16[640,32,80]{0,2,1:T(8,128)(2,1)S(1)} slice(bf16[640,32,104]{0,2,1:T(8,128)(2,1)} %bitcast.94), slice={[0:640], [0:32], [0:80]} | slice | bytes 6553600 | tf_op jit(solution)/shard_map/slice | solution.py:96
  140.0 2.1 collective-permute-start.5
  145.7 0.4 fusion.51
  146.2 0.4 fusion.53
  146.6 0.4 fusion.55
  147.0 0.8 collective-permute-done.5
  147.8 4.5 %convert_bitcast_fusion = bf16[8,384,2,4,80]{1,4,3,0,2:T(8,128)(2,1)S(1)} fusion(bf16[1,640,8,4,80]{1,4,3,2,0:T(8,128)(2,1)S(1)} %bitcast.111, bf16[1,640,8,4,80]{1,4,3,2,0:T(8,128)(2,1)S(1)} %bitcast.95, bf16[384,640]{1,0:T(8,128)(2,1)S(1)} %fusion.55), kind=kOutput, calls=%fused_computation.4 | convolution fusion | flops 2521825280 | bytes 10977280 | tf_op jit(solution)/shard_map/rk,ckyxn->yrcxn/dot_general | solution.py:120
  152.3 2.3 %copy.9 = bf16[8,384,2,4,80]{1,4,3,2,0:T(8,128)(2,1)} copy(bf16[8,384,2,4,80]{1,4,3,0,2:T(8,128)(2,1)S(1)} %convert_bitcast_fusion) | data formatting | bytes 7864320 | tf_op jit(solution)/shard_map/convert_element_type | solution.py:122
  154.6 55.0 %reduce-scatter.2.cloned.1.call-done = bf16[1,384,640]{1,2,0:T(8,128)(2,1)} async-done(((bf16[8,384,640]{1,2,0:T(8,128)(2,1)}), bf16[1,384,640]{1,2,0:T(8,128)(2,1)}) %reduce-scatter.2.cloned.1.call-update) | async-done | bytes 491536 | tf_op jit(solution)/shard_map/reduce_scatter | solution.py:122
  209.7 1.4 fusion.69
  211.1 1.0 copy.11
  (61 shorter events, 5.5 us)
Async XLA Ops:
  6.5 59.1 %copy-start = (bf16[384,640]{1,0:T(8,128)(2,1)S(1)}, bf16[384,640]{1,0:T(8,128)(2,1)}, u32[]{:S(2)}) copy-start(bf16[384,640]{1,0:T(8,128)(2,1)} %param.9) | copy-start | bytes 1474564
  6.5 59.1 %copy-start.1 = (bf16[384,640]{1,0:T(8,128)(2,1)S(1)}, bf16[384,640]{1,0:T(8,128)(2,1)}, u32[]{:S(2)}) copy-start(bf16[384,640]{1,0:T(8,128)(2,1)} %param.10) | copy-start | bytes 1474564
  6.5 127.5 %all-gather.2.cloned.1.call-start = ((), (), s32[]{:S(2)}) async-start(), calls=%async_computation.1 | async-start | bytes 4792320 | tf_op jit(solution)/shard_map/all_gather | solution.py:89
  8.9 23.3 %collective-permute-start.2 = (bf16[2,384,640]{2,1,0:T(8,128)(2,1)}, bf16[2,384,640]{2,1,0:T(8,128)(2,1)}, u32[]{:S(2)}, u32[]{:S(2)}) collective-permute-start(bf16[2,384,640]{2,1,0:T(8,128)(2,1)} %pad_maximum_fusion), channel_id=1, source_target_pairs={{0,48},{8,56},{16,0},{24,8},{32,16},{40,24},{48,32},{56,40},{64,11... | collective-permute-start | bytes 2949128 | tf_op jit(solution)/shard_map/ppermute | solution.py:33
  14.1 51.5 %collective-permute-start = (bf16[2,384,640]{2,1,0:T(8,128)(2,1)}, bf16[2,384,640]{2,1,0:T(8,128)(2,1)S(1)}, u32[]{:S(2)}, u32[]{:S(2)}) collective-permute-start(bf16[2,384,640]{2,1,0:T(8,128)(2,1)} %pad_maximum_fusion), channel_id=1, source_target_pairs={{0,16},{8,24},{16,32},{24,40},{32,48},{40,56},{48,64},{56,72},{64,... | collective-permute-start | bytes 2949128 | tf_op jit(solution)/shard_map/ppermute | solution.py:17
  32.1 33.5 %collective-permute-start.3 = (bf16[2,384,640]{2,1,0:T(8,128)(2,1)}, bf16[2,384,640]{2,1,0:T(8,128)(2,1)S(1)}, u32[]{:S(2)}, u32[]{:S(2)}) collective-permute-start(bf16[2,384,640]{2,1,0:T(8,128)(2,1)} %collective-permute-done.2), channel_id=1, source_target_pairs={{48,32},{56,40},{0,48},{8,56},{16,64},{24,72},{32,80},{40,88},{112... | collective-permute-start | bytes 2949128 | tf_op jit(solution)/shard_map/ppermute | solution.py:34
  38.5 35.7 %copy-start.4 = (s32[64]{0:T(128)S(1)}, s32[64]{0:T(128)}, u32[]{:S(2)}) copy-start(s32[64]{0:T(128)} %param.14) | copy-start | bytes 772
  38.5 39.6 %copy-start.3 = (s32[64]{0:T(128)S(1)}, s32[64]{0:T(128)}, u32[]{:S(2)}) copy-start(s32[64]{0:T(128)} %param.15) | copy-start | bytes 772
  65.6 144.1 %reduce-scatter.2.cloned.1.call-start = ((), (), s32[]{:S(2)}) async-start(), calls=%async_computation.2 | async-start | bytes 4423680 | tf_op jit(solution)/shard_map/reduce_scatter | solution.py:122
  67.2 18.1 %collective-permute-start.1 = (bf16[2,384,640]{2,1,0:T(8,128)(2,1)}, bf16[2,384,640]{2,1,0:T(8,128)(2,1)}, u32[]{:S(2)}, u32[]{:S(2)}) collective-permute-start(bf16[2,384,640]{2,1,0:T(8,128)(2,1)} %get-tuple-element.65), channel_id=1, source_target_pairs={{0,8},{8,0},{1,9},{9,1},{2,10},{10,2},{3,11},{11,3},{4,12},{12,4},... | collective-permute-start | bytes 2949128 | tf_op jit(solution)/shard_map/ppermute | solution.py:38
  80.5 6.2 %collective-permute-start.4 = (bf16[2,384,640]{2,1,0:T(8,128)(2,1)}, bf16[2,384,640]{2,1,0:T(8,128)(2,1)}, u32[]{:S(2)}, u32[]{:S(2)}) collective-permute-start(bf16[2,384,640]{2,1,0:T(8,128)(2,1)} %get-tuple-element.64), channel_id=1, source_target_pairs={{0,8},{8,0},{1,9},{9,1},{2,10},{10,2},{3,11},{11,3},{4,12},{12,4},... | collective-permute-start | bytes 2949128 | tf_op jit(solution)/shard_map/ppermute | solution.py:38
  86.6 1.7 copy-start.2
  135.2 6.9 %collective-permute-start.6 = (bf16[640,32,16]{0,2,1:T(8,128)(2,1)S(1)}, bf16[640,32,16]{0,2,1:T(8,128)(2,1)S(1)}, u32[]{:S(2)}, u32[]{:S(2)}) collective-permute-start(bf16[640,32,16]{0,2,1:T(8,128)(2,1)S(1)} %get-tuple-element.53), channel_id=1, source_target_pairs={{0,8},{8,0},{1,9},{9,1},{2,10},{10,2},{3,11},{11,3},{4,12},{12,4},... | collective-permute-start | bytes 1966088 | tf_op jit(solution)/shard_map/ppermute | solution.py:38
  140.0 7.7 %collective-permute-start.5 = (bf16[640,32,80]{0,2,1:T(8,128)(2,1)S(1)}, bf16[640,32,80]{0,2,1:T(8,128)(2,1)S(1)}, u32[]{:S(2)}, u32[]{:S(2)}) collective-permute-start(bf16[640,32,80]{0,2,1:T(8,128)(2,1)S(1)} %slice.211), channel_id=1, source_target_pairs={{0,8},{8,0},{1,9},{9,1},{2,10},{10,2},{3,11},{11,3},{4,12},{12,4},... | collective-permute-start | bytes 9830408 | tf_op jit(solution)/shard_map/ppermute | solution.py:38
Sparse Core Ops, SparseCore 0:
  65.7 68.3 all-gather.1
  154.8 54.8 reduce-scatter.1

commit v11 on v8

--- a/solution.py
+++ b/solution.py
@@ -86,7 +86,9 @@
     tokens = text_keys.shape[0]
     spare = jnp.zeros((width, GATHER_SPARE), out_weight.dtype)
     packed = jnp.concatenate([out_weight, text_keys.T, text_values.T, spare], axis=1)
-    packed = lax.all_gather(lax.all_gather(packed, "y", axis=1, tiled=True), "x", axis=1, tiled=True)
+    packed = lax.all_gather(packed, "y", axis=1, tiled=True).reshape(width, lax.axis_size("y"), -1)
+    packed = packed[:, :, : block + 2 * tokens].reshape(width, -1)
+    packed = lax.all_gather(packed, "x", axis=1, tiled=True)
     packed, frame_parts = lax.optimization_barrier((packed, frame_parts))
     packed = packed.reshape(width, chips, -1)
     text_own = packed[:, :, block : block + 2 * tokens]

time: 203 us -> 219 us (1.079)
  waiting for transfers between devices: 119 us -> 131 us
    all_gather x1, waiting for transfers between devices: 18.3 us -> 0.02 us  [on_device(): lax.all_gather(packed, 'y', axis=1, tiled=True)]
    ppermute x1, waiting for transfers between devices: 0.01 us -> 17 us  [relay_back(): return lax.ppermute(hop, FRAME_AXES, second)]
    all_gather x1, waiting for transfers between devices: 28.8 us -> 42.2 us  [on_device(): packed = lax.all_gather(packed, 'x', axis=1, tiled=True)]
    slice x0 -> x1, local copies, waits for them, and re-layouts: none -> 2.24 us  [on_device(): packed = packed[:, :, :block + 2 * tokens].reshape(width, -1)]
where the time goes in v11:
time: 219 us; the launch traced here: 218 us
  waiting for transfers between devices  131 us (60%)
  starting transfers between devices  25.8 us (12%)
  between operations  16.6 us (8%)
  local copies, waits for them, and re-layouts  15.2 us (7%)
  other arithmetic  14.8 us (7%)
  matrix products  14.5 us (7%)
    reduce_scatter x1, waiting for transfers between devices, on_device(): lax.psum_scatter(partial_out.astype(jnp.bfloat16), 'head', scatter_dimens...  56.3 us
    all_gather x1, waiting for transfers between devices, on_device(): packed = lax.all_gather(packed, 'x', axis=1, tiled=True)  42.2 us
    ppermute x1, waiting for transfers between devices, relay_back(): return lax.ppermute(hop, FRAME_AXES, second)  17 us
    ppermute x1, waiting for transfers between devices, relay_back(): hop = lax.ppermute(value, FRAME_AXES, first)  14.8 us
    ppermute x4, starting transfers between devices, swap_cores(): return lax.ppermute(value, 'c', [(0, 1), (1, 0)])  13.6 us
    ppermute x1, starting transfers between devices, relay_back(): return lax.ppermute(hop, FRAME_AXES, second)  5.36 us
    ppermute x1, starting transfers between devices, relay_back(): hop = lax.ppermute(value, FRAME_AXES, first)  5.34 us
    dot_general x1, matrix products, on_device(): jnp.einsum('rk,ckxyn->yrcxn', attended_all, w5, preferred_element_type=jn...  4.53 us
  transfers between devices with their start and end apart: 10, of which 5 were waited for; matrix products, arithmetic and copies ran while one was open for 14% of the time, Pallas kernels for 0%

profile of v11, /device:TPU:1, one launch (start us, length us, event | category | flops | bytes accessed | tf_op | source)
XLA Modules:
  0.0 218.3 jit_solution(14147695448890881034)
XLA Ops:
  6.5 2.3 %pad_maximum_fusion = bf16[2,384,640]{2,1,0:T(8,128)(2,1)} fusion(bf16[1,384,640]{2,1,0:T(8,128)(2,1)} %bitcast.93, bf16[1,384,640]{2,1,0:T(8,128)(2,1)} %bitcast.91), kind=kLoop, calls=%fused_computation.72 | loop fusion | flops 491520 | bytes 1966080 | tf_op jit(solution)/shard_map/stack | solution.py:51
  8.8 5.3 %collective-permute-start.2 = (bf16[2,384,640]{2,1,0:T(8,128)(2,1)}, bf16[2,384,640]{2,1,0:T(8,128)(2,1)}, u32[]{:S(2)}, u32[]{:S(2)}) collective-permute-start(bf16[2,384,640]{2,1,0:T(8,128)(2,1)} %pad_maximum_fusion), channel_id=1, source_target_pairs={{0,48},{8,56},{16,0},{24,8},{32,16},{40,24},{48,32},{56,40},{64,11... | collective-permute-start | bytes 2949128 | tf_op jit(solution)/shard_map/ppermute | solution.py:33
  14.2 1.7 maximum_maximum_fusion
  16.0 1.4 collective-permute-start
  17.4 14.8 %collective-permute-done.2 = bf16[2,384,640]{2,1,0:T(8,128)(2,1)} collective-permute-done((bf16[2,384,640]{2,1,0:T(8,128)(2,1)}, bf16[2,384,640]{2,1,0:T(8,128)(2,1)}, u32[]{:S(2)}, u32[]{:S(2)}) %collective-permute-start.2) | collective-permute-done | bytes 983072 | tf_op jit(solution)/shard_map/ppermute | solution.py:33
  32.2 5.4 %collective-permute-start.3 = (bf16[2,384,640]{2,1,0:T(8,128)(2,1)}, bf16[2,384,640]{2,1,0:T(8,128)(2,1)S(1)}, u32[]{:S(2)}, u32[]{:S(2)}) collective-permute-start(bf16[2,384,640]{2,1,0:T(8,128)(2,1)} %collective-permute-done.2), channel_id=1, source_target_pairs={{48,32},{56,40},{0,48},{8,56},{16,64},{24,72},{32,80},{40,88},{112... | collective-permute-start | bytes 2949128 | tf_op jit(solution)/shard_map/ppermute | solution.py:34
  37.6 17.0 %collective-permute-done.3 = bf16[2,384,640]{2,1,0:T(8,128)(2,1)S(1)} collective-permute-done((bf16[2,384,640]{2,1,0:T(8,128)(2,1)}, bf16[2,384,640]{2,1,0:T(8,128)(2,1)S(1)}, u32[]{:S(2)}, u32[]{:S(2)}) %collective-permute-start.3) | collective-permute-done | bytes 983072 | tf_op jit(solution)/shard_map/ppermute | solution.py:34
  54.6 2.7 %broadcast_select_fusion = (bf16[2,384,640]{2,1,0:T(8,128)(2,1)}, bf16[2,384,640]{2,1,0:T(8,128)(2,1)}) fusion(bf16[2,384,640]{2,1,0:T(8,128)(2,1)S(1)} %collective-permute-done, bf16[2,384,640]{2,1,0:T(8,128)(2,1)S(1)} %collective-permute-done.3, pred[]{:T(512)S(6)} %eq.3, bf16[1,384,640]{2,1,0:T(8,128)(2,1)} %bitcast.94, bf16[1,384,640]{2,1,0:T(8,128)(2,1)} %bitcast.92), kind=kLoop, calls=%fused_computation.73 | loop fusion | flops 1474560 | bytes 4915201 | tf_op jit(solution)/shard_map/jit(_where)/select_n | solution.py:55
  57.3 7.0 %collective-permute-start.1 = (bf16[2,384,640]{2,1,0:T(8,128)(2,1)}, bf16[2,384,640]{2,1,0:T(8,128)(2,1)}, u32[]{:S(2)}, u32[]{:S(2)}) collective-permute-start(bf16[2,384,640]{2,1,0:T(8,128)(2,1)} %get-tuple-element.65), channel_id=1, source_target_pairs={{0,8},{8,0},{1,9},{9,1},{2,10},{10,2},{3,11},{11,3},{4,12},{12,4},... | collective-permute-start | bytes 2949128 | tf_op jit(solution)/shard_map/ppermute | solution.py:38
  64.4 0.6 dynamic_slice.18
  66.3 0.7 fusion.137
  67.0 0.6 fusion.110
  67.6 2.2 %slice.197 = bf16[640,8,96]{0,2,1:T(8,128)(2,1)} slice(bf16[640,8,104]{0,2,1:T(8,128)(2,1)} %bitcast.100), slice={[0:640], [0:8], [0:96]} | slice | bytes 1966080 | tf_op jit(solution)/shard_map/slice | solution.py:90
  69.9 0.6 fusion.109
  72.9 1.9 collective-permute-start.4
  74.8 0.6 fusion.111
  75.7 0.7 fusion.112
  76.6 0.6 fusion.113
  77.6 1.3 fusion.82
  79.2 1.3 fusion.80
  80.7 0.7 fusion.142
  81.4 0.5 fusion.18
  81.9 0.7 fusion.141
  82.6 0.5 fusion.16
  83.2 0.7 fusion.140
  83.9 0.5 fusion.14
  84.4 0.7 fusion.139
  85.1 0.5 fusion.12
  85.6 0.7 fusion.138
  86.4 0.5 fusion.10
  86.9 0.6 fusion.21
  87.5 0.6 fusion.23
  88.1 0.6 fusion.25
  88.7 0.6 fusion.27
  89.3 0.6 fusion.29
  90.0 42.2 %all-gather.5.cloned.1.call-done = bf16[640,3072]{0,1:T(8,128)(2,1)} async-done(((bf16[640,768]{0,1:T(8,128)(2,1)}), bf16[640,3072]{0,1:T(8,128)(2,1)}) %all-gather.5.cloned.1.call-update) | async-done | bytes 3932176 | tf_op jit(solution)/shard_map/all_gather | solution.py:91
  132.2 1.2 slice_bitcast_fusion.8
  133.4 2.6 %collective-permute-start.6 = (bf16[640,32,16]{0,2,1:T(8,128)(2,1)S(1)}, bf16[640,32,16]{0,2,1:T(8,128)(2,1)S(1)}, u32[]{:S(2)}, u32[]{:S(2)}) collective-permute-start(bf16[640,32,16]{0,2,1:T(8,128)(2,1)S(1)} %get-tuple-element.53), channel_id=1, source_target_pairs={{0,8},{8,0},{1,9},{9,1},{2,10},{10,2},{3,11},{11,3},{4,12},{12,4},... | collective-permute-start | bytes 1966088 | tf_op jit(solution)/shard_map/ppermute | solution.py:38
  136.0 2.2 %slice.216 = bf16[640,32,80]{0,2,1:T(8,128)(2,1)S(1)} slice(bf16[640,32,96]{0,2,1:T(8,128)(2,1)} %bitcast.96), slice={[0:640], [0:32], [0:80]} | slice | bytes 6553600 | tf_op jit(solution)/shard_map/slice | solution.py:98
  138.2 2.1 collective-permute-start.5
  143.9 0.4 fusion.51
  144.3 0.4 fusion.53
  145.1 0.8 collective-permute-done.5
  145.9 4.5 %convert_bitcast_fusion = bf16[8,384,2,4,80]{1,4,0,3,2:T(8,128)(2,1)S(1)} fusion(bf16[1,640,4,8,80]{1,4,3,2,0:T(8,128)(2,1)S(1)} %bitcast.115, bf16[1,640,4,8,80]{1,4,3,2,0:T(8,128)(2,1)S(1)} %bitcast.98, bf16[384,640]{1,0:T(8,128)(2,1)S(1)} %fusion.55), kind=kOutput, calls=%fused_computation.4 | convolution fusion | flops 2521825280 | bytes 10977280 | tf_op jit(solution)/shard_map/rk,ckxyn->yrcxn/dot_general | solution.py:122
  150.5 2.5 %copy.9 = bf16[8,384,2,4,80]{1,4,3,2,0:T(8,128)(2,1)} copy(bf16[8,384,2,4,80]{1,4,0,3,2:T(8,128)(2,1)S(1)} %convert_bitcast_fusion) | data formatting | bytes 7864320 | tf_op jit(solution)/shard_map/convert_element_type | solution.py:124
  153.0 56.3 %reduce-scatter.2.cloned.1.call-done = bf16[1,384,640]{1,2,0:T(8,128)(2,1)} async-done(((bf16[8,384,640]{1,2,0:T(8,128)(2,1)}), bf16[1,384,640]{1,2,0:T(8,128)(2,1)}) %reduce-scatter.2.cloned.1.call-update) | async-done | bytes 491536 | tf_op jit(solution)/shard_map/reduce_scatter | solution.py:124
  209.3 1.4 fusion.69
  210.7 1.0 copy.11
  (64 shorter events, 5.9 us)
Async XLA Ops:
  6.5 61.0 %all-gather.3.cloned.1.call-start = ((), (), s32[]{:S(2)}) async-start(), calls=%async_computation.1 | async-start | bytes 1198080 | tf_op jit(solution)/shard_map/all_gather | solution.py:89
  8.8 55.6 %copy-start.4 = (s32[64]{0:T(128)S(1)}, s32[64]{0:T(128)}, u32[]{:S(2)}) copy-start(s32[64]{0:T(128)} %param.14) | copy-start | bytes 772
  8.8 57.5 %copy-start.3 = (s32[64]{0:T(128)S(1)}, s32[64]{0:T(128)}, u32[]{:S(2)}) copy-start(s32[64]{0:T(128)} %param.15) | copy-start | bytes 772
  8.8 23.4 %collective-permute-start.2 = (bf16[2,384,640]{2,1,0:T(8,128)(2,1)}, bf16[2,384,640]{2,1,0:T(8,128)(2,1)}, u32[]{:S(2)}, u32[]{:S(2)}) collective-permute-start(bf16[2,384,640]{2,1,0:T(8,128)(2,1)} %pad_maximum_fusion), channel_id=1, source_target_pairs={{0,48},{8,56},{16,0},{24,8},{32,16},{40,24},{48,32},{56,40},{64,11... | collective-permute-start | bytes 2949128 | tf_op jit(solution)/shard_map/ppermute | solution.py:33
  15.9 116.2 %all-gather.5.cloned.1.call-start = ((), (), s32[]{:S(2)}) async-start(), calls=%async_computation.2 | async-start | bytes 4915200 | tf_op jit(solution)/shard_map/all_gather | solution.py:91
  16.0 21.6 %collective-permute-start = (bf16[2,384,640]{2,1,0:T(8,128)(2,1)}, bf16[2,384,640]{2,1,0:T(8,128)(2,1)S(1)}, u32[]{:S(2)}, u32[]{:S(2)}) collective-permute-start(bf16[2,384,640]{2,1,0:T(8,128)(2,1)} %pad_maximum_fusion), channel_id=1, source_target_pairs={{0,16},{8,24},{16,32},{24,40},{32,48},{40,56},{48,64},{56,72},{64,... | collective-permute-start | bytes 2949128 | tf_op jit(solution)/shard_map/ppermute | solution.py:17
  32.2 22.4 %collective-permute-start.3 = (bf16[2,384,640]{2,1,0:T(8,128)(2,1)}, bf16[2,384,640]{2,1,0:T(8,128)(2,1)S(1)}, u32[]{:S(2)}, u32[]{:S(2)}) collective-permute-start(bf16[2,384,640]{2,1,0:T(8,128)(2,1)} %collective-permute-done.2), channel_id=1, source_target_pairs={{48,32},{56,40},{0,48},{8,56},{16,64},{24,72},{32,80},{40,88},{112... | collective-permute-start | bytes 2949128 | tf_op jit(solution)/shard_map/ppermute | solution.py:34
  37.6 39.9 %copy-start = (bf16[384,640]{1,0:T(8,128)(2,1)S(1)}, bf16[384,640]{1,0:T(8,128)(2,1)}, u32[]{:S(2)}) copy-start(bf16[384,640]{1,0:T(8,128)(2,1)} %param.9) | copy-start | bytes 1474564
  37.6 39.9 %copy-start.1 = (bf16[384,640]{1,0:T(8,128)(2,1)S(1)}, bf16[384,640]{1,0:T(8,128)(2,1)}, u32[]{:S(2)}) copy-start(bf16[384,640]{1,0:T(8,128)(2,1)} %param.10) | copy-start | bytes 1474564
  57.3 20.3 %collective-permute-start.1 = (bf16[2,384,640]{2,1,0:T(8,128)(2,1)}, bf16[2,384,640]{2,1,0:T(8,128)(2,1)}, u32[]{:S(2)}, u32[]{:S(2)}) collective-permute-start(bf16[2,384,640]{2,1,0:T(8,128)(2,1)} %get-tuple-element.65), channel_id=1, source_target_pairs={{0,8},{8,0},{1,9},{9,1},{2,10},{10,2},{3,11},{11,3},{4,12},{12,4},... | collective-permute-start | bytes 2949128 | tf_op jit(solution)/shard_map/ppermute | solution.py:38
  69.8 139.5 %reduce-scatter.2.cloned.1.call-start = ((), (), s32[]{:S(2)}) async-start(), calls=%async_computation.3 | async-start | bytes 4423680 | tf_op jit(solution)/shard_map/reduce_scatter | solution.py:124
  72.9 6.3 %collective-permute-start.4 = (bf16[2,384,640]{2,1,0:T(8,128)(2,1)}, bf16[2,384,640]{2,1,0:T(8,128)(2,1)}, u32[]{:S(2)}, u32[]{:S(2)}) collective-permute-start(bf16[2,384,640]{2,1,0:T(8,128)(2,1)} %get-tuple-element.64), channel_id=1, source_target_pairs={{0,8},{8,0},{1,9},{9,1},{2,10},{10,2},{3,11},{11,3},{4,12},{12,4},... | collective-permute-start | bytes 2949128 | tf_op jit(solution)/shard_map/ppermute | solution.py:38
  79.0 1.7 copy-start.2
  133.4 6.9 %collective-permute-start.6 = (bf16[640,32,16]{0,2,1:T(8,128)(2,1)S(1)}, bf16[640,32,16]{0,2,1:T(8,128)(2,1)S(1)}, u32[]{:S(2)}, u32[]{:S(2)}) collective-permute-start(bf16[640,32,16]{0,2,1:T(8,128)(2,1)S(1)} %get-tuple-element.53), channel_id=1, source_target_pairs={{0,8},{8,0},{1,9},{9,1},{2,10},{10,2},{3,11},{11,3},{4,12},{12,4},... | collective-permute-start | bytes 1966088 | tf_op jit(solution)/shard_map/ppermute | solution.py:38
  138.2 7.7 %collective-permute-start.5 = (bf16[640,32,80]{0,2,1:T(8,128)(2,1)S(1)}, bf16[640,32,80]{0,2,1:T(8,128)(2,1)S(1)}, u32[]{:S(2)}, u32[]{:S(2)}) collective-permute-start(bf16[640,32,80]{0,2,1:T(8,128)(2,1)S(1)} %slice.216), channel_id=1, source_target_pairs={{0,8},{8,0},{1,9},{9,1},{2,10},{10,2},{3,11},{11,3},{4,12},{12,4},... | collective-permute-start | bytes 9830408 | tf_op jit(solution)/shard_map/ppermute | solution.py:38
Sparse Core Ops, SparseCore 0:
  16.1 39.8 all-gather.2
  70.0 62.1 all-gather.4
  153.1 56.1 reduce-scatter.1

commit v12 on v8

--- a/solution.py
+++ b/solution.py
@@ -48,6 +48,13 @@
     core = lax.axis_index("c")
     first_core = core == 0
 
+    chips = lax.axis_size(CHIP_AXES)
+    block = out_weight.shape[1]
+    tokens = text_keys.shape[0]
+    spare = jnp.zeros((width, GATHER_SPARE), out_weight.dtype)
+    packed = jnp.concatenate([out_weight, text_keys.T, text_values.T, spare], axis=1)
+    packed, keys, values = lax.optimization_barrier((packed, keys, values))
+    packed = lax.all_gather(lax.all_gather(packed, "y", axis=1, tiled=True), "x", axis=1, tiled=True)
     own = jnp.stack([keys, values])
     back2 = shift_frames(own, 2)
     back4 = relay_back(own, 2)
@@ -81,12 +88,6 @@
                         preferred_element_type=jnp.float32)
         frame_parts.append((top_f, total_f, acc_f))
 
-    chips = lax.axis_size(CHIP_AXES)
-    block = out_weight.shape[1]
-    tokens = text_keys.shape[0]
-    spare = jnp.zeros((width, GATHER_SPARE), out_weight.dtype)
-    packed = jnp.concatenate([out_weight, text_keys.T, text_values.T, spare], axis=1)
-    packed = lax.all_gather(lax.all_gather(packed, "y", axis=1, tiled=True), "x", axis=1, tiled=True)
     packed, frame_parts = lax.optimization_barrier((packed, frame_parts))
     packed = packed.reshape(width, chips, -1)
     text_own = packed[:, :, block : block + 2 * tokens]

time: 203 us -> 203 us (level)
  transfers between devices with their start and end apart: 10 -> 10, of which waited for: 5 -> 6; matrix products, arithmetic and copies ran while one was open for 14% -> 13% of each run, Pallas kernels for 0% -> 0%
where the time goes in v12:
time: 203 us
  waiting for transfers between devices  119 us (59%)
  starting transfers between devices  25.6 us (13%)
  between operations  16.7 us (8%)
  matrix products  14.5 us (7%)
  other arithmetic  13.8 us (7%)
  local copies, waits for them, and re-layouts  13.2 us (7%)
    reduce_scatter x1, waiting for transfers between devices, on_device(): lax.psum_scatter(partial_out.astype(jnp.bfloat16), 'head', scatter_dimens...  56.4 us
    all_gather x1, waiting for transfers between devices, on_device(): lax.all_gather(lax.all_gather(packed, 'y', axis=1, tiled=True), 'x', axis...  27.8 us
    ppermute x1, waiting for transfers between devices, relay_back(): hop = lax.ppermute(value, FRAME_AXES, first)  16.6 us
    all_gather x1, waiting for transfers between devices, on_device(): lax.all_gather(packed, 'y', axis=1, tiled=True)  16.6 us
    ppermute x4, starting transfers between devices, swap_cores(): return lax.ppermute(value, 'c', [(0, 1), (1, 0)])  13.6 us
    ppermute x1, starting transfers between devices, relay_back(): return lax.ppermute(hop, FRAME_AXES, second)  5.36 us
    ppermute x1, starting transfers between devices, relay_back(): hop = lax.ppermute(value, FRAME_AXES, first)  5.21 us
    dot_general x1, matrix products, on_device(): jnp.einsum('rk,ckxyn->yrcxn', attended_all, w5, preferred_element_type=jn...  4.52 us
  transfers between devices with their start and end apart: 10, of which 6 were waited for; matrix products, arithmetic and copies ran while one was open for 13% of the time, Pallas kernels for 0%

profile of v12, /device:TPU:1, one launch (start us, length us, event | category | flops | bytes accessed | tf_op | source)
XLA Modules:
  0.0 202.5 jit_solution(1458209897267036796)
XLA Ops:
  6.6 1.7 maximum_maximum_fusion
  8.4 2.3 %pad_maximum_fusion = bf16[2,384,640]{2,1,0:T(8,128)(2,1)} fusion(bf16[1,384,640]{2,1,0:T(8,128)(2,1)} %bitcast.91, bf16[1,384,640]{2,1,0:T(8,128)(2,1)} %bitcast.89), kind=kLoop, calls=%fused_computation.72 | loop fusion | flops 491520 | bytes 1966080 | tf_op jit(solution)/shard_map/stack | solution.py:58
  10.6 5.2 %collective-permute-start.2 = (bf16[2,384,640]{2,1,0:T(8,128)(2,1)}, bf16[2,384,640]{2,1,0:T(8,128)(2,1)}, u32[]{:S(2)}, u32[]{:S(2)}) collective-permute-start(bf16[2,384,640]{2,1,0:T(8,128)(2,1)} %pad_maximum_fusion), channel_id=1, source_target_pairs={{0,48},{8,56},{16,0},{24,8},{32,16},{40,24},{48,32},{56,40},{64,11... | collective-permute-start | bytes 2949128 | tf_op jit(solution)/shard_map/ppermute | solution.py:33
  15.9 1.4 collective-permute-start
  17.3 16.6 %collective-permute-done.2 = bf16[2,384,640]{2,1,0:T(8,128)(2,1)} collective-permute-done((bf16[2,384,640]{2,1,0:T(8,128)(2,1)}, bf16[2,384,640]{2,1,0:T(8,128)(2,1)}, u32[]{:S(2)}, u32[]{:S(2)}) %collective-permute-start.2) | collective-permute-done | bytes 983072 | tf_op jit(solution)/shard_map/ppermute | solution.py:33
  33.9 5.4 %collective-permute-start.3 = (bf16[2,384,640]{2,1,0:T(8,128)(2,1)}, bf16[2,384,640]{2,1,0:T(8,128)(2,1)S(1)}, u32[]{:S(2)}, u32[]{:S(2)}) collective-permute-start(bf16[2,384,640]{2,1,0:T(8,128)(2,1)} %collective-permute-done.2), channel_id=1, source_target_pairs={{48,32},{56,40},{0,48},{8,56},{16,64},{24,72},{32,80},{40,88},{112... | collective-permute-start | bytes 2949128 | tf_op jit(solution)/shard_map/ppermute | solution.py:34
  39.3 16.6 %all-gather.3.cloned.1.call-done = bf16[640,832]{0,1:T(8,128)(2,1)} async-done(((bf16[640,104]{0,1:T(8,128)(2,1)}), bf16[640,832]{0,1:T(8,128)(2,1)}) %all-gather.3.cloned.1.call-update) | async-done | bytes 1064976 | tf_op jit(solution)/shard_map/all_gather | solution.py:57
  56.3 1.5 broadcast_select_fusion
  57.9 7.0 %collective-permute-start.1 = (bf16[2,384,640]{2,1,0:T(8,128)(2,1)}, bf16[2,384,640]{2,1,0:T(8,128)(2,1)}, u32[]{:S(2)}, u32[]{:S(2)}) collective-permute-start(bf16[2,384,640]{2,1,0:T(8,128)(2,1)} %get-tuple-element.71), channel_id=1, source_target_pairs={{0,8},{8,0},{1,9},{9,1},{2,10},{10,2},{3,11},{11,3},{4,12},{12,4},... | collective-permute-start | bytes 2949128 | tf_op jit(solution)/shard_map/ppermute | solution.py:38
  65.0 0.6 dynamic_slice.18
  68.8 0.7 fusion.137
  69.5 0.6 fusion.109
  70.4 0.7 fusion.110
  71.3 1.9 collective-permute-start.4
  73.3 0.6 fusion.111
  74.1 0.7 fusion.112
  75.1 0.7 fusion.113
  76.1 1.4 fusion.82
  77.7 1.4 fusion.80
  79.3 0.7 fusion.142
  80.0 0.5 fusion.18
  80.6 0.7 fusion.141
  81.3 0.5 fusion.16
  81.8 0.7 fusion.140
  82.5 0.5 fusion.14
  83.1 0.7 fusion.139
  83.8 0.5 fusion.12
  84.3 0.7 fusion.138
  85.0 0.5 fusion.10
  85.5 0.6 fusion.21
  86.2 0.6 fusion.23
  86.8 0.6 fusion.25
  87.4 0.6 fusion.27
  88.0 0.6 fusion.29
  88.6 27.8 %all-gather.5.cloned.1.call-done = bf16[640,3328]{0,1:T(8,128)(2,1)} async-done(((bf16[640,832]{0,1:T(8,128)(2,1)}), bf16[640,3328]{0,1:T(8,128)(2,1)}) %all-gather.5.cloned.1.call-update) | async-done | bytes 4259856 | tf_op jit(solution)/shard_map/all_gather | solution.py:57
  116.4 1.2 slice_bitcast_fusion.8
  117.6 2.6 %collective-permute-start.6 = (bf16[640,32,16]{0,2,1:T(8,128)(2,1)S(1)}, bf16[640,32,16]{0,2,1:T(8,128)(2,1)S(1)}, u32[]{:S(2)}, u32[]{:S(2)}) collective-permute-start(bf16[640,32,16]{0,2,1:T(8,128)(2,1)S(1)} %get-tuple-element.59), channel_id=1, source_target_pairs={{0,8},{8,0},{1,9},{9,1},{2,10},{10,2},{3,11},{11,3},{4,12},{12,4},... | collective-permute-start | bytes 1966088 | tf_op jit(solution)/shard_map/ppermute | solution.py:38
  120.2 2.2 %slice.211 = bf16[640,32,80]{0,2,1:T(8,128)(2,1)S(1)} slice(bf16[640,32,104]{0,2,1:T(8,128)(2,1)} %bitcast.94), slice={[0:640], [0:32], [0:80]} | slice | bytes 6553600 | tf_op jit(solution)/shard_map/slice | solution.py:97
  122.4 2.1 %collective-permute-start.5 = (bf16[640,32,80]{0,2,1:T(8,128)(2,1)S(1)}, bf16[640,32,80]{0,2,1:T(8,128)(2,1)S(1)}, u32[]{:S(2)}, u32[]{:S(2)}) collective-permute-start(bf16[640,32,80]{0,2,1:T(8,128)(2,1)S(1)} %slice.211), channel_id=1, source_target_pairs={{0,8},{8,0},{1,9},{9,1},{2,10},{10,2},{3,11},{11,3},{4,12},{12,4},... | collective-permute-start | bytes 9830408 | tf_op jit(solution)/shard_map/ppermute | solution.py:38
  128.1 0.4 fusion.51
  128.5 0.4 fusion.53
  128.9 0.4 fusion.55
  129.3 0.8 collective-permute-done.5
  130.1 4.5 %convert_bitcast_fusion = bf16[8,384,2,4,80]{1,4,0,3,2:T(8,128)(2,1)S(1)} fusion(bf16[1,640,4,8,80]{1,4,3,2,0:T(8,128)(2,1)S(1)} %bitcast.111, bf16[1,640,4,8,80]{1,4,3,2,0:T(8,128)(2,1)S(1)} %bitcast.95, bf16[384,640]{1,0:T(8,128)(2,1)S(1)} %fusion.55), kind=kOutput, calls=%fused_computation.4 | convolution fusion | flops 2521825280 | bytes 10977280 | tf_op jit(solution)/shard_map/rk,ckxyn->yrcxn/dot_general | solution.py:121
  134.7 2.5 %copy.9 = bf16[8,384,2,4,80]{1,4,3,2,0:T(8,128)(2,1)} copy(bf16[8,384,2,4,80]{1,4,0,3,2:T(8,128)(2,1)S(1)} %convert_bitcast_fusion) | data formatting | bytes 7864320 | tf_op jit(solution)/shard_map/convert_element_type | solution.py:123
  137.2 56.4 %reduce-scatter.2.cloned.1.call-done = bf16[1,384,640]{1,2,0:T(8,128)(2,1)} async-done(((bf16[8,384,640]{1,2,0:T(8,128)(2,1)}), bf16[1,384,640]{1,2,0:T(8,128)(2,1)}) %reduce-scatter.2.cloned.1.call-update) | async-done | bytes 491536 | tf_op jit(solution)/shard_map/reduce_scatter | solution.py:123
  193.6 1.4 fusion.69
  195.0 1.0 copy.11
  (63 shorter events, 5.9 us)
Async XLA Ops:
  6.5 49.8 %copy-start.1 = (bf16[384,640]{1,0:T(8,128)(2,1)S(1)}, bf16[384,640]{1,0:T(8,128)(2,1)}, u32[]{:S(2)}) copy-start(bf16[384,640]{1,0:T(8,128)(2,1)} %param.10) | copy-start | bytes 1474564
  6.5 49.8 %copy-start = (bf16[384,640]{1,0:T(8,128)(2,1)S(1)}, bf16[384,640]{1,0:T(8,128)(2,1)}, u32[]{:S(2)}) copy-start(bf16[384,640]{1,0:T(8,128)(2,1)} %param.9) | copy-start | bytes 1474564
  6.5 49.3 %all-gather.3.cloned.1.call-start = ((), (), s32[]{:S(2)}) async-start(), calls=%async_computation.1 | async-start | bytes 1198080 | tf_op jit(solution)/shard_map/all_gather | solution.py:57
  10.6 23.3 %collective-permute-start.2 = (bf16[2,384,640]{2,1,0:T(8,128)(2,1)}, bf16[2,384,640]{2,1,0:T(8,128)(2,1)}, u32[]{:S(2)}, u32[]{:S(2)}) collective-permute-start(bf16[2,384,640]{2,1,0:T(8,128)(2,1)} %pad_maximum_fusion), channel_id=1, source_target_pairs={{0,48},{8,56},{16,0},{24,8},{32,16},{40,24},{48,32},{56,40},{64,11... | collective-permute-start | bytes 2949128 | tf_op jit(solution)/shard_map/ppermute | solution.py:33
  15.9 100.5 %all-gather.5.cloned.1.call-start = ((), (), s32[]{:S(2)}) async-start(), calls=%async_computation.2 | async-start | bytes 5324800 | tf_op jit(solution)/shard_map/all_gather | solution.py:57
  15.9 40.0 %collective-permute-start = (bf16[2,384,640]{2,1,0:T(8,128)(2,1)}, bf16[2,384,640]{2,1,0:T(8,128)(2,1)S(1)}, u32[]{:S(2)}, u32[]{:S(2)}) collective-permute-start(bf16[2,384,640]{2,1,0:T(8,128)(2,1)} %pad_maximum_fusion), channel_id=1, source_target_pairs={{0,16},{8,24},{16,32},{24,40},{32,48},{40,56},{48,64},{56,72},{64,... | collective-permute-start | bytes 2949128 | tf_op jit(solution)/shard_map/ppermute | solution.py:17
  33.9 22.4 %collective-permute-start.3 = (bf16[2,384,640]{2,1,0:T(8,128)(2,1)}, bf16[2,384,640]{2,1,0:T(8,128)(2,1)S(1)}, u32[]{:S(2)}, u32[]{:S(2)}) collective-permute-start(bf16[2,384,640]{2,1,0:T(8,128)(2,1)} %collective-permute-done.2), channel_id=1, source_target_pairs={{48,32},{56,40},{0,48},{8,56},{16,64},{24,72},{32,80},{40,88},{112... | collective-permute-start | bytes 2949128 | tf_op jit(solution)/shard_map/ppermute | solution.py:34
  55.8 9.1 %copy-start.4 = (s32[64]{0:T(128)S(1)}, s32[64]{0:T(128)}, u32[]{:S(2)}) copy-start(s32[64]{0:T(128)} %param.14) | copy-start | bytes 772
  55.8 13.0 %copy-start.3 = (s32[64]{0:T(128)S(1)}, s32[64]{0:T(128)}, u32[]{:S(2)}) copy-start(s32[64]{0:T(128)} %param.15) | copy-start | bytes 772
  55.9 137.7 %reduce-scatter.2.cloned.1.call-start = ((), (), s32[]{:S(2)}) async-start(), calls=%async_computation.3 | async-start | bytes 4423680 | tf_op jit(solution)/shard_map/reduce_scatter | solution.py:123
  57.9 18.2 %collective-permute-start.1 = (bf16[2,384,640]{2,1,0:T(8,128)(2,1)}, bf16[2,384,640]{2,1,0:T(8,128)(2,1)}, u32[]{:S(2)}, u32[]{:S(2)}) collective-permute-start(bf16[2,384,640]{2,1,0:T(8,128)(2,1)} %get-tuple-element.71), channel_id=1, source_target_pairs={{0,8},{8,0},{1,9},{9,1},{2,10},{10,2},{3,11},{11,3},{4,12},{12,4},... | collective-permute-start | bytes 2949128 | tf_op jit(solution)/shard_map/ppermute | solution.py:38
  71.3 6.4 %collective-permute-start.4 = (bf16[2,384,640]{2,1,0:T(8,128)(2,1)}, bf16[2,384,640]{2,1,0:T(8,128)(2,1)}, u32[]{:S(2)}, u32[]{:S(2)}) collective-permute-start(bf16[2,384,640]{2,1,0:T(8,128)(2,1)} %get-tuple-element.70), channel_id=1, source_target_pairs={{0,8},{8,0},{1,9},{9,1},{2,10},{10,2},{3,11},{11,3},{4,12},{12,4},... | collective-permute-start | bytes 2949128 | tf_op jit(solution)/shard_map/ppermute | solution.py:38
  77.5 1.8 copy-start.2
  117.6 6.9 %collective-permute-start.6 = (bf16[640,32,16]{0,2,1:T(8,128)(2,1)S(1)}, bf16[640,32,16]{0,2,1:T(8,128)(2,1)S(1)}, u32[]{:S(2)}, u32[]{:S(2)}) collective-permute-start(bf16[640,32,16]{0,2,1:T(8,128)(2,1)S(1)} %get-tuple-element.59), channel_id=1, source_target_pairs={{0,8},{8,0},{1,9},{9,1},{2,10},{10,2},{3,11},{11,3},{4,12},{12,4},... | collective-permute-start | bytes 1966088 | tf_op jit(solution)/shard_map/ppermute | solution.py:38
  122.4 7.7 %collective-permute-start.5 = (bf16[640,32,80]{0,2,1:T(8,128)(2,1)S(1)}, bf16[640,32,80]{0,2,1:T(8,128)(2,1)S(1)}, u32[]{:S(2)}, u32[]{:S(2)}) collective-permute-start(bf16[640,32,80]{0,2,1:T(8,128)(2,1)S(1)} %slice.211), channel_id=1, source_target_pairs={{0,8},{8,0},{1,9},{9,1},{2,10},{10,2},{3,11},{11,3},{4,12},{12,4},... | collective-permute-start | bytes 9830408 | tf_op jit(solution)/shard_map/ppermute | solution.py:38
Sparse Core Ops, SparseCore 0:
  16.0 39.8 all-gather.2
  57.9 58.4 all-gather.4
  137.3 56.2 reduce-scatter.1

commit v13 on v12

--- a/solution.py
+++ b/solution.py
@@ -95,7 +95,8 @@
     text_kt = text_pair[:, :, :, :tokens].transpose(1, 0, 2, 3).reshape(width, -1)
     text_vt = text_pair[:, :, :, tokens:].transpose(1, 0, 2, 3).reshape(width, -1)
     weight_own = packed[:, :, :block]
-    weight_pair = jnp.stack([weight_own, swap_cores(weight_own)])
+    weight_other = swap_cores(weight_own)
+    weight_pair = jnp.where(first_core, jnp.stack([weight_own, weight_other]), jnp.stack([weight_other, weight_own]))
 
     head_outputs = []
     for head_index in range(local_heads):
@@ -122,7 +123,6 @@
     partial_out = partial_out.reshape(groups, rows, -1)
     mixed = lax.psum_scatter(partial_out.astype(jnp.bfloat16), "head", scatter_dimension=0, tiled=True)
     mixed = mixed.reshape(rows, 2, xs, block)
-    mixed = jnp.where(first_core, mixed, mixed[:, ::-1])
     return mixed.transpose(0, 2, 1, 3).reshape(rows, -1)
 
 

time: 203 us -> 203 us (level)
  no operation moved by 1% of the time
where the time goes in v13:
time: 203 us; the launch traced here: 202 us
  waiting for transfers between devices  119 us (59%)
  starting transfers between devices  25.6 us (13%)
  between operations  16.7 us (8%)
  matrix products  14.7 us (7%)
  local copies, waits for them, and re-layouts  14.2 us (7%)
  other arithmetic  12.5 us (6%)
    reduce_scatter x1, waiting for transfers between devices, on_device(): lax.psum_scatter(partial_out.astype(jnp.bfloat16), 'head', scatter_dimens...  56.4 us
    all_gather x1, waiting for transfers between devices, on_device(): lax.all_gather(lax.all_gather(packed, 'y', axis=1, tiled=True), 'x', axis...  27.8 us
    ppermute x1, waiting for transfers between devices, relay_back(): hop = lax.ppermute(value, FRAME_AXES, first)  16.6 us
    all_gather x1, waiting for transfers between devices, on_device(): lax.all_gather(packed, 'y', axis=1, tiled=True)  16.6 us
    ppermute x4, starting transfers between devices, swap_cores(): return lax.ppermute(value, 'c', [(0, 1), (1, 0)])  13.6 us
    ppermute x1, starting transfers between devices, relay_back(): return lax.ppermute(hop, FRAME_AXES, second)  5.36 us
    ppermute x1, starting transfers between devices, relay_back(): hop = lax.ppermute(value, FRAME_AXES, first)  5.21 us
    dot_general x1, matrix products, on_device(): jnp.einsum('rk,ckxyn->yrcxn', attended_all, w5, preferred_element_type=jn...  4.72 us
  transfers between devices with their start and end apart: 10, of which 6 were waited for; matrix products, arithmetic and copies ran while one was open for 13% of the time, Pallas kernels for 0%

profile of v13, /device:TPU:1, one launch (start us, length us, event | category | flops | bytes accessed | tf_op | source)
XLA Modules:
  0.0 202.4 jit_solution(5313471305251070740)
XLA Ops:
  6.6 1.7 maximum_maximum_fusion
  8.4 2.3 %pad_maximum_fusion = bf16[2,384,640]{2,1,0:T(8,128)(2,1)} fusion(bf16[1,384,640]{2,1,0:T(8,128)(2,1)} %bitcast.91, bf16[1,384,640]{2,1,0:T(8,128)(2,1)} %bitcast.89), kind=kLoop, calls=%fused_computation.76 | loop fusion | flops 491520 | bytes 1966080 | tf_op jit(solution)/shard_map/stack | solution.py:58
  10.6 5.2 %collective-permute-start.2 = (bf16[2,384,640]{2,1,0:T(8,128)(2,1)}, bf16[2,384,640]{2,1,0:T(8,128)(2,1)}, u32[]{:S(2)}, u32[]{:S(2)}) collective-permute-start(bf16[2,384,640]{2,1,0:T(8,128)(2,1)} %pad_maximum_fusion), channel_id=1, source_target_pairs={{0,48},{8,56},{16,0},{24,8},{32,16},{40,24},{48,32},{56,40},{64,11... | collective-permute-start | bytes 2949128 | tf_op jit(solution)/shard_map/ppermute | solution.py:33
  15.9 1.4 collective-permute-start
  17.3 16.6 %collective-permute-done.2 = bf16[2,384,640]{2,1,0:T(8,128)(2,1)} collective-permute-done((bf16[2,384,640]{2,1,0:T(8,128)(2,1)}, bf16[2,384,640]{2,1,0:T(8,128)(2,1)}, u32[]{:S(2)}, u32[]{:S(2)}) %collective-permute-start.2) | collective-permute-done | bytes 983072 | tf_op jit(solution)/shard_map/ppermute | solution.py:33
  33.9 5.4 %collective-permute-start.3 = (bf16[2,384,640]{2,1,0:T(8,128)(2,1)}, bf16[2,384,640]{2,1,0:T(8,128)(2,1)S(1)}, u32[]{:S(2)}, u32[]{:S(2)}) collective-permute-start(bf16[2,384,640]{2,1,0:T(8,128)(2,1)} %collective-permute-done.2), channel_id=1, source_target_pairs={{48,32},{56,40},{0,48},{8,56},{16,64},{24,72},{32,80},{40,88},{112... | collective-permute-start | bytes 2949128 | tf_op jit(solution)/shard_map/ppermute | solution.py:34
  39.3 16.6 %all-gather.3.cloned.1.call-done = bf16[640,832]{0,1:T(8,128)(2,1)} async-done(((bf16[640,104]{0,1:T(8,128)(2,1)}), bf16[640,832]{0,1:T(8,128)(2,1)}) %all-gather.3.cloned.1.call-update) | async-done | bytes 1064976 | tf_op jit(solution)/shard_map/all_gather | solution.py:57
  56.3 1.5 broadcast_select_fusion
  57.9 7.0 %collective-permute-start.1 = (bf16[2,384,640]{2,1,0:T(8,128)(2,1)}, bf16[2,384,640]{2,1,0:T(8,128)(2,1)}, u32[]{:S(2)}, u32[]{:S(2)}) collective-permute-start(bf16[2,384,640]{2,1,0:T(8,128)(2,1)} %get-tuple-element.71), channel_id=1, source_target_pairs={{0,8},{8,0},{1,9},{9,1},{2,10},{10,2},{3,11},{11,3},{4,12},{12,4},... | collective-permute-start | bytes 2949128 | tf_op jit(solution)/shard_map/ppermute | solution.py:38
  65.0 0.6 dynamic_slice.18
  68.8 0.7 fusion.137
  69.5 0.6 fusion.109
  70.4 0.7 fusion.110
  71.3 1.9 collective-permute-start.4
  73.3 0.6 fusion.111
  74.1 0.7 fusion.112
  75.1 0.7 fusion.113
  76.1 1.4 fusion.82
  77.7 1.4 fusion.80
  79.3 0.7 fusion.142
  80.0 0.5 fusion.21
  80.6 0.7 fusion.141
  81.3 0.5 fusion.19
  81.8 0.7 fusion.140
  82.5 0.5 fusion.17
  83.1 0.7 fusion.139
  83.8 0.5 fusion.15
  84.3 0.7 fusion.138
  85.0 0.5 fusion.13
  85.5 0.6 fusion.22
  86.2 0.6 fusion.24
  86.8 0.6 fusion.26
  87.4 0.6 fusion.28
  88.0 0.6 fusion.30
  88.6 27.8 %all-gather.5.cloned.1.call-done = bf16[640,3328]{0,1:T(8,128)(2,1)} async-done(((bf16[640,832]{0,1:T(8,128)(2,1)}), bf16[640,3328]{0,1:T(8,128)(2,1)}) %all-gather.5.cloned.1.call-update) | async-done | bytes 4259856 | tf_op jit(solution)/shard_map/all_gather | solution.py:57
  116.4 1.2 slice_bitcast_fusion.8
  117.6 2.6 %collective-permute-start.6 = (bf16[640,32,16]{0,2,1:T(8,128)(2,1)S(1)}, bf16[640,32,16]{0,2,1:T(8,128)(2,1)S(1)}, u32[]{:S(2)}, u32[]{:S(2)}) collective-permute-start(bf16[640,32,16]{0,2,1:T(8,128)(2,1)S(1)} %get-tuple-element.59), channel_id=1, source_target_pairs={{0,8},{8,0},{1,9},{9,1},{2,10},{10,2},{3,11},{11,3},{4,12},{12,4},... | collective-permute-start | bytes 1966088 | tf_op jit(solution)/shard_map/ppermute | solution.py:38
  120.2 2.2 %slice.211 = bf16[640,32,80]{0,2,1:T(8,128)(2,1)S(1)} slice(bf16[640,32,104]{0,2,1:T(8,128)(2,1)} %bitcast.94), slice={[0:640], [0:32], [0:80]} | slice | bytes 6553600 | tf_op jit(solution)/shard_map/slice | solution.py:97
  122.4 2.1 %collective-permute-start.5 = (bf16[640,32,80]{0,2,1:T(8,128)(2,1)S(1)}, bf16[640,32,80]{0,2,1:T(8,128)(2,1)S(1)}, u32[]{:S(2)}, u32[]{:S(2)}) collective-permute-start(bf16[640,32,80]{0,2,1:T(8,128)(2,1)S(1)} %slice.211), channel_id=1, source_target_pairs={{0,8},{8,0},{1,9},{9,1},{2,10},{10,2},{3,11},{11,3},{4,12},{12,4},... | collective-permute-start | bytes 9830408 | tf_op jit(solution)/shard_map/ppermute | solution.py:38
  128.1 0.4 fusion.52
  128.5 0.4 fusion.54
  128.9 0.4 fusion.56
  129.3 0.8 collective-permute-done.5
  130.1 4.7 %convert_bitcast_fusion = bf16[8,384,2,4,80]{1,4,0,3,2:T(8,128)(2,1)S(1)} fusion(bf16[1,640,4,8,80]{1,4,3,2,0:T(8,128)(2,1)S(1)} %bitcast.111, bf16[1,640,4,8,80]{1,4,3,2,0:T(8,128)(2,1)S(1)} %bitcast.95, pred[]{:T(512)S(6)} %eq.3, bf16[384,640]{1,0:T(8,128)(2,1)S(1)} %fusion.56), kind=kOutput, calls=%fused_computation.8 | convolution fusion | flops 2528378880 | bytes 10977281 | tf_op jit(solution)/shard_map/rk,ckxyn->yrcxn/dot_general | solution.py:122
  134.9 2.5 %copy.9 = bf16[8,384,2,4,80]{1,4,3,2,0:T(8,128)(2,1)} copy(bf16[8,384,2,4,80]{1,4,0,3,2:T(8,128)(2,1)S(1)} %convert_bitcast_fusion) | data formatting | bytes 7864320 | tf_op jit(solution)/shard_map/convert_element_type | solution.py:124
  137.4 56.4 %reduce-scatter.2.cloned.1.call-done = bf16[1,384,640]{1,2,0:T(8,128)(2,1)} async-done(((bf16[8,384,640]{1,2,0:T(8,128)(2,1)}), bf16[1,384,640]{1,2,0:T(8,128)(2,1)}) %reduce-scatter.2.cloned.1.call-update) | async-done | bytes 491536 | tf_op jit(solution)/shard_map/reduce_scatter | solution.py:124
  193.8 1.1 copy.10
  194.9 1.0 copy.11
  (62 shorter events, 5.9 us)
Async XLA Ops:
  6.5 49.8 %copy-start.1 = (bf16[384,640]{1,0:T(8,128)(2,1)S(1)}, bf16[384,640]{1,0:T(8,128)(2,1)}, u32[]{:S(2)}) copy-start(bf16[384,640]{1,0:T(8,128)(2,1)} %param.10) | copy-start | bytes 1474564
  6.5 49.8 %copy-start = (bf16[384,640]{1,0:T(8,128)(2,1)S(1)}, bf16[384,640]{1,0:T(8,128)(2,1)}, u32[]{:S(2)}) copy-start(bf16[384,640]{1,0:T(8,128)(2,1)} %param.9) | copy-start | bytes 1474564
  6.5 49.3 %all-gather.3.cloned.1.call-start = ((), (), s32[]{:S(2)}) async-start(), calls=%async_computation.1 | async-start | bytes 1198080 | tf_op jit(solution)/shard_map/all_gather | solution.py:57
  10.6 23.3 %collective-permute-start.2 = (bf16[2,384,640]{2,1,0:T(8,128)(2,1)}, bf16[2,384,640]{2,1,0:T(8,128)(2,1)}, u32[]{:S(2)}, u32[]{:S(2)}) collective-permute-start(bf16[2,384,640]{2,1,0:T(8,128)(2,1)} %pad_maximum_fusion), channel_id=1, source_target_pairs={{0,48},{8,56},{16,0},{24,8},{32,16},{40,24},{48,32},{56,40},{64,11... | collective-permute-start | bytes 2949128 | tf_op jit(solution)/shard_map/ppermute | solution.py:33
  15.9 100.5 %all-gather.5.cloned.1.call-start = ((), (), s32[]{:S(2)}) async-start(), calls=%async_computation.2 | async-start | bytes 5324800 | tf_op jit(solution)/shard_map/all_gather | solution.py:57
  15.9 40.0 %collective-permute-start = (bf16[2,384,640]{2,1,0:T(8,128)(2,1)}, bf16[2,384,640]{2,1,0:T(8,128)(2,1)S(1)}, u32[]{:S(2)}, u32[]{:S(2)}) collective-permute-start(bf16[2,384,640]{2,1,0:T(8,128)(2,1)} %pad_maximum_fusion), channel_id=1, source_target_pairs={{0,16},{8,24},{16,32},{24,40},{32,48},{40,56},{48,64},{56,72},{64,... | collective-permute-start | bytes 2949128 | tf_op jit(solution)/shard_map/ppermute | solution.py:17
  33.9 22.4 %collective-permute-start.3 = (bf16[2,384,640]{2,1,0:T(8,128)(2,1)}, bf16[2,384,640]{2,1,0:T(8,128)(2,1)S(1)}, u32[]{:S(2)}, u32[]{:S(2)}) collective-permute-start(bf16[2,384,640]{2,1,0:T(8,128)(2,1)} %collective-permute-done.2), channel_id=1, source_target_pairs={{48,32},{56,40},{0,48},{8,56},{16,64},{24,72},{32,80},{40,88},{112... | collective-permute-start | bytes 2949128 | tf_op jit(solution)/shard_map/ppermute | solution.py:34
  55.8 9.1 %copy-start.4 = (s32[64]{0:T(128)S(1)}, s32[64]{0:T(128)}, u32[]{:S(2)}) copy-start(s32[64]{0:T(128)} %param.14) | copy-start | bytes 772
  55.8 13.0 %copy-start.3 = (s32[64]{0:T(128)S(1)}, s32[64]{0:T(128)}, u32[]{:S(2)}) copy-start(s32[64]{0:T(128)} %param.15) | copy-start | bytes 772
  55.9 137.9 %reduce-scatter.2.cloned.1.call-start = ((), (), s32[]{:S(2)}) async-start(), calls=%async_computation.3 | async-start | bytes 4423680 | tf_op jit(solution)/shard_map/reduce_scatter | solution.py:124
  57.9 18.2 %collective-permute-start.1 = (bf16[2,384,640]{2,1,0:T(8,128)(2,1)}, bf16[2,384,640]{2,1,0:T(8,128)(2,1)}, u32[]{:S(2)}, u32[]{:S(2)}) collective-permute-start(bf16[2,384,640]{2,1,0:T(8,128)(2,1)} %get-tuple-element.71), channel_id=1, source_target_pairs={{0,8},{8,0},{1,9},{9,1},{2,10},{10,2},{3,11},{11,3},{4,12},{12,4},... | collective-permute-start | bytes 2949128 | tf_op jit(solution)/shard_map/ppermute | solution.py:38
  71.3 6.4 %collective-permute-start.4 = (bf16[2,384,640]{2,1,0:T(8,128)(2,1)}, bf16[2,384,640]{2,1,0:T(8,128)(2,1)}, u32[]{:S(2)}, u32[]{:S(2)}) collective-permute-start(bf16[2,384,640]{2,1,0:T(8,128)(2,1)} %get-tuple-element.70), channel_id=1, source_target_pairs={{0,8},{8,0},{1,9},{9,1},{2,10},{10,2},{3,11},{11,3},{4,12},{12,4},... | collective-permute-start | bytes 2949128 | tf_op jit(solution)/shard_map/ppermute | solution.py:38
  77.5 1.8 copy-start.2
  117.6 6.9 %collective-permute-start.6 = (bf16[640,32,16]{0,2,1:T(8,128)(2,1)S(1)}, bf16[640,32,16]{0,2,1:T(8,128)(2,1)S(1)}, u32[]{:S(2)}, u32[]{:S(2)}) collective-permute-start(bf16[640,32,16]{0,2,1:T(8,128)(2,1)S(1)} %get-tuple-element.59), channel_id=1, source_target_pairs={{0,8},{8,0},{1,9},{9,1},{2,10},{10,2},{3,11},{11,3},{4,12},{12,4},... | collective-permute-start | bytes 1966088 | tf_op jit(solution)/shard_map/ppermute | solution.py:38
  122.4 7.7 %collective-permute-start.5 = (bf16[640,32,80]{0,2,1:T(8,128)(2,1)S(1)}, bf16[640,32,80]{0,2,1:T(8,128)(2,1)S(1)}, u32[]{:S(2)}, u32[]{:S(2)}) collective-permute-start(bf16[640,32,80]{0,2,1:T(8,128)(2,1)S(1)} %slice.211), channel_id=1, source_target_pairs={{0,8},{8,0},{1,9},{9,1},{2,10},{10,2},{3,11},{11,3},{4,12},{12,4},... | collective-permute-start | bytes 9830408 | tf_op jit(solution)/shard_map/ppermute | solution.py:38
Sparse Core Ops, SparseCore 0:
  16.0 39.8 all-gather.2
  57.9 58.4 all-gather.4
  137.5 56.2 reduce-scatter.1
